TPU v7x, 32 devices: a whole 2x2x4 slice. The times are simulated.
32 devices in a mesh: groups: 2 (over y), dp: 8 (over z, core), vocab: 2 (over x).
Axes of the slice: x: 2, y: 2, z: 4, core: 2. Of those that a mesh axis runs over, the one named last changes fastest.
Arguments:
- teacher_hidden: bfloat16 [128, 5120], P(('groups', 'dp')), parts along dimension 0, may hold values from -110 to 110
- teacher_head: bfloat16 [5120, 98304], P(None, ('dp', 'vocab')), may hold values from -0.078125 to 0.078125
- map_dest: int32 [768, 4], P(('dp', 'vocab')), may hold values from 0 to 7, all different within a row; in each aligned block of 48 rows (0 to 47, 48 to 95, ...) at most 24 rows name the same one
- map_slot: int32 [768, 4], P(('dp', 'vocab')), may hold values from 0 to 31
- map_weight: bfloat16 [768, 4, 128, 128], P(('dp', 'vocab')), may hold values from 0.019897461 to 1
- student_hidden: bfloat16 [128, 4096], P(('groups', 'dp')), parts along dimension 0, may hold values from -110 to 110
- student_head: bfloat16 [4096, 65536], P(None, ('dp', 'vocab')), may hold values from -0.09375 to 0.09375
- targets: int32 [128], P(('groups', 'dp')), parts along dimension 0, may hold values from 0 to 65535
Outputs:
- grad_hidden: bfloat16 [128, 4096], P(('groups', 'dp', 'vocab')), parts along dimension 0
There are 2 independent parts, one for each index of `groups`. A program takes and returns all parts, laid end to end along the dimension named above; an argument that names none is the same for every part. Nothing has to cross between parts.
Inputs may be any that keep to these rules, and one draw needn't show every extreme that they name: `map_dest`: the 4 entries of a row differ. Among the 48 rows of one device (aligned blocks of rows) no value appears more than 24 times, and some value appears exactly 24 times.
All inputs are finite; a program needn't handle non-finite values.
Results may differ from a plain program's by a relative error of at most 0.012.
Values may be sent and summed in bfloat16 or wider, within the bound.
No kernel may reach another device: no remote copies, remote signals or barrier semaphores. Data moves between devices by JAX's collectives and lax.ppermute only.
A program may use at most 192 MiB of HBM per device.

v0:
```python
import jax
import jax.numpy as jnp
from jax import lax
from jax.sharding import PartitionSpec as P

hard_weight = 0.25
loss_scale = 64.0


def on_device(
    teacher_hidden,
    teacher_head,
    map_dest,
    map_slot,
    map_weight,
    student_hidden,
    student_head,
    targets,
):
    dp_count = lax.axis_size("dp")
    vocab_count = lax.axis_size("vocab")
    block_size = map_weight.shape[2]
    teacher_blocks = map_dest.shape[0]
    fan_count = map_dest.shape[1]
    student_cols = student_head.shape[1]
    student_blocks = student_cols // block_size
    capacity = max(2, (teacher_blocks * fan_count + dp_count - 1) // dp_count)
    device_flat = lax.axis_index("dp") * vocab_count + lax.axis_index("vocab")
    teacher_logits = jnp.dot(
        lax.all_gather(teacher_hidden, "dp", axis=0, tiled=True),
        teacher_head,
        preferred_element_type=jnp.float32,
    )
    student_logits = jnp.dot(
        lax.all_gather(student_hidden, "dp", axis=0, tiled=True),
        student_head,
        preferred_element_type=jnp.float32,
    )
    all_targets = lax.all_gather(targets, "dp", axis=0, tiled=True)
    tokens_all = teacher_logits.shape[0]
    teacher_peak = lax.pmax(jnp.max(teacher_logits, axis=1), ("dp", "vocab"))
    teacher_exp = jnp.exp(teacher_logits - teacher_peak[:, None])
    student_peak = lax.pmax(jnp.max(student_logits, axis=1), ("dp", "vocab"))
    student_total = lax.psum(
        jnp.sum(jnp.exp(student_logits - student_peak[:, None]), axis=1), ("dp", "vocab")
    )
    teacher_weights = teacher_exp.astype(jnp.bfloat16)
    prob_blocks = teacher_weights.reshape(tokens_all, teacher_blocks, block_size)
    mapped_terms = jnp.einsum(
        "gkc,krcd->krgd", prob_blocks, map_weight, preferred_element_type=jnp.float32
    ).astype(jnp.bfloat16)
    item_count = teacher_blocks * fan_count
    dest_flat = map_dest.reshape(item_count)
    dest_onehot = (dest_flat[:, None] == jnp.arange(dp_count, dtype=jnp.int32)[None, :]).astype(
        jnp.int32
    )
    earlier_same = jnp.sum(jnp.cumsum(dest_onehot, axis=0) * dest_onehot, axis=1) - 1
    slot_index = dest_flat * capacity + earlier_same
    placement = (
        jnp.arange(dp_count * capacity, dtype=jnp.int32)[:, None] == slot_index[None, :]
    ).astype(jnp.bfloat16)
    outgoing = jnp.dot(
        placement,
        mapped_terms.reshape(item_count, tokens_all * block_size),
        preferred_element_type=jnp.float32,
    )
    outgoing = outgoing.astype(jnp.bfloat16).reshape(dp_count, capacity, tokens_all, block_size)
    slot_onehot = (
        map_slot.reshape(item_count)[:, None]
        == jnp.arange(student_blocks, dtype=jnp.int32)[None, :]
    ).astype(jnp.bfloat16)
    slot_marks = jnp.dot(placement, slot_onehot, preferred_element_type=jnp.float32).astype(
        jnp.bfloat16
    )
    slot_marks = slot_marks.reshape(dp_count, capacity, student_blocks)
    incoming, marks_in = (
        lax.all_to_all(outgoing, "dp", split_axis=0, concat_axis=0, tiled=True),
        lax.all_to_all(slot_marks, "dp", split_axis=0, concat_axis=0, tiled=True),
    )
    mapped = jnp.dot(
        marks_in.reshape(dp_count * capacity, student_blocks).T,
        incoming.reshape(dp_count * capacity, tokens_all * block_size),
        preferred_element_type=jnp.float32,
    )
    mapped = jnp.transpose(
        mapped.reshape(student_blocks, tokens_all, block_size), (1, 0, 2)
    ).reshape(tokens_all, student_cols)
    target_total = lax.psum(jnp.sum(mapped, axis=1), ("dp", "vocab"))
    target_probs = mapped / target_total[:, None]
    student_probs = jnp.exp(student_logits - student_peak[:, None]) / student_total[:, None]
    columns = device_flat * student_cols + jnp.arange(student_cols, dtype=jnp.int32)
    target_hits = (all_targets[:, None] == columns[None, :]).astype(jnp.float32)
    logit_grad = (
        loss_scale
        * (student_probs - (1.0 - hard_weight) * target_probs - hard_weight * target_hits)
    ).astype(jnp.bfloat16)
    gradient = lax.psum_scatter(
        lax.dot_general(
            logit_grad, student_head, (((1,), (1,)), ((), ())), preferred_element_type=jnp.float32
        ),
        ("dp", "vocab"),
        scatter_dimension=0,
        tiled=True,
    )
    return gradient.astype(jnp.bfloat16)


def solution(mesh):
    placed = (
        P(("groups", "dp"), None),
        P(None, ("dp", "vocab")),
        P(("dp", "vocab"), None),
        P(("dp", "vocab"), None),
        P(("dp", "vocab"), None, None, None),
        P(("groups", "dp"), None),
        P(None, ("dp", "vocab")),
        P(("groups", "dp")),
    )
    return jax.shard_map(
        on_device,
        mesh=mesh,
        in_specs=placed,
        out_specs=P(("groups", "dp", "vocab"), None),
        check_vma=False,
    )
```

profile of v0, /device:TPU:1, one launch (start us, length us, event | category | flops | bytes accessed | tf_op | source)
XLA Modules:
  0.0 320.8 jit_solution(15093153480868843150)
XLA Ops:
  0.0 0.8 copy.14
  0.8 0.1 reshape.57
  0.9 0.6 reduce-window.6
  1.5 0.2 slice_reduce_fusion
  1.7 0.1 add_bitcast_fusion
  1.9 0.8 copy.15
  2.6 0.1 eq.70
  2.7 0.3 convolution_convert_fusion.2
  3.0 0.1 copy.21
  3.1 0.7 reshape.77
  3.8 6.4 %all-to-all-start = ((bf16[8,2,384]{2,1,0:T(2,128)(2,1)}), bf16[8,2,384]{2,1,0:T(2,128)(2,1)S(1)}, u32[]{:S(2)}, u32[]{:S(2)}) async-start(bf16[8,2,384]{2,1,0:T(2,128)(2,1)} %reshape.77), calls=%async_computation | async-start | bytes 24576 | tf_op jit(solution)/shard_map/all_to_all | solution.py:78
  10.2 15.6 %all_gather.10 = bf16[64,5120]{1,0:T(8,128)(2,1)S(1)} all-gather(bf16[8,5120]{1,0:T(8,128)(2,1)} %param.8), channel_id=1, replica_groups=mesh['groups'=2,'dp'=8,'vocab'=2] {'dp'}, dimensions={0}, use_global_device_ids=true | all-gather | bytes 737280 | tf_op jit(solution)/shard_map/all_gather | solution.py:30
  25.8 15.1 %all_gather.9 = bf16[64,4096]{1,0:T(8,128)(2,1)S(1)} all-gather(bf16[8,4096]{1,0:T(8,128)(2,1)} %param.13), channel_id=1, replica_groups=mesh['groups'=2,'dp'=8,'vocab'=2] {'dp'}, dimensions={0}, use_global_device_ids=true | all-gather | bytes 589824 | tf_op jit(solution)/shard_map/all_gather | solution.py:35
  40.9 23.0 %fusion.35 = (f32[64]{0:T(128)S(1)}, f32[64,6144]{1,0:T(8,128)S(1)}) fusion(bf16[64,5120]{1,0:T(8,128)(2,1)S(1)} %all_gather.10, bf16[5120,6144]{1,0:T(8,128)(2,1)} %param.9), kind=kOutput, calls=%fused_computation.50 | convolution fusion | flops 4026925056 | bytes 65143040 | tf_op jit(solution)/shard_map/dot_general | solution.py:29
  63.9 13.7 %fusion.36 = (f32[64]{0:T(128)S(1)}, f32[64,4096]{1,0:T(8,128)S(1)}) fusion(bf16[64,4096]{1,0:T(8,128)(2,1)S(1)} %all_gather.9, bf16[4096,4096]{1,0:T(8,128)(2,1)} %param.14), kind=kOutput, calls=%fused_computation.51 | convolution fusion | flops 2147745792 | bytes 35127552 | tf_op jit(solution)/shard_map/dot_general | solution.py:34
  77.7 31.7 %all-reduce.4 = (f32[64]{0:T(128)S(1)}, f32[64]{0:T(128)S(1)}) all-reduce(f32[64]{0:T(128)S(1)} %get-tuple-element.9, f32[64]{0:T(128)S(1)} %get-tuple-element.11), channel_id=1, replica_groups=mesh['groups'=2,'dp'=8,'vocab'=2] {'dp','vocab'}, use_global_device_ids=true, to_apply=%region_8.9 | all-reduce | flops 128 | bytes 1024 | tf_op jit(solution)/shard_map/pmax | solution.py:41
  109.4 0.3 fusion.14
  109.7 0.1 copy.26
  109.8 3.8 %convolution_convert_fusion.1 = bf16[48,64,4,128]{3,1,2,0:T(8,128)(2,1)S(1)} fusion(bf16[48,4,128,128]{3,2,1,0:T(8,128)(2,1)} %param.12, bf16[64,48,128,1]{2,1,0,3:T(8,128)(2,1)S(1)} %bitcast.69), kind=kOutput, calls=%fused_computation.7 | convolution fusion | flops 404226048 | bytes 10223616 | tf_op jit(solution)/shard_map/gkc,krcd->krgd/dot_general | solution.py:49
  113.6 2.4 fusion.5
  116.0 2.6 copy.28
  118.6 0.0 all-to-all-done
  118.6 0.0 copy-start.2
  118.6 0.0 copy-start.1
  118.6 0.0 copy-start
  118.6 7.0 %all-to-all-start.1 = ((bf16[8,24,64,128]{3,2,1,0:T(8,128)(2,1)}), bf16[8,24,64,128]{3,2,1,0:T(8,128)(2,1)}, u32[]{:S(2)}, u32[]{:S(2)}) async-start(bf16[8,24,64,128]{3,2,1,0:T(8,128)(2,1)} %bitcast.24), calls=%async_computation.1 | async-start | bytes 6291456 | tf_op jit(solution)/shard_map/all_to_all | solution.py:77
  125.6 0.0 copy-done.2
  125.6 0.6 dynamic-slice
  126.8 0.0 copy-done.1
  126.8 0.6 dynamic-slice.1
  128.0 0.0 copy-done
  128.0 0.2 dynamic-update-slice
  128.3 68.2 %all-reduce.1 = s32[64]{0:T(128)S(1)} all-reduce(s32[64]{0:T(128)S(1)} %dynamic-update-slice), channel_id=1, replica_groups=mesh['groups'=2,'dp'=8,'vocab'=2] {'dp'}, use_global_device_ids=true, to_apply=%add.1 | all-reduce | flops 64 | bytes 512
  196.5 0.3 fusion.13
  196.8 0.1 reshape.78
  196.9 0.0 all-to-all-done.1
  196.9 4.0 %fusion.37 = (f32[64]{0:T(128)S(1)}, f32[32,64,128]{2,0,1:T(8,128)S(1)}) fusion(bf16[192,32,1]{1,0,2:T(8,128)(2,1)S(1)} %bitcast.72, bf16[24,8,64,128]{3,2,1,0:T(8,128)(2,1)} %bitcast.26), kind=kOutput, calls=%fused_computation.52 | convolution fusion | flops 100925376 | bytes 4206848 | tf_op jit(solution)/shard_map/dot_general | solution.py:80
  200.9 28.2 %all-reduce.3 = (f32[64]{0:T(128)S(1)}, f32[64]{0:T(128)S(1)}) all-reduce(f32[64]{0:T(128)S(1)} %get-tuple-element.13, f32[64]{0:T(128)S(1)} %fusion.13), channel_id=1, replica_groups=mesh['groups'=2,'dp'=8,'vocab'=2] {'dp','vocab'}, use_global_device_ids=true, to_apply=%region_10.11 | all-reduce | flops 128 | bytes 1024 | tf_op jit(solution)/shard_map/psum | solution.py:88
  229.0 16.1 %fusion.16 = f32[64,4096]{1,0:T(8,128)S(1)} fusion(bf16[4096,4096]{1,0:T(8,128)(2,1)} %param.14, f32[8,8,32,128]{3,2,1,0:T(8,128)S(1)} %bitcast.70, f32[64,4096]{1,0:T(8,128)S(1)} %get-tuple-element.12, s32[4096]{0:T(1024)S(1)} %iota_add_fusion, f32[64]{0:T(128)S(1)} %get-tuple-element.5, f32[64]{0:T(128)S(1)} %get-tuple-element.6, ...), kind=kOutput, calls=%fused_computation.21 | convolution fusion | flops 2150105088 | bytes 36717568 | tf_op jit(solution)/shard_map/dot_general | solution.py:98
  245.1 75.0 %all-reduce.6 = bf16[64,4096]{1,0:T(8,128)(2,1)S(1)} all-reduce(f32[64,4096]{1,0:T(8,128)S(1)} %fusion.16), channel_id=2, replica_groups=mesh['groups'=2,'dp'=8,'vocab'=2] {'dp','vocab'}, use_global_device_ids=true, to_apply=%region_11.12.clone | all-reduce | flops 262144 | bytes 1572864
  320.2 0.6 dynamic-slice_convert_fusion
  (8 shorter events, 0.1 us)
Async XLA Ops:
  3.8 114.8 %all-to-all-start = ((bf16[8,2,384]{2,1,0:T(2,128)(2,1)}), bf16[8,2,384]{2,1,0:T(2,128)(2,1)S(1)}, u32[]{:S(2)}, u32[]{:S(2)}) async-start(bf16[8,2,384]{2,1,0:T(2,128)(2,1)} %reshape.77), calls=%async_computation | async-start | bytes 24576 | tf_op jit(solution)/shard_map/all_to_all | solution.py:78
  118.6 7.0 %copy-start.2 = (u32[32]{0:T(128)S(1)}, u32[32]{0:T(128)}, u32[]{:S(2)}) copy-start(u32[32]{0:T(128)} %constant.43) | copy-start | bytes 388
  118.6 8.2 %copy-start.1 = (u32[32]{0:T(128)S(1)}, u32[32]{0:T(128)}, u32[]{:S(2)}) copy-start(u32[32]{0:T(128)} %constant.49) | copy-start | bytes 388
  118.6 9.4 %copy-start = (s32[8]{0:T(128)S(1)}, s32[8]{0:T(128)}, u32[]{:S(2)}) copy-start(s32[8]{0:T(128)} %param.15) | copy-start | bytes 100
  118.6 78.3 %all-to-all-start.1 = ((bf16[8,24,64,128]{3,2,1,0:T(8,128)(2,1)}), bf16[8,24,64,128]{3,2,1,0:T(8,128)(2,1)}, u32[]{:S(2)}, u32[]{:S(2)}) async-start(bf16[8,24,64,128]{3,2,1,0:T(8,128)(2,1)} %bitcast.24), calls=%async_computation.1 | async-start | bytes 6291456 | tf_op jit(solution)/shard_map/all_to_all | solution.py:77
where the time goes:
time: 324 us; the launch traced here: 321 us
  blocking collectives  234 us (72%)
  matrix products  63.2 us (20%)
  starting transfers between devices  13.3 us (4%)
  local copies, waits for them, and re-layouts  7.67 us (2%)
    unnamed x2, blocking collectives  143 us
    pmax x1, blocking collectives, on_device(): teacher_peak = lax.pmax(jnp.max(teacher_logits, axis=1), ('dp', 'vocab'))  31.7 us
    psum x1, blocking collectives, on_device(): target_total = lax.psum(jnp.sum(mapped, axis=1), ('dp', 'vocab'))  28.2 us
    dot_general x1, matrix products, on_device(): jnp.dot(lax.all_gather(teacher_hidden, 'dp', axis=0, tiled=True), teacher...  23 us
    dot_general x1, matrix products, on_device(): lax.dot_general(logit_grad, student_head, (((1,), (1,)), ((), ())), prefe...  16.1 us
    all_gather x1, blocking collectives, on_device(): lax.all_gather(teacher_hidden, 'dp', axis=0, tiled=True)  15.6 us
    all_gather x1, blocking collectives, on_device(): lax.all_gather(student_hidden, 'dp', axis=0, tiled=True)  15.1 us
    dot_general x1, matrix products, on_device(): jnp.dot(lax.all_gather(student_hidden, 'dp', axis=0, tiled=True), student...  13.7 us
  transfers between devices with their start and end apart: 2, of which 0 were waited for; matrix products, arithmetic and copies ran while one was open for 15% of the time, Pallas kernels for 0%

commit v1 on v0

v1 whole, which is shorter than its diff:
```python
import jax
import jax.numpy as jnp
from jax import lax
from jax.sharding import PartitionSpec as P

hard_weight = 0.25
loss_scale = 64.0


def _code(values):
    return values.astype(jnp.float32).astype(jnp.bfloat16)


def _decode(values):
    return jnp.round(values.astype(jnp.float32)).astype(jnp.int32)


def on_device(
    teacher_hidden,
    teacher_head,
    map_dest,
    map_slot,
    map_weight,
    student_hidden,
    student_head,
    targets,
):
    dp_count = lax.axis_size("dp")
    vocab_count = lax.axis_size("vocab")
    my_dp = lax.axis_index("dp")
    my_vocab = lax.axis_index("vocab")
    block_size = map_weight.shape[2]
    teacher_blocks = map_dest.shape[0]
    fan_count = map_dest.shape[1]
    student_cols = student_head.shape[1]
    student_blocks = student_cols // block_size
    capacity = max(2, (teacher_blocks * fan_count + dp_count - 1) // dp_count)
    device_flat = my_dp * vocab_count + my_vocab
    item_count = teacher_blocks * fan_count
    local_tokens = teacher_hidden.shape[0]
    teacher_width = teacher_hidden.shape[1]
    student_width = student_hidden.shape[1]

    coded = jnp.concatenate(
        [
            _code(map_dest.reshape(item_count)),
            _code(map_slot.reshape(item_count)),
            _code(targets // 256),
            _code(targets % 256),
        ]
    )
    extra_width = -(-coded.shape[0] // local_tokens)
    extra_width = -(-extra_width // 128) * 128
    coded = jnp.pad(coded, (0, extra_width * local_tokens - coded.shape[0]))
    packed = jnp.concatenate(
        [teacher_hidden, student_hidden, coded.reshape(local_tokens, extra_width)], axis=1
    )
    gathered = lax.all_gather(packed, "dp", axis=0, tiled=True)
    tokens_all = gathered.shape[0]
    teacher_all = gathered[:, :teacher_width]
    student_all = gathered[:, teacher_width : teacher_width + student_width]
    extra_all = gathered[:, teacher_width + student_width :].reshape(
        dp_count, local_tokens * extra_width
    )
    src_dest = _decode(extra_all[:, :item_count])
    src_slot = _decode(extra_all[:, item_count : 2 * item_count])
    t_hi = _decode(extra_all[:, 2 * item_count : 2 * item_count + local_tokens])
    t_lo = _decode(extra_all[:, 2 * item_count + local_tokens : 2 * item_count + 2 * local_tokens])
    all_targets = (t_hi * 256 + t_lo).reshape(tokens_all)

    teacher_logits = jnp.dot(teacher_all, teacher_head, preferred_element_type=jnp.float32)
    teacher_local_peak = jnp.max(teacher_logits, axis=1)
    teacher_weights = jnp.exp(teacher_logits - teacher_local_peak[:, None]).astype(jnp.bfloat16)
    prob_blocks = teacher_weights.reshape(tokens_all, teacher_blocks, block_size)
    mapped_terms = jnp.einsum(
        "gkc,krcd->krgd", prob_blocks, map_weight, preferred_element_type=jnp.float32
    ).astype(jnp.bfloat16)
    mapped_mass = jnp.sum(mapped_terms.astype(jnp.float32), axis=(0, 1, 3))

    dest_flat = map_dest.reshape(item_count)
    dest_onehot = (dest_flat[:, None] == jnp.arange(dp_count, dtype=jnp.int32)[None, :]).astype(
        jnp.int32
    )
    earlier_same = jnp.sum(jnp.cumsum(dest_onehot, axis=0) * dest_onehot, axis=1) - 1
    slot_index = dest_flat * capacity + earlier_same
    placement = (
        jnp.arange(dp_count * capacity, dtype=jnp.int32)[:, None] == slot_index[None, :]
    ).astype(jnp.bfloat16)
    outgoing = jnp.dot(
        placement,
        mapped_terms.reshape(item_count, tokens_all * block_size),
        preferred_element_type=jnp.float32,
    )
    outgoing = outgoing.astype(jnp.bfloat16).reshape(dp_count, capacity, tokens_all, block_size)
    incoming = lax.all_to_all(outgoing, "dp", split_axis=0, concat_axis=0, tiled=True)

    student_logits = jnp.dot(student_all, student_head, preferred_element_type=jnp.float32)
    student_local_peak = jnp.max(student_logits, axis=1)
    student_local_total = jnp.sum(jnp.exp(student_logits - student_local_peak[:, None]), axis=1)

    stats = jnp.stack(
        [teacher_local_peak, mapped_mass, student_local_peak, student_local_total]
    )
    all_stats = lax.all_gather(stats, ("dp", "vocab"), axis=0, tiled=False)
    teacher_peak = jnp.max(all_stats[:, 0], axis=0)
    teacher_scale = jnp.exp(all_stats[:, 0] - teacher_peak[None, :])
    target_total = jnp.sum(teacher_scale * all_stats[:, 1], axis=0)
    student_peak = jnp.max(all_stats[:, 2], axis=0)
    student_total = jnp.sum(
        jnp.exp(all_stats[:, 2] - student_peak[None, :]) * all_stats[:, 3], axis=0
    )
    source_scale = teacher_scale.reshape(dp_count, vocab_count, tokens_all)[:, my_vocab]

    is_mine = (src_dest == my_dp).astype(jnp.int32)
    rank = jnp.cumsum(is_mine, axis=1) - 1
    at_cap = (
        (rank[:, :, None] == jnp.arange(capacity, dtype=jnp.int32)[None, None, :])
        & (is_mine[:, :, None] > 0)
    ).astype(jnp.float32)
    at_slot = (
        src_slot[:, :, None] == jnp.arange(student_blocks, dtype=jnp.int32)[None, None, :]
    ).astype(jnp.float32)
    marks = jnp.einsum("xec,xes->xcs", at_cap, at_slot)
    scaled_in = incoming.astype(jnp.float32) * source_scale[:, None, :, None]
    mapped = jnp.einsum(
        "xcs,xctd->tsd", marks, scaled_in, precision=lax.Precision.HIGHEST,
        preferred_element_type=jnp.float32,
    ).reshape(tokens_all, student_cols)

    target_probs = mapped / target_total[:, None]
    student_probs = jnp.exp(student_logits - student_peak[:, None]) / student_total[:, None]
    columns = device_flat * student_cols + jnp.arange(student_cols, dtype=jnp.int32)
    target_hits = (all_targets[:, None] == columns[None, :]).astype(jnp.float32)
    logit_grad = (
        loss_scale
        * (student_probs - (1.0 - hard_weight) * target_probs - hard_weight * target_hits)
    ).astype(jnp.bfloat16)
    gradient = lax.psum_scatter(
        lax.dot_general(
            logit_grad, student_head, (((1,), (1,)), ((), ())), preferred_element_type=jnp.float32
        ),
        ("dp", "vocab"),
        scatter_dimension=0,
        tiled=True,
    )
    return gradient.astype(jnp.bfloat16)


def solution(mesh):
    placed = (
        P(("groups", "dp"), None),
        P(None, ("dp", "vocab")),
        P(("dp", "vocab"), None),
        P(("dp", "vocab"), None),
        P(("dp", "vocab"), None, None, None),
        P(("groups", "dp"), None),
        P(None, ("dp", "vocab")),
        P(("groups", "dp")),
    )
    return jax.shard_map(
        on_device,
        mesh=mesh,
        in_specs=placed,
        out_specs=P(("groups", "dp", "vocab"), None),
        check_vma=False,
    )
```

time: 324 us -> 264 us (0.81)
  blocking collectives: 234 us -> 139 us
  waiting for transfers between devices: 0.01 us -> 25.5 us
  between operations: 1.38 us -> 14.2 us
  starting transfers between devices: 13.3 us -> 3.97 us
  other arithmetic: 1.35 us -> 5.34 us
    unnamed x2 -> x1, blocking collectives: 143 us -> 71 us
    all_gather x2 -> x1, blocking collectives: 30.7 us -> 68.4 us  [on_device(): all_stats = lax.all_gather(stats, ('dp', 'vocab'), axis=0, tiled=False)]
    pmax x1 -> x0, blocking collectives: 31.7 us -> none  [on_device(): teacher_peak = lax.pmax(jnp.max(teacher_logits, axis=1), ('dp', 'vocab'))]
    psum x1 -> x0, blocking collectives: 28.2 us -> none  [on_device(): target_total = lax.psum(jnp.sum(mapped, axis=1), ('dp', 'vocab'))]
    all_gather x0 -> x1, waiting for transfers between devices: none -> 25.5 us  [on_device(): gathered = lax.all_gather(packed, 'dp', axis=0, tiled=True)]
    all_to_all x1 -> x0, starting transfers between devices: 6.37 us -> none  [on_device(): lax.all_to_all(slot_marks, 'dp', split_axis=0, concat_axis=0, tiled=True)]
    reshape x2 -> x3, local copies, waits for them, and re-layouts: 0.22 us -> 3.92 us  [the longest x1 3.81 us: on_device(): outgoing.astype(jnp.bfloat16)]
    unnamed x16 -> x10, local copies, waits for them, and re-layouts: 6.49 us -> 3.34 us
  transfers between devices with their start and end apart: 2 -> 2, of which waited for: 0 -> 1; matrix products, arithmetic and copies ran while one was open for 15% -> 6% of each run, Pallas kernels for 0% -> 0%
where the time goes in v1:
time: 264 us; the launch traced here: 261 us
  blocking collectives  139 us (53%)
  matrix products  63.8 us (24%)
  waiting for transfers between devices  25.5 us (10%)
  between operations  14.2 us (5%)
  local copies, waits for them, and re-layouts  8.67 us (3%)
  other arithmetic  5.34 us (2%)
  starting transfers between devices  3.97 us (2%)
    unnamed x1, blocking collectives  71 us
    all_gather x1, blocking collectives, on_device(): all_stats = lax.all_gather(stats, ('dp', 'vocab'), axis=0, tiled=False)  68.4 us
    all_gather x1, waiting for transfers between devices, on_device(): gathered = lax.all_gather(packed, 'dp', axis=0, tiled=True)  25.5 us
    dot_general x1, matrix products, on_device(): jnp.dot(teacher_all, teacher_head, preferred_element_type=jnp.float32)  23.2 us
    dot_general x1, matrix products, on_device(): lax.dot_general(logit_grad, student_head, (((1,), (1,)), ((), ())), prefe...  16.3 us
    dot_general x1, matrix products, on_device(): jnp.dot(student_all, student_head, preferred_element_type=jnp.float32)  13.9 us
  transfers between devices with their start and end apart: 2, of which 1 were waited for; matrix products, arithmetic and copies ran while one was open for 6% of the time, Pallas kernels for 0%

profile of v1, /device:TPU:1, one launch (start us, length us, event | category | flops | bytes accessed | tf_op | source)
XLA Modules:
  0.0 260.9 jit_solution(4911078604870435215)
XLA Ops:
  6.5 0.0 all-gather.4.cloned.1.call-start
  6.5 0.7 convert_convert_fusion
  7.2 0.7 convert_convert_fusion.2
  7.9 0.1 copy.29
  8.0 0.1 convert_element_type.91
  8.1 0.8 copy.28
  8.9 0.1 reshape.80
  9.0 0.6 reduce-window.14
  9.6 0.2 slice_reduce_fusion.1
  9.9 0.1 add_bitcast_fusion.1
  10.0 0.1 fusion.47
  10.1 1.6 pad_maximum_fusion
  11.6 0.0 all-gather.4.cloned.1.call-update
  11.7 25.5 %all-gather.4.cloned.1.call-done = bf16[64,9344]{1,0:T(8,128)(2,1)} async-done(((bf16[8,9344]{1,0:T(8,128)(2,1)}), bf16[64,9344]{1,0:T(8,128)(2,1)}) %all-gather.4.cloned.1.call-update) | async-done | bytes 1196048 | tf_op jit(solution)/shard_map/all_gather | solution.py:58
  37.1 23.2 %fusion.56 = (f32[64]{0:T(128)S(1)}, f32[64,6144]{1,0:T(8,128)S(1)}) fusion(bf16[5120,6144]{1,0:T(8,128)(2,1)} %param.9, bf16[64,9344]{1,0:T(8,128)(2,1)} %all-gather.4.cloned.1.call-done), kind=kOutput, calls=%fused_computation.93 | convolution fusion | flops 4026925056 | bytes 65143040 | tf_op jit(solution)/shard_map/dot_general | solution.py:71
  60.4 0.3 fusion.14
  60.7 0.1 copy.42
  60.8 4.0 %convert_reduce_fusion = (f32[64]{0:T(128)S(1)}, bf16[48,64,4,128]{3,1,2,0:T(8,128)(2,1)S(1)}) fusion(bf16[48,4,128,128]{3,2,1,0:T(8,128)(2,1)} %param.12, bf16[64,48,128,1]{2,1,0,3:T(8,128)(2,1)S(1)} %bitcast.79), kind=kOutput, calls=%fused_computation.4 | convolution fusion | flops 407371712 | bytes 10223872 | tf_op jit(solution)/shard_map/gkc,krcd->krgd/dot_general | solution.py:75
  64.8 2.4 fusion.6
  67.1 0.9 copy.44
  68.0 3.8 %copy.32 = bf16[8,24,64,128]{3,1,2,0:T(8,128)(2,1)} copy(bf16[8,24,64,128]{3,2,1,0:T(8,128)(2,1)S(1)} %bitcast.76) | data formatting | bytes 6291456 | tf_op jit(solution)/shard_map/reshape | solution.py:94
  71.8 0.0 copy-start.2
  71.8 0.0 slice-start
  71.8 4.0 %all-to-all-start = ((bf16[8,24,64,128]{3,1,2,0:T(8,128)(2,1)}), bf16[8,24,64,128]{3,1,2,0:T(8,128)(2,1)S(1)}, u32[]{:S(2)}, u32[]{:S(2)}) async-start(bf16[8,24,64,128]{3,1,2,0:T(8,128)(2,1)} %copy.32), calls=%async_computation | async-start | bytes 6291456 | tf_op jit(solution)/shard_map/all_to_all | solution.py:95
  75.8 0.0 copy-done.2
  75.8 0.6 dynamic-slice
  77.1 0.0 slice-done
  77.1 0.1 convert_add_fusion
  77.2 0.1 eq.99
  77.3 0.6 reduce-window.16
  77.9 0.2 slice_reduce_fusion
  78.1 13.9 %fusion.55 = (f32[64]{0:T(128)S(1)}, f32[64,4096]{1,0:T(8,128)S(1)}) fusion(bf16[4096,4096]{1,0:T(8,128)(2,1)} %param.14, bf16[64,9344]{1,0:T(8,128)(2,1)} %all-gather.4.cloned.1.call-done), kind=kOutput, calls=%fused_computation.92 | convolution fusion | flops 2147745792 | bytes 35127552 | tf_op jit(solution)/shard_map/dot_general | solution.py:97
  92.0 0.0 copy-start
  92.0 1.0 copy-done
  93.0 0.3 exponential_reduce_fusion
  93.3 68.4 %all-gather.1 = f32[16,4,64]{2,1,0:T(4,128)S(1)} all-gather(f32[1,4,64]{2,1,0:T(4,128)S(1)} %maximum_bitcast_fusion), channel_id=2, replica_groups=mesh['groups'=2,'dp'=8,'vocab'=2] {'dp','vocab'}, dimensions={0}, use_global_device_ids=true | all-gather | bytes 17408 | tf_op jit(solution)/shard_map/all_gather | solution.py:104
  161.8 0.1 round-nearest-even_convert_fusion
  161.9 0.1 add_bitcast_fusion
  162.0 0.2 convolution_bitcast_fusion
  162.2 0.0 all-to-all-done
  162.2 0.0 copy-start.1
  162.2 3.9 %fusion = f32[64,128,32,1]{1,2,0,3:T(8,128)S(1)} fusion(f32[8,24,32,1]{2,1,3,0:T(8,128)S(1)} %convolution_bitcast_fusion, bf16[8,24,64,128]{3,1,2,0:T(8,128)(2,1)S(1)} %all-to-all-done, f32[8,64]{1,0:T(8,128)S(1)} %bitcast.87), kind=kOutput, calls=%fused_computation.1 | convolution fusion | flops 607125504 | bytes 4220928 | tf_op jit(solution)/shard_map/xcs,xctd->tsd/dot_general | solution.py:125
  166.1 0.0 copy-done.1
  166.1 16.3 %fusion.18 = f32[64,4096]{1,0:T(8,128)S(1)} fusion(bf16[4096,4096]{1,0:T(8,128)(2,1)} %param.14, f32[8,8,32,128]{3,2,1,0:T(8,128)S(1)} %bitcast.78, f32[64,4096]{1,0:T(8,128)S(1)} %copy-done.1, s32[4096]{0:T(1024)S(1)} %iota_add_fusion, f32[64]{0:T(128)S(1)} %get-tuple-element.21, f32[64]{0:T(128)S(1)} %get-tuple-element.22, f32[64]{0:T(128)S(1)} %reduce_max.38, ...), kind=kOutput, calls=%fused_computation.23 | convolution fusion | flops 2150105088 | bytes 36717568 | tf_op jit(solution)/shard_map/dot_general | solution.py:139
  182.4 71.0 %all-reduce.5 = bf16[64,4096]{1,0:T(8,128)(2,1)S(1)} all-reduce(f32[64,4096]{1,0:T(8,128)S(1)} %fusion.18), channel_id=3, replica_groups=mesh['groups'=2,'dp'=8,'vocab'=2] {'dp','vocab'}, use_global_device_ids=true, to_apply=%region_13.14.clone | all-reduce | flops 262144 | bytes 1572864
  253.5 0.6 dynamic-slice_convert_fusion
  (19 shorter events, 0.3 us)
Async XLA Ops:
  6.5 30.6 %all-gather.4.cloned.1.call-start = ((), (), s32[]{:S(2)}) async-start(), calls=%async_computation.1 | async-start | bytes 1345536 | tf_op jit(solution)/shard_map/all_gather | solution.py:58
  71.8 4.0 %copy-start.2 = (u32[32]{0:T(128)S(1)}, u32[32]{0:T(128)}, u32[]{:S(2)}) copy-start(u32[32]{0:T(128)} %constant.82) | copy-start | bytes 388
  71.8 5.2 %slice-start = ((bf16[64,9344]{1,0:T(8,128)(2,1)}), bf16[64,128]{1,0:T(8,128)(2,1)S(1)}, s32[]{:S(2)}) async-start(bf16[64,9344]{1,0:T(8,128)(2,1)} %all-gather.4.cloned.1.call-done), calls=%async_computation.2 | async-start | bytes 32768 | tf_op jit(solution)/shard_map/slice | solution.py:62
  71.8 90.4 %all-to-all-start = ((bf16[8,24,64,128]{3,1,2,0:T(8,128)(2,1)}), bf16[8,24,64,128]{3,1,2,0:T(8,128)(2,1)S(1)}, u32[]{:S(2)}, u32[]{:S(2)}) async-start(bf16[8,24,64,128]{3,1,2,0:T(8,128)(2,1)} %copy.32), calls=%async_computation | async-start | bytes 6291456 | tf_op jit(solution)/shard_map/all_to_all | solution.py:95
  92.0 1.0 copy-start
  162.2 3.9 %copy-start.1 = (f32[64,4096]{1,0:T(8,128)S(1)}, f32[64,4096]{1,0:T(8,128)}, u32[]{:S(2)}) copy-start(f32[64,4096]{1,0:T(8,128)} %copy-done) | copy-start | bytes 3145732
Sparse Core Ops, SparseCore 0:
  11.8 25.3 all-gather.3

commit v2 on v1

--- a/solution.py
+++ b/solution.py
@@ -135,14 +135,13 @@
         loss_scale
         * (student_probs - (1.0 - hard_weight) * target_probs - hard_weight * target_hits)
     ).astype(jnp.bfloat16)
-    gradient = lax.psum_scatter(
-        lax.dot_general(
-            logit_grad, student_head, (((1,), (1,)), ((), ())), preferred_element_type=jnp.float32
-        ),
-        ("dp", "vocab"),
-        scatter_dimension=0,
-        tiled=True,
-    )
+    partial = lax.dot_general(
+        logit_grad, student_head, (((1,), (1,)), ((), ())), preferred_element_type=jnp.float32
+    ).astype(jnp.bfloat16)
+    shard_count = dp_count * vocab_count
+    partial = partial.reshape(shard_count, tokens_all // shard_count, partial.shape[1])
+    received = lax.all_to_all(partial, ("dp", "vocab"), split_axis=0, concat_axis=0, tiled=True)
+    gradient = jnp.sum(received.astype(jnp.float32), axis=0)
     return gradient.astype(jnp.bfloat16)
 
 

time: 264 us -> 212 us (0.80)
  blocking collectives: 139 us -> 90.8 us
    unnamed x1 -> x0, blocking collectives: 71 us -> none
    all_to_all x0 -> x1, blocking collectives: none -> 21.1 us  [on_device(): lax.all_to_all(partial, ('dp', 'vocab'), split_axis=0, concat_axis=0, til...]
  transfers between devices with their start and end apart: 2 -> 2, of which waited for: 1 -> 1; matrix products, arithmetic and copies ran while one was open for 6% -> 7% of each run, Pallas kernels for 0% -> 0%
where the time goes in v2:
time: 212 us
  blocking collectives  90.8 us (43%)
  matrix products  63.9 us (30%)
  waiting for transfers between devices  25.5 us (12%)
  between operations  13.6 us (6%)
  local copies, waits for them, and re-layouts  7.64 us (4%)
  other arithmetic  6.18 us (3%)
  starting transfers between devices  3.97 us (2%)
    all_gather x1, blocking collectives, on_device(): all_stats = lax.all_gather(stats, ('dp', 'vocab'), axis=0, tiled=False)  69.7 us
    all_gather x1, waiting for transfers between devices, on_device(): gathered = lax.all_gather(packed, 'dp', axis=0, tiled=True)  25.5 us
    dot_general x1, matrix products, on_device(): jnp.dot(teacher_all, teacher_head, preferred_element_type=jnp.float32)  23.2 us
    all_to_all x1, blocking collectives, on_device(): lax.all_to_all(partial, ('dp', 'vocab'), split_axis=0, concat_axis=0, til...  21.1 us
    dot_general x1, matrix products, on_device(): lax.dot_general(logit_grad, student_head, (((1,), (1,)), ((), ())), prefe...  16.4 us
    dot_general x1, matrix products, on_device(): jnp.dot(student_all, student_head, preferred_element_type=jnp.float32)  13.9 us
  transfers between devices with their start and end apart: 2, of which 1 were waited for; matrix products, arithmetic and copies ran while one was open for 7% of the time, Pallas kernels for 0%

profile of v2, /device:TPU:1, one launch (start us, length us, event | category | flops | bytes accessed | tf_op | source)
XLA Modules:
  0.0 211.5 jit_solution(11825458879451816008)
XLA Ops:
  6.5 0.0 all-gather.4.cloned.1.call-start
  6.5 0.7 convert_convert_fusion
  7.2 0.7 convert_convert_fusion.2
  7.9 0.1 copy.29
  8.0 0.1 convert_element_type.93
  8.1 0.8 copy.28
  8.9 0.1 reshape.83
  9.0 0.6 reduce-window.14
  9.6 0.2 slice_reduce_fusion.1
  9.9 0.1 add_bitcast_fusion.1
  10.0 0.1 fusion.46
  10.1 1.6 pad_maximum_fusion
  11.6 0.0 all-gather.4.cloned.1.call-update
  11.7 25.5 %all-gather.4.cloned.1.call-done = bf16[64,9344]{1,0:T(8,128)(2,1)} async-done(((bf16[8,9344]{1,0:T(8,128)(2,1)}), bf16[64,9344]{1,0:T(8,128)(2,1)}) %all-gather.4.cloned.1.call-update) | async-done | bytes 1196048 | tf_op jit(solution)/shard_map/all_gather | solution.py:58
  37.1 23.2 %fusion.54 = (f32[64]{0:T(128)S(1)}, f32[64,6144]{1,0:T(8,128)S(1)}) fusion(bf16[5120,6144]{1,0:T(8,128)(2,1)} %param.9, bf16[64,9344]{1,0:T(8,128)(2,1)} %all-gather.4.cloned.1.call-done), kind=kOutput, calls=%fused_computation.91 | convolution fusion | flops 4026925056 | bytes 65143040 | tf_op jit(solution)/shard_map/dot_general | solution.py:71
  60.4 0.3 fusion.14
  60.7 0.1 copy.42
  60.8 4.0 %convert_reduce_fusion = (f32[64]{0:T(128)S(1)}, bf16[48,64,4,128]{3,1,2,0:T(8,128)(2,1)S(1)}) fusion(bf16[48,4,128,128]{3,2,1,0:T(8,128)(2,1)} %param.12, bf16[64,48,128,1]{2,1,0,3:T(8,128)(2,1)S(1)} %bitcast.78), kind=kOutput, calls=%fused_computation.4 | convolution fusion | flops 407371712 | bytes 10223872 | tf_op jit(solution)/shard_map/gkc,krcd->krgd/dot_general | solution.py:75
  64.8 2.4 %fusion.6 = bf16[24,8,64,128]{3,1,2,0:T(8,128)(2,1)S(1)} fusion(bf16[24,8,64,128]{3,2,1,0:T(8,128)(2,1)S(1)} %bitcast.76, s32[192]{0:T(256)S(1)} %get-tuple-element.11), kind=kOutput, calls=%fused_computation.10 | convolution fusion | flops 605589504 | bytes 6292224 | tf_op jit(solution)/shard_map/dot_general | solution.py:89
  67.1 0.9 copy.44
  68.0 3.8 %copy.32 = bf16[8,24,64,128]{3,1,2,0:T(8,128)(2,1)} copy(bf16[8,24,64,128]{3,2,1,0:T(8,128)(2,1)S(1)} %bitcast.75) | data formatting | bytes 6291456 | tf_op jit(solution)/shard_map/reshape | solution.py:94
  71.8 0.0 slice-start
  71.8 4.0 %all-to-all-start = ((bf16[8,24,64,128]{3,1,2,0:T(8,128)(2,1)}), bf16[8,24,64,128]{3,1,2,0:T(8,128)(2,1)S(1)}, u32[]{:S(2)}, u32[]{:S(2)}) async-start(bf16[8,24,64,128]{3,1,2,0:T(8,128)(2,1)} %copy.32), calls=%async_computation | async-start | bytes 6291456 | tf_op jit(solution)/shard_map/all_to_all | solution.py:95
  75.8 0.0 slice-done
  75.8 0.1 convert_add_fusion
  75.9 0.1 eq.99
  76.0 0.6 reduce-window.16
  76.6 0.2 slice_reduce_fusion
  76.9 13.9 %fusion.55 = (f32[64]{0:T(128)S(1)}, f32[64,4096]{1,0:T(8,128)S(1)}) fusion(bf16[4096,4096]{1,0:T(8,128)(2,1)} %param.14, bf16[64,9344]{1,0:T(8,128)(2,1)} %all-gather.4.cloned.1.call-done), kind=kOutput, calls=%fused_computation.92 | convolution fusion | flops 2147745792 | bytes 35127552 | tf_op jit(solution)/shard_map/dot_general | solution.py:97
  90.7 0.0 copy-start
  90.7 1.0 copy-done
  91.7 0.3 exponential_reduce_fusion
  92.0 69.7 %all-gather.1 = f32[16,4,64]{2,1,0:T(4,128)S(1)} all-gather(f32[1,4,64]{2,1,0:T(4,128)S(1)} %maximum_bitcast_fusion), channel_id=2, replica_groups=mesh['groups'=2,'dp'=8,'vocab'=2] {'dp','vocab'}, dimensions={0}, use_global_device_ids=true | all-gather | bytes 17408 | tf_op jit(solution)/shard_map/all_gather | solution.py:104
  161.8 0.1 round-nearest-even_convert_fusion
  161.9 0.1 add_bitcast_fusion
  162.0 0.2 convolution_bitcast_fusion
  162.2 0.0 all-to-all-done
  162.2 0.0 copy-start.1
  162.2 3.9 %fusion = f32[64,128,32,1]{1,2,0,3:T(8,128)S(1)} fusion(f32[8,24,32,1]{2,1,3,0:T(8,128)S(1)} %convolution_bitcast_fusion, bf16[8,24,64,128]{3,1,2,0:T(8,128)(2,1)S(1)} %all-to-all-done, f32[8,64]{1,0:T(8,128)S(1)} %bitcast.86), kind=kOutput, calls=%fused_computation.1 | convolution fusion | flops 607125504 | bytes 4220928 | tf_op jit(solution)/shard_map/xcs,xctd->tsd/dot_general | solution.py:125
  166.1 0.0 copy-done.1
  166.1 16.4 %convolution_convert_fusion.1 = bf16[64,4096]{1,0:T(8,128)(2,1)S(1)} fusion(bf16[4096,4096]{1,0:T(8,128)(2,1)} %param.14, f32[8,8,32,128]{3,2,1,0:T(8,128)S(1)} %bitcast.77, f32[64,4096]{1,0:T(8,128)S(1)} %copy-done.1, s32[4096]{0:T(1024)S(1)} %iota_add_fusion, f32[64]{0:T(128)S(1)} %get-tuple-element.21, f32[64]{0:T(128)S(1)} %get-tuple-element.22, ...), kind=kOutput, calls=%fused_computation.5 | convolution fusion | flops 2150367232 | bytes 36193280 | tf_op jit(solution)/shard_map/dot_general | solution.py:138
  182.5 0.2 reshape.94
  182.7 21.1 %all_to_all.10 = bf16[16,4,4096]{2,1,0:T(4,128)(2,1)S(1)} all-to-all(bf16[16,4,4096]{2,1,0:T(4,128)(2,1)S(1)} %reshape.94), channel_id=1, replica_groups=mesh['groups'=2,'dp'=8,'vocab'=2] {'dp','vocab'}, dimensions={0} | all-to-all | bytes 1048576 | tf_op jit(solution)/shard_map/all_to_all | solution.py:143
  203.8 0.8 reduce_sum.62
  (19 shorter events, 0.3 us)
Async XLA Ops:
  6.5 30.6 %all-gather.4.cloned.1.call-start = ((), (), s32[]{:S(2)}) async-start(), calls=%async_computation.2 | async-start | bytes 1345536 | tf_op jit(solution)/shard_map/all_gather | solution.py:58
  71.8 4.0 %slice-start = ((bf16[64,9344]{1,0:T(8,128)(2,1)}), bf16[64,128]{1,0:T(8,128)(2,1)S(1)}, s32[]{:S(2)}) async-start(bf16[64,9344]{1,0:T(8,128)(2,1)} %all-gather.4.cloned.1.call-done), calls=%async_computation.3 | async-start | bytes 32768 | tf_op jit(solution)/shard_map/slice | solution.py:62
  71.8 90.4 %all-to-all-start = ((bf16[8,24,64,128]{3,1,2,0:T(8,128)(2,1)}), bf16[8,24,64,128]{3,1,2,0:T(8,128)(2,1)S(1)}, u32[]{:S(2)}, u32[]{:S(2)}) async-start(bf16[8,24,64,128]{3,1,2,0:T(8,128)(2,1)} %copy.32), calls=%async_computation | async-start | bytes 6291456 | tf_op jit(solution)/shard_map/all_to_all | solution.py:95
  90.7 1.0 copy-start
  162.2 3.9 %copy-start.1 = (f32[64,4096]{1,0:T(8,128)S(1)}, f32[64,4096]{1,0:T(8,128)}, u32[]{:S(2)}) copy-start(f32[64,4096]{1,0:T(8,128)} %copy-done) | copy-start | bytes 3145732
Sparse Core Ops, SparseCore 0:
  11.8 25.3 all-gather.3

commit v3 on v2

--- a/solution.py
+++ b/solution.py
@@ -34,21 +34,13 @@
     fan_count = map_dest.shape[1]
     student_cols = student_head.shape[1]
     student_blocks = student_cols // block_size
-    capacity = max(2, (teacher_blocks * fan_count + dp_count - 1) // dp_count)
     device_flat = my_dp * vocab_count + my_vocab
     item_count = teacher_blocks * fan_count
     local_tokens = teacher_hidden.shape[0]
     teacher_width = teacher_hidden.shape[1]
     student_width = student_hidden.shape[1]
 
-    coded = jnp.concatenate(
-        [
-            _code(map_dest.reshape(item_count)),
-            _code(map_slot.reshape(item_count)),
-            _code(targets // 256),
-            _code(targets % 256),
-        ]
-    )
+    coded = jnp.concatenate([_code(targets // 256), _code(targets % 256)])
     extra_width = -(-coded.shape[0] // local_tokens)
     extra_width = -(-extra_width // 128) * 128
     coded = jnp.pad(coded, (0, extra_width * local_tokens - coded.shape[0]))
@@ -62,10 +54,8 @@
     extra_all = gathered[:, teacher_width + student_width :].reshape(
         dp_count, local_tokens * extra_width
     )
-    src_dest = _decode(extra_all[:, :item_count])
-    src_slot = _decode(extra_all[:, item_count : 2 * item_count])
-    t_hi = _decode(extra_all[:, 2 * item_count : 2 * item_count + local_tokens])
-    t_lo = _decode(extra_all[:, 2 * item_count + local_tokens : 2 * item_count + 2 * local_tokens])
+    t_hi = _decode(extra_all[:, :local_tokens])
+    t_lo = _decode(extra_all[:, local_tokens : 2 * local_tokens])
     all_targets = (t_hi * 256 + t_lo).reshape(tokens_all)
 
     teacher_logits = jnp.dot(teacher_all, teacher_head, preferred_element_type=jnp.float32)
@@ -77,54 +67,58 @@
     ).astype(jnp.bfloat16)
     mapped_mass = jnp.sum(mapped_terms.astype(jnp.float32), axis=(0, 1, 3))
 
-    dest_flat = map_dest.reshape(item_count)
-    dest_onehot = (dest_flat[:, None] == jnp.arange(dp_count, dtype=jnp.int32)[None, :]).astype(
-        jnp.int32
-    )
-    earlier_same = jnp.sum(jnp.cumsum(dest_onehot, axis=0) * dest_onehot, axis=1) - 1
-    slot_index = dest_flat * capacity + earlier_same
+    relative = jnp.bitwise_xor(map_dest.reshape(item_count), my_dp)
+    row = relative * student_blocks + map_slot.reshape(item_count)
     placement = (
-        jnp.arange(dp_count * capacity, dtype=jnp.int32)[:, None] == slot_index[None, :]
+        jnp.arange(dp_count * student_blocks, dtype=jnp.int32)[:, None] == row[None, :]
     ).astype(jnp.bfloat16)
-    outgoing = jnp.dot(
+    held = jnp.dot(
         placement,
         mapped_terms.reshape(item_count, tokens_all * block_size),
         preferred_element_type=jnp.float32,
-    )
-    outgoing = outgoing.astype(jnp.bfloat16).reshape(dp_count, capacity, tokens_all, block_size)
-    incoming = lax.all_to_all(outgoing, "dp", split_axis=0, concat_axis=0, tiled=True)
+    ).reshape(dp_count, student_blocks, tokens_all, block_size)
 
     student_logits = jnp.dot(student_all, student_head, preferred_element_type=jnp.float32)
     student_local_peak = jnp.max(student_logits, axis=1)
     student_local_total = jnp.sum(jnp.exp(student_logits - student_local_peak[:, None]), axis=1)
 
-    stats = jnp.stack(
-        [teacher_local_peak, mapped_mass, student_local_peak, student_local_total]
-    )
-    all_stats = lax.all_gather(stats, ("dp", "vocab"), axis=0, tiled=False)
-    teacher_peak = jnp.max(all_stats[:, 0], axis=0)
-    teacher_scale = jnp.exp(all_stats[:, 0] - teacher_peak[None, :])
-    target_total = jnp.sum(teacher_scale * all_stats[:, 1], axis=0)
-    student_peak = jnp.max(all_stats[:, 2], axis=0)
-    student_total = jnp.sum(
-        jnp.exp(all_stats[:, 2] - student_peak[None, :]) * all_stats[:, 3], axis=0
-    )
-    source_scale = teacher_scale.reshape(dp_count, vocab_count, tokens_all)[:, my_vocab]
+    peak, mass = teacher_local_peak, mapped_mass
+    s_peak, s_total = student_local_peak, student_local_total
 
-    is_mine = (src_dest == my_dp).astype(jnp.int32)
-    rank = jnp.cumsum(is_mine, axis=1) - 1
-    at_cap = (
-        (rank[:, :, None] == jnp.arange(capacity, dtype=jnp.int32)[None, None, :])
-        & (is_mine[:, :, None] > 0)
-    ).astype(jnp.float32)
-    at_slot = (
-        src_slot[:, :, None] == jnp.arange(student_blocks, dtype=jnp.int32)[None, None, :]
-    ).astype(jnp.float32)
-    marks = jnp.einsum("xec,xes->xcs", at_cap, at_slot)
-    scaled_in = incoming.astype(jnp.float32) * source_scale[:, None, :, None]
-    mapped = jnp.einsum(
-        "xcs,xctd->tsd", marks, scaled_in, precision=lax.Precision.HIGHEST,
-        preferred_element_type=jnp.float32,
+    def merge(stats, other):
+        new_peak = jnp.maximum(stats[0], other[0])
+        new_s_peak = jnp.maximum(stats[2], other[2])
+        own, far = jnp.exp(stats[0] - new_peak), jnp.exp(other[0] - new_peak)
+        s_own, s_far = jnp.exp(stats[2] - new_s_peak), jnp.exp(other[2] - new_s_peak)
+        merged = jnp.stack(
+            [new_peak, stats[1] * own + other[1] * far, new_s_peak,
+             stats[3] * s_own + other[3] * s_far]
+        )
+        return merged, own, far
+
+    stats = jnp.stack([peak, mass, s_peak, s_total])
+    stage = 1
+    while stage < dp_count:
+        pairs = [(j, j ^ stage) for j in range(dp_count)]
+        halves = held.reshape(held.shape[0] // 2, 2, student_blocks, tokens_all, block_size)
+        arrived = lax.ppermute(halves[:, 1].astype(jnp.bfloat16), "dp", pairs)
+        other = lax.ppermute(stats, "dp", pairs)
+        stats, own, far = merge(stats, other)
+        held = (
+            halves[:, 0] * own[None, None, :, None]
+            + arrived.astype(jnp.float32) * far[None, None, :, None]
+        )
+        stage *= 2
+    column_peak = stats[0]
+    stage = 1
+    while stage < vocab_count:
+        pairs = [(j, j ^ stage) for j in range(vocab_count)]
+        stats = merge(stats, lax.ppermute(stats, "vocab", pairs))[0]
+        stage *= 2
+    teacher_peak, target_total = stats[0], stats[1]
+    student_peak, student_total = stats[2], stats[3]
+    mapped = jnp.transpose(
+        held[0] * jnp.exp(column_peak - teacher_peak)[None, :, None], (1, 0, 2)
     ).reshape(tokens_all, student_cols)
 
     target_probs = mapped / target_total[:, None]

time: 212 us -> 195 us (0.920)
  blocking collectives: 90.8 us -> 19.9 us
  waiting for transfers between devices: 25.5 us -> 74.1 us
  other arithmetic: 6.18 us -> 10.5 us
  matrix products: 63.9 us -> 59.9 us
  starting transfers between devices: 3.97 us -> 6.86 us
  local copies, waits for them, and re-layouts: 7.64 us -> 10.2 us
    all_gather x1 -> x0, blocking collectives: 69.7 us -> none  [on_device(): all_stats = lax.all_gather(stats, ('dp', 'vocab'), axis=0, tiled=False)]
    ppermute x0 -> x7, waiting for transfers between devices: none -> 49.5 us  [the longest x3 43.9 us: on_device(): arrived = lax.ppermute(halves[:, 1].astype(jnp.bfloat16), 'dp', pairs)]
    ppermute x0 -> x7, starting transfers between devices: none -> 6.86 us  [the longest x3 2.91 us: on_device(): other = lax.ppermute(stats, 'dp', pairs)]
    dot_general x2 -> x0, matrix products: 4.08 us -> none  [the longest x1 3.88 us: on_device(): jnp.einsum('xcs,xctd->tsd', marks, scaled_in, precision=lax.Precision.HIG...]
    unnamed x7 -> x9, local copies, waits for them, and re-layouts: 2.75 us -> 6.8 us
    all_to_all x1 -> x0, starting transfers between devices: 3.97 us -> none  [on_device(): lax.all_to_all(outgoing, 'dp', split_axis=0, concat_axis=0, tiled=True)]
    reshape x2 -> x0, local copies, waits for them, and re-layouts: 3.91 us -> none  [the longest x1 3.81 us: on_device(): outgoing.astype(jnp.bfloat16)]
    add x1 -> x6, other arithmetic: 0.01 us -> 3.03 us  [the longest x1 2.25 us: on_device(): halves[:, 0] * own[None, None, :, None]]
  transfers between devices with their start and end apart: 2 -> 8, of which waited for: 1 -> 7; matrix products, arithmetic and copies ran while one was open for 7% -> 8% of each run, Pallas kernels for 0% -> 0%
where the time goes in v3:
time: 195 us
  waiting for transfers between devices  74.1 us (38%)
  matrix products  59.9 us (31%)
  blocking collectives  19.9 us (10%)
  between operations  13.6 us (7%)
  other arithmetic  10.5 us (5%)
  local copies, waits for them, and re-layouts  10.2 us (5%)
  starting transfers between devices  6.86 us (4%)
    ppermute x3, waiting for transfers between devices, on_device(): arrived = lax.ppermute(halves[:, 1].astype(jnp.bfloat16), 'dp', pairs)  43.9 us
    all_gather x1, waiting for transfers between devices, on_device(): gathered = lax.all_gather(packed, 'dp', axis=0, tiled=True)  24.6 us
    dot_general x1, matrix products, on_device(): jnp.dot(teacher_all, teacher_head, preferred_element_type=jnp.float32)  23.2 us
    all_to_all x1, blocking collectives, on_device(): lax.all_to_all(partial, ('dp', 'vocab'), split_axis=0, concat_axis=0, til...  19.9 us
    dot_general x1, matrix products, on_device(): lax.dot_general(logit_grad, student_head, (((1,), (1,)), ((), ())), prefe...  16.4 us
    dot_general x1, matrix products, on_device(): jnp.dot(student_all, student_head, preferred_element_type=jnp.float32)  13.8 us
    unnamed x9, local copies, waits for them, and re-layouts  6.8 us
    ppermute x3, waiting for transfers between devices, on_device(): other = lax.ppermute(stats, 'dp', pairs)  4.22 us
  transfers between devices with their start and end apart: 8, of which 7 were waited for; matrix products, arithmetic and copies ran while one was open for 8% of the time, Pallas kernels for 0%

profile of v3, /device:TPU:1, one launch (start us, length us, event | category | flops | bytes accessed | tf_op | source)
XLA Modules:
  0.0 195.1 jit_solution(2562622014719721813)
XLA Ops:
  6.5 0.0 all-gather.2.cloned.1.call-start
  6.5 0.7 convert_convert_fusion
  7.2 0.1 fusion.42
  7.3 1.6 pad_maximum_fusion
  8.9 0.0 all-gather.2.cloned.1.call-update
  8.9 0.7 multiply_add_fusion.1
  9.6 0.1 copy.14
  9.7 0.1 add.144
  9.8 24.6 %all-gather.2.cloned.1.call-done = bf16[64,9344]{1,0:T(8,128)(2,1)} async-done(((bf16[8,9344]{1,0:T(8,128)(2,1)}), bf16[64,9344]{1,0:T(8,128)(2,1)}) %all-gather.2.cloned.1.call-update) | async-done | bytes 1196048 | tf_op jit(solution)/shard_map/all_gather | solution.py:50
  34.4 23.2 %fusion.75 = (f32[64]{0:T(128)S(1)}, f32[64,6144]{1,0:T(8,128)S(1)}) fusion(bf16[5120,6144]{1,0:T(8,128)(2,1)} %param.9, bf16[64,9344]{1,0:T(8,128)(2,1)} %all-gather.2.cloned.1.call-done), kind=kOutput, calls=%fused_computation.139 | convolution fusion | flops 4026925056 | bytes 65143040 | tf_op jit(solution)/shard_map/dot_general | solution.py:61
  57.6 0.3 fusion.18
  57.9 0.1 copy.29
  58.0 4.0 %convert_reduce_fusion = (f32[64]{0:T(128)S(1)}, bf16[48,64,4,128]{3,1,2,0:T(8,128)(2,1)S(1)}) fusion(bf16[48,4,128,128]{3,2,1,0:T(8,128)(2,1)} %param.12, bf16[64,48,128,1]{2,1,0,3:T(8,128)(2,1)S(1)} %bitcast.249), kind=kOutput, calls=%fused_computation | convolution fusion | flops 407371712 | bytes 10223872 | tf_op jit(solution)/shard_map/gkc,krcd->krgd/dot_general | solution.py:65
  62.0 2.9 %copy.54 = bf16[24,8,64,128]{3,1,2,0:T(8,128)(2,1)S(1)} copy(bf16[24,8,64,128]{3,2,1,0:T(8,128)(2,1)S(1)} %bitcast.246) | data formatting | bytes 6291456
  64.8 0.9 copy.31
  65.7 2.5 %fusion.2 = f32[4,2,32,64,128]{4,2,3,1,0:T(8,128)S(1)} fusion(bf16[64,128,192,1,1]{1,0,2,4,3:T(8,128)(2,1)S(1)} %bitcast.247, s32[192]{0:T(256)S(1)} %add.144, s32[4,2,32]{2,1,0:T(2,128)S(1)} %multiply_add_fusion), kind=kOutput, calls=%fused_computation.7 | convolution fusion | flops 805355520 | bytes 11536128 | tf_op jit(solution)/shard_map/dot_general | solution.py:75
  68.2 0.0 copy-start.1
  68.3 1.8 fusion.4
  70.1 0.3 collective-permute-start.4
  70.4 0.0 copy-done.1
  70.4 13.8 %fusion.76 = (f32[64]{0:T(128)S(1)}, f32[64,4096]{1,0:T(8,128)S(1)}) fusion(bf16[4096,4096]{1,0:T(8,128)(2,1)} %param.14, bf16[64,9344]{1,0:T(8,128)(2,1)S(1)} %copy-done.1), kind=kOutput, calls=%fused_computation.140 | convolution fusion | flops 2147745792 | bytes 35127552 | tf_op jit(solution)/shard_map/dot_general | solution.py:81
  84.2 0.3 exponential_reduce_fusion
  84.5 0.3 collective-permute-start
  84.9 0.9 collective-permute-done
  85.8 1.0 collective-permute-start.1
  86.8 1.5 collective-permute-done.1
  88.3 1.6 collective-permute-start.2
  89.9 1.8 collective-permute-done.2
  91.8 1.1 collective-permute-start.3
  92.9 1.4 collective-permute-done.3
  94.3 0.0 collective-permute-done.4
  94.3 2.3 %fusion.1 = f32[4,32,64,128]{3,1,2,0:T(8,128)S(1)} fusion(f32[4,2,32,64,128]{4,2,3,1,0:T(8,128)S(1)} %fusion.2, bf16[4,32,64,128]{3,1,2,0:T(8,128)(2,1)} %collective-permute-done.4, f32[64]{0:T(128)S(1)} %get-tuple-element.12, f32[64]{0:T(128)S(1)} %get-tuple-element.11), kind=kLoop, calls=%fused_computation.5 | loop fusion | flops 4194304 | bytes 10486272 | tf_op jit(solution)/shard_map/add | solution.py:108
  96.6 0.0 copy-start
  96.6 1.9 copy-done
  98.5 0.2 fusion.8
  98.7 1.0 collective-permute-start.5
  99.8 20.0 %collective-permute-done.5 = bf16[2,32,64,128]{3,1,2,0:T(8,128)(2,1)S(1)} collective-permute-done((bf16[2,32,64,128]{3,1,2,0:T(8,128)(2,1)S(1)}, bf16[2,32,64,128]{3,1,2,0:T(8,128)(2,1)S(1)}, u32[]{:S(2)}, u32[]{:S(2)}) %collective-permute-start.5) | collective-permute-done | bytes 1048608 | tf_op jit(solution)/shard_map/ppermute | solution.py:104
  119.8 0.0 copy-start.2
  119.8 1.0 copy-done.2
  120.8 0.0 slice-start
  120.8 2.3 %fusion.7 = f32[1,2,32,64,128]{4,2,3,1,0:T(8,128)S(1)} fusion(bf16[2,32,64,128]{3,1,2,0:T(8,128)(2,1)} %copy-done.2, f32[64]{0:T(128)S(1)} %get-tuple-element.9, f32[64]{0:T(128)S(1)} %get-tuple-element.8, f32[2,2,32,64,128]{4,2,3,1,0:T(8,128)} %bitcast.245), kind=kLoop, calls=%fused_computation.15 | loop fusion | flops 2097152 | bytes 5243392 | tf_op jit(solution)/shard_map/reshape | solution.py:103
  123.1 0.9 fusion.23
  124.0 1.5 collective-permute-start.6
  125.5 0.0 slice-done
  125.5 0.1 convert_add_fusion
  125.6 0.1 eq.56
  125.7 23.9 %collective-permute-done.6 = bf16[1,32,64,128]{3,1,2,0:T(8,128)(2,1)} collective-permute-done((bf16[1,32,64,128]{3,1,2,0:T(8,128)(2,1)}, bf16[1,32,64,128]{3,1,2,0:T(8,128)(2,1)}, u32[]{:S(2)}, u32[]{:S(2)}) %collective-permute-start.6) | collective-permute-done | bytes 524320 | tf_op jit(solution)/shard_map/ppermute | solution.py:104
  149.6 1.3 fusion.16
  150.9 16.4 %convolution_convert_fusion = bf16[64,4096]{1,0:T(8,128)(2,1)S(1)} fusion(bf16[4096,4096]{1,0:T(8,128)(2,1)} %param.14, f32[8,8,32,128]{3,2,1,0:T(8,128)S(1)} %bitcast.248, f32[64,4096]{1,0:T(8,128)S(1)} %get-tuple-element.39, s32[4096]{0:T(1024)S(1)} %iota_add_fusion, f32[64]{0:T(128)S(1)} %get-tuple-element.7, f32[64]{0:T(128)S(1)} %get-tuple-element.5, ...), kind=kOutput, calls=%fused_computation.1 | convolution fusion | flops 2150367232 | bytes 36193280 | tf_op jit(solution)/shard_map/dot_general | solution.py:132
  167.3 0.2 reshape.401
  167.5 19.9 %all_to_all.5 = bf16[16,4,4096]{2,1,0:T(4,128)(2,1)S(1)} all-to-all(bf16[16,4,4096]{2,1,0:T(4,128)(2,1)S(1)} %reshape.401), channel_id=1, replica_groups=mesh['groups'=2,'dp'=8,'vocab'=2] {'dp','vocab'}, dimensions={0} | all-to-all | bytes 1048576 | tf_op jit(solution)/shard_map/all_to_all | solution.py:137
  187.4 0.8 reduce_sum.32
  (12 shorter events, 0.2 us)
Async XLA Ops:
  6.5 27.8 %all-gather.2.cloned.1.call-start = ((), (), s32[]{:S(2)}) async-start(), calls=%async_computation.1 | async-start | bytes 1345536 | tf_op jit(solution)/shard_map/all_gather | solution.py:50
  68.2 2.1 %copy-start.1 = (bf16[64,9344]{1,0:T(8,128)(2,1)S(1)}, bf16[64,9344]{1,0:T(8,128)(2,1)}, u32[]{:S(2)}) copy-start(bf16[64,9344]{1,0:T(8,128)(2,1)} %all-gather.2.cloned.1.call-done) | copy-start | bytes 3588100
  70.1 24.2 %collective-permute-start.4 = (bf16[4,32,64,128]{3,1,2,0:T(8,128)(2,1)}, bf16[4,32,64,128]{3,1,2,0:T(8,128)(2,1)}, u32[]{:S(2)}, u32[]{:S(2)}) collective-permute-start(bf16[4,32,64,128]{3,1,2,0:T(8,128)(2,1)} %fusion.4), channel_id=1, source_target_pairs={{0,2},{2,0},{4,6},{6,4},{8,10},{10,8},{12,14},{14,12},{1,3},{3,1},... | collective-permute-start | bytes 6291464 | tf_op jit(solution)/shard_map/ppermute | solution.py:104
  84.5 1.2 collective-permute-start
  85.8 2.5 %collective-permute-start.1 = (f32[4,64]{1,0:T(4,128)S(1)}, f32[4,64]{1,0:T(4,128)S(1)}, u32[]{:S(2)}, u32[]{:S(2)}) collective-permute-start(f32[4,64]{1,0:T(4,128)S(1)} %pad_maximum_fusion.2), channel_id=1, source_target_pairs={{0,4},{2,6},{4,0},{6,2},{8,12},{10,14},{12,8},{14,10},{1,5},{3,7},... | collective-permute-start | bytes 3080 | tf_op jit(solution)/shard_map/ppermute | solution.py:105
  88.3 3.4 %collective-permute-start.2 = (f32[4,64]{1,0:T(4,128)S(1)}, f32[4,64]{1,0:T(4,128)S(1)}, u32[]{:S(2)}, u32[]{:S(2)}) collective-permute-start(f32[4,64]{1,0:T(4,128)S(1)} %pad_maximum_fusion.3), channel_id=1, source_target_pairs={{0,8},{2,10},{4,12},{6,14},{8,0},{10,2},{12,4},{14,6},{1,9},{3,11}... | collective-permute-start | bytes 3080 | tf_op jit(solution)/shard_map/ppermute | solution.py:105
  91.8 2.5 %collective-permute-start.3 = (f32[4,64]{1,0:T(4,128)S(1)}, f32[4,64]{1,0:T(4,128)S(1)}, u32[]{:S(2)}, u32[]{:S(2)}) collective-permute-start(f32[4,64]{1,0:T(4,128)S(1)} %pad_maximum_fusion.4), channel_id=1, source_target_pairs={{0,1},{1,0},{2,3},{3,2},{4,5},{5,4},{6,7},{7,6},{8,9},{9,8},{10,11... | collective-permute-start | bytes 3080 | tf_op jit(solution)/shard_map/ppermute | solution.py:116
  96.6 1.9 copy-start
  98.7 21.1 %collective-permute-start.5 = (bf16[2,32,64,128]{3,1,2,0:T(8,128)(2,1)S(1)}, bf16[2,32,64,128]{3,1,2,0:T(8,128)(2,1)S(1)}, u32[]{:S(2)}, u32[]{:S(2)}) collective-permute-start(bf16[2,32,64,128]{3,1,2,0:T(8,128)(2,1)S(1)} %fusion.8), channel_id=1, source_target_pairs={{0,4},{2,6},{4,0},{6,2},{8,12},{10,14},{12,8},{14,10},{1,5},{3,7},... | collective-permute-start | bytes 3145736 | tf_op jit(solution)/shard_map/ppermute | solution.py:104
  119.8 1.0 copy-start.2
  120.8 4.7 %slice-start = ((bf16[64,9344]{1,0:T(8,128)(2,1)}), bf16[64,128]{1,0:T(8,128)(2,1)S(1)}, s32[]{:S(2)}) async-start(bf16[64,9344]{1,0:T(8,128)(2,1)} %all-gather.2.cloned.1.call-done), calls=%async_computation.2 | async-start | bytes 32768 | tf_op jit(solution)/shard_map/slice | solution.py:54
  124.0 25.6 %collective-permute-start.6 = (bf16[1,32,64,128]{3,1,2,0:T(8,128)(2,1)}, bf16[1,32,64,128]{3,1,2,0:T(8,128)(2,1)}, u32[]{:S(2)}, u32[]{:S(2)}) collective-permute-start(bf16[1,32,64,128]{3,1,2,0:T(8,128)(2,1)} %fusion.23), channel_id=1, source_target_pairs={{0,8},{2,10},{4,12},{6,14},{8,0},{10,2},{12,4},{14,6},{1,9},{3,11}... | collective-permute-start | bytes 1572872 | tf_op jit(solution)/shard_map/ppermute | solution.py:104
Sparse Core Ops, SparseCore 0:
  9.0 25.3 all-gather.1

commit v4 on v3

--- a/solution.py
+++ b/solution.py
@@ -45,15 +45,16 @@
     extra_width = -(-extra_width // 128) * 128
     coded = jnp.pad(coded, (0, extra_width * local_tokens - coded.shape[0]))
     packed = jnp.concatenate(
-        [teacher_hidden, student_hidden, coded.reshape(local_tokens, extra_width)], axis=1
+        [teacher_hidden, coded.reshape(local_tokens, extra_width)], axis=1
     )
     gathered = lax.all_gather(packed, "dp", axis=0, tiled=True)
+    student_all = lax.all_to_all(
+        jnp.broadcast_to(student_hidden[None], (dp_count,) + student_hidden.shape),
+        "dp", split_axis=0, concat_axis=0, tiled=True,
+    ).reshape(dp_count * local_tokens, student_width)
     tokens_all = gathered.shape[0]
     teacher_all = gathered[:, :teacher_width]
-    student_all = gathered[:, teacher_width : teacher_width + student_width]
-    extra_all = gathered[:, teacher_width + student_width :].reshape(
-        dp_count, local_tokens * extra_width
-    )
+    extra_all = gathered[:, teacher_width:].reshape(dp_count, local_tokens * extra_width)
     t_hi = _decode(extra_all[:, :local_tokens])
     t_lo = _decode(extra_all[:, local_tokens : 2 * local_tokens])
     all_targets = (t_hi * 256 + t_lo).reshape(tokens_all)

time: 195 us -> 190 us (0.974)
  waiting for transfers between devices: 74.1 us -> 46.8 us
  blocking collectives: 19.9 us -> 43.3 us
  between operations: 13.6 us -> 0.24 us
  starting transfers between devices: 6.86 us -> 15.9 us
  local copies, waits for them, and re-layouts: 10.2 us -> 13.7 us
    all_gather x1 -> x0, waiting for transfers between devices: 24.6 us -> none  [on_device(): gathered = lax.all_gather(packed, 'dp', axis=0, tiled=True)]
    all_gather x0 -> x1, blocking collectives: none -> 21.7 us  [on_device(): gathered = lax.all_gather(packed, 'dp', axis=0, tiled=True)]
    all_to_all x0 -> x1, starting transfers between devices: none -> 6.37 us  [on_device(): lax.all_to_all(jnp.broadcast_to(student_hidden[None], (dp_count,) + stude...]
    unnamed x9 -> x17, local copies, waits for them, and re-layouts: 6.8 us -> 9.97 us
  transfers between devices with their start and end apart: 8 -> 8, of which waited for: 7 -> 6; matrix products, arithmetic and copies ran while one was open for 8% -> 27% of each run, Pallas kernels for 0% -> 0%
where the time goes in v4:
time: 190 us; the launch traced here: 189 us
  matrix products  60.4 us (32%)
  waiting for transfers between devices  46.8 us (25%)
  blocking collectives  43.3 us (23%)
  starting transfers between devices  15.9 us (8%)
  local copies, waits for them, and re-layouts  13.7 us (7%)
  other arithmetic  9.09 us (5%)
    ppermute x3, waiting for transfers between devices, on_device(): arrived = lax.ppermute(halves[:, 1].astype(jnp.bfloat16), 'dp', pairs)  42.5 us
    dot_general x1, matrix products, on_device(): jnp.dot(teacher_all, teacher_head, preferred_element_type=jnp.float32)  23.4 us
    all_gather x1, blocking collectives, on_device(): gathered = lax.all_gather(packed, 'dp', axis=0, tiled=True)  21.7 us
    all_to_all x1, blocking collectives, on_device(): lax.all_to_all(partial, ('dp', 'vocab'), split_axis=0, concat_axis=0, til...  21.6 us
    dot_general x1, matrix products, on_device(): lax.dot_general(logit_grad, student_head, (((1,), (1,)), ((), ())), prefe...  16.4 us
    dot_general x1, matrix products, on_device(): jnp.dot(student_all, student_head, preferred_element_type=jnp.float32)  14.2 us
    unnamed x17, local copies, waits for them, and re-layouts  9.97 us
    all_to_all x1, starting transfers between devices, on_device(): lax.all_to_all(jnp.broadcast_to(student_hidden[None], (dp_count,) + stude...  6.37 us
  transfers between devices with their start and end apart: 8, of which 6 were waited for; matrix products, arithmetic and copies ran while one was open for 27% of the time, Pallas kernels for 0%

profile of v4, /device:TPU:1, one launch (start us, length us, event | category | flops | bytes accessed | tf_op | source)
XLA Modules:
  0.0 189.4 jit_solution(4004824478695724376)
XLA Ops:
  0.0 1.7 broadcast_in_dim.2
  1.7 6.4 %all-to-all-start = ((bf16[8,8,4096]{2,1,0:T(8,128)(2,1)}), bf16[8,8,4096]{2,1,0:T(8,128)(2,1)}, u32[]{:S(2)}, u32[]{:S(2)}) async-start(bf16[8,8,4096]{2,1,0:T(8,128)(2,1)} %broadcast_in_dim.2), calls=%async_computation | async-start | bytes 1048576 | tf_op jit(solution)/shard_map/all_to_all | solution.py:51
  8.0 0.7 convert_convert_fusion
  8.7 0.1 fusion.42
  8.8 0.9 pad_maximum_fusion
  9.7 21.7 %all_gather.3 = bf16[64,5248]{1,0:T(8,128)(2,1)S(1)} all-gather(bf16[8,5248]{1,0:T(8,128)(2,1)S(1)} %pad_maximum_fusion), channel_id=1, replica_groups=mesh['groups'=2,'dp'=8,'vocab'=2] {'dp'}, dimensions={0}, use_global_device_ids=true | all-gather | bytes 755712 | tf_op jit(solution)/shard_map/all_gather | solution.py:50
  31.4 0.0 copy-start.3
  31.4 23.4 %fusion.75 = (f32[64]{0:T(128)S(1)}, f32[64,6144]{1,0:T(8,128)S(1)}) fusion(bf16[5120,6144]{1,0:T(8,128)(2,1)} %param.9, bf16[64,5248]{1,0:T(8,128)(2,1)S(1)} %all_gather.3), kind=kOutput, calls=%fused_computation.139 | convolution fusion | flops 4026925056 | bytes 65143040 | tf_op jit(solution)/shard_map/dot_general | solution.py:62
  54.8 0.0 copy-done.3
  54.8 0.3 fusion.18
  55.1 0.1 copy.29
  55.2 0.0 copy-start.5
  55.2 0.0 copy-start.6
  55.2 4.0 %convert_reduce_fusion = (f32[64]{0:T(128)S(1)}, bf16[48,64,4,128]{3,1,2,0:T(8,128)(2,1)S(1)}) fusion(bf16[48,4,128,128]{3,2,1,0:T(8,128)(2,1)} %param.12, bf16[64,48,128,1]{2,1,0,3:T(8,128)(2,1)S(1)} %bitcast.254), kind=kOutput, calls=%fused_computation | convolution fusion | flops 407371712 | bytes 10223872 | tf_op jit(solution)/shard_map/gkc,krcd->krgd/dot_general | solution.py:66
  59.2 0.0 copy-done.5
  59.2 0.0 copy-done.6
  59.2 0.1 copy.14
  59.3 0.1 add.144
  59.4 2.8 %copy.54 = bf16[24,8,64,128]{3,1,2,0:T(8,128)(2,1)S(1)} copy(bf16[24,8,64,128]{3,2,1,0:T(8,128)(2,1)S(1)} %bitcast.251) | data formatting | bytes 6291456
  62.3 0.9 copy.31
  63.2 2.5 %fusion.2 = f32[4,2,32,64,128]{4,2,3,1,0:T(8,128)S(1)} fusion(bf16[64,128,192,1,1]{1,0,2,4,3:T(8,128)(2,1)S(1)} %bitcast.252, s32[192]{0:T(256)S(1)} %add.144, s32[4,2,32]{2,1,0:T(2,128)S(1)} %multiply_add_fusion), kind=kOutput, calls=%fused_computation.7 | convolution fusion | flops 805355520 | bytes 11536128 | tf_op jit(solution)/shard_map/dot_general | solution.py:76
  65.7 0.0 copy-start
  65.7 3.2 %copy-done = f32[4,2,32,64,128]{4,2,3,1,0:T(8,128)} copy-done((f32[4,2,32,64,128]{4,2,3,1,0:T(8,128)}, f32[4,2,32,64,128]{4,2,3,1,0:T(8,128)S(1)}, u32[]{:S(2)}) %copy-start) | copy-done | bytes 8388632
  68.9 0.5 fusion.4
  69.4 0.2 collective-permute-start.4
  69.6 0.0 all-to-all-done
  69.6 0.0 copy-start.1
  69.6 14.2 %fusion.76 = (f32[64]{0:T(128)S(1)}, f32[64,4096]{1,0:T(8,128)S(1)}) fusion(bf16[4096,4096]{1,0:T(8,128)(2,1)} %param.14, bf16[8,8,4096]{2,1,0:T(8,128)(2,1)} %all-to-all-done), kind=kOutput, calls=%fused_computation.140 | convolution fusion | flops 2147745792 | bytes 35127552 | tf_op jit(solution)/shard_map/dot_general | solution.py:82
  83.8 0.3 exponential_reduce_fusion
  84.2 0.4 collective-permute-start
  84.6 0.8 collective-permute-done
  85.4 1.7 collective-permute-start.1
  87.1 1.0 collective-permute-done.1
  88.1 2.2 %collective-permute-start.2 = (f32[4,64]{1,0:T(4,128)S(1)}, f32[4,64]{1,0:T(4,128)S(1)}, u32[]{:S(2)}, u32[]{:S(2)}) collective-permute-start(f32[4,64]{1,0:T(4,128)S(1)} %pad_maximum_fusion.3), channel_id=1, source_target_pairs={{0,8},{2,10},{4,12},{6,14},{8,0},{10,2},{12,4},{14,6},{1,9},{3,11}... | collective-permute-start | bytes 3080 | tf_op jit(solution)/shard_map/ppermute | solution.py:106
  90.3 1.2 collective-permute-done.2
  91.6 1.3 collective-permute-start.3
  92.8 1.2 collective-permute-done.3
  94.1 0.0 collective-permute-done.4
  94.1 0.0 copy-done.1
  94.1 0.0 slice-start
  94.1 2.2 %fusion.1 = f32[4,32,64,128]{3,1,2,0:T(8,128)S(1)} fusion(f32[4,2,32,64,128]{4,2,3,1,0:T(8,128)S(1)} %copy-done.1, bf16[4,32,64,128]{3,1,2,0:T(8,128)(2,1)} %collective-permute-done.4, f32[64]{0:T(128)S(1)} %get-tuple-element.12, f32[64]{0:T(128)S(1)} %get-tuple-element.11), kind=kLoop, calls=%fused_computation.5 | loop fusion | flops 4194304 | bytes 10486272 | tf_op jit(solution)/shard_map/add | solution.py:109
  96.3 0.0 copy-start.2
  96.3 1.9 %copy-done.2 = f32[4,32,64,128]{3,1,2,0:T(8,128)} copy-done((f32[4,32,64,128]{3,1,2,0:T(8,128)}, f32[4,32,64,128]{3,1,2,0:T(8,128)S(1)}, u32[]{:S(2)}) %copy-start.2) | copy-done | bytes 4194328
  98.3 0.2 fusion.8
  98.5 1.5 collective-permute-start.5
  100.0 0.0 slice-done
  100.1 19.6 %collective-permute-done.5 = bf16[2,32,64,128]{3,1,2,0:T(8,128)(2,1)S(1)} collective-permute-done((bf16[2,32,64,128]{3,1,2,0:T(8,128)(2,1)S(1)}, bf16[2,32,64,128]{3,1,2,0:T(8,128)(2,1)S(1)}, u32[]{:S(2)}, u32[]{:S(2)}) %collective-permute-start.5) | collective-permute-done | bytes 1048608 | tf_op jit(solution)/shard_map/ppermute | solution.py:105
  119.7 0.0 copy-start.4
  119.7 1.0 copy-done.4
  120.6 2.3 %fusion.7 = f32[1,2,32,64,128]{4,2,3,1,0:T(8,128)S(1)} fusion(bf16[2,32,64,128]{3,1,2,0:T(8,128)(2,1)} %copy-done.4, f32[64]{0:T(128)S(1)} %get-tuple-element.9, f32[64]{0:T(128)S(1)} %get-tuple-element.8, f32[2,2,32,64,128]{4,2,3,1,0:T(8,128)} %bitcast.250), kind=kLoop, calls=%fused_computation.15 | loop fusion | flops 2097152 | bytes 5243392 | tf_op jit(solution)/shard_map/reshape | solution.py:104
  122.9 0.9 fusion.23
  123.8 2.2 %collective-permute-start.6 = (bf16[1,32,64,128]{3,1,2,0:T(8,128)(2,1)}, bf16[1,32,64,128]{3,1,2,0:T(8,128)(2,1)}, u32[]{:S(2)}, u32[]{:S(2)}) collective-permute-start(bf16[1,32,64,128]{3,1,2,0:T(8,128)(2,1)} %fusion.23), channel_id=1, source_target_pairs={{0,8},{2,10},{4,12},{6,14},{8,0},{10,2},{12,4},{14,6},{1,9},{3,11}... | collective-permute-start | bytes 1572872 | tf_op jit(solution)/shard_map/ppermute | solution.py:105
  126.0 0.1 convert_add_fusion
  126.1 0.1 eq.56
  126.2 22.9 %collective-permute-done.6 = bf16[1,32,64,128]{3,1,2,0:T(8,128)(2,1)} collective-permute-done((bf16[1,32,64,128]{3,1,2,0:T(8,128)(2,1)}, bf16[1,32,64,128]{3,1,2,0:T(8,128)(2,1)}, u32[]{:S(2)}, u32[]{:S(2)}) %collective-permute-start.6) | collective-permute-done | bytes 524320 | tf_op jit(solution)/shard_map/ppermute | solution.py:105
  149.1 1.3 fusion.16
  150.4 16.4 %convolution_convert_fusion = bf16[64,4096]{1,0:T(8,128)(2,1)S(1)} fusion(bf16[4096,4096]{1,0:T(8,128)(2,1)} %param.14, f32[8,8,32,128]{3,2,1,0:T(8,128)S(1)} %bitcast.253, f32[64,4096]{1,0:T(8,128)S(1)} %get-tuple-element.39, s32[4096]{0:T(1024)S(1)} %iota_add_fusion, f32[64]{0:T(128)S(1)} %get-tuple-element.7, f32[64]{0:T(128)S(1)} %get-tuple-element.5, ...), kind=kOutput, calls=%fused_computation.1 | convolution fusion | flops 2150367232 | bytes 36193280 | tf_op jit(solution)/shard_map/dot_general | solution.py:133
  166.8 0.2 reshape.406
  167.0 21.6 %all_to_all.10 = bf16[16,4,4096]{2,1,0:T(4,128)(2,1)S(1)} all-to-all(bf16[16,4,4096]{2,1,0:T(4,128)(2,1)S(1)} %reshape.406), channel_id=1, replica_groups=mesh['groups'=2,'dp'=8,'vocab'=2] {'dp','vocab'}, dimensions={0} | all-to-all | bytes 1048576 | tf_op jit(solution)/shard_map/all_to_all | solution.py:138
  188.6 0.8 reduce_sum.32
  (13 shorter events, 0.2 us)
Async XLA Ops:
  1.7 68.0 %all-to-all-start = ((bf16[8,8,4096]{2,1,0:T(8,128)(2,1)}), bf16[8,8,4096]{2,1,0:T(8,128)(2,1)}, u32[]{:S(2)}, u32[]{:S(2)}) async-start(bf16[8,8,4096]{2,1,0:T(8,128)(2,1)} %broadcast_in_dim.2), calls=%async_computation | async-start | bytes 1048576 | tf_op jit(solution)/shard_map/all_to_all | solution.py:51
  31.4 23.4 %copy-start.3 = (bf16[64,5248]{1,0:T(8,128)(2,1)}, bf16[64,5248]{1,0:T(8,128)(2,1)S(1)}, u32[]{:S(2)}) copy-start(bf16[64,5248]{1,0:T(8,128)(2,1)S(1)} %all_gather.3) | copy-start | bytes 2015236
  55.2 4.0 %copy-start.5 = (s32[48,4]{0,1:T(4,128)S(1)}, s32[48,4]{0,1:T(4,128)}, u32[]{:S(2)}) copy-start(s32[48,4]{0,1:T(4,128)} %param.11) | copy-start | bytes 2308
  55.2 4.0 %copy-start.6 = (s32[48,4]{0,1:T(4,128)S(1)}, s32[48,4]{0,1:T(4,128)}, u32[]{:S(2)}) copy-start(s32[48,4]{0,1:T(4,128)} %param.10) | copy-start | bytes 2308
  65.7 3.2 %copy-start = (f32[4,2,32,64,128]{4,2,3,1,0:T(8,128)}, f32[4,2,32,64,128]{4,2,3,1,0:T(8,128)S(1)}, u32[]{:S(2)}) copy-start(f32[4,2,32,64,128]{4,2,3,1,0:T(8,128)S(1)} %fusion.2) | copy-start | bytes 25165828
  69.4 24.7 %collective-permute-start.4 = (bf16[4,32,64,128]{3,1,2,0:T(8,128)(2,1)S(1)}, bf16[4,32,64,128]{3,1,2,0:T(8,128)(2,1)}, u32[]{:S(2)}, u32[]{:S(2)}) collective-permute-start(bf16[4,32,64,128]{3,1,2,0:T(8,128)(2,1)S(1)} %fusion.4), channel_id=1, source_target_pairs={{0,2},{2,0},{4,6},{6,4},{8,10},{10,8},{12,14},{14,12},{1,3},{3,1},... | collective-permute-start | bytes 6291464 | tf_op jit(solution)/shard_map/ppermute | solution.py:105
  69.6 24.5 %copy-start.1 = (f32[4,2,32,64,128]{4,2,3,1,0:T(8,128)S(1)}, f32[4,2,32,64,128]{4,2,3,1,0:T(8,128)}, u32[]{:S(2)}) copy-start(f32[4,2,32,64,128]{4,2,3,1,0:T(8,128)} %copy-done) | copy-start | bytes 25165828
  84.2 1.2 collective-permute-start
  85.4 2.7 %collective-permute-start.1 = (f32[4,64]{1,0:T(4,128)S(1)}, f32[4,64]{1,0:T(4,128)S(1)}, u32[]{:S(2)}, u32[]{:S(2)}) collective-permute-start(f32[4,64]{1,0:T(4,128)S(1)} %pad_maximum_fusion.2), channel_id=1, source_target_pairs={{0,4},{2,6},{4,0},{6,2},{8,12},{10,14},{12,8},{14,10},{1,5},{3,7},... | collective-permute-start | bytes 3080 | tf_op jit(solution)/shard_map/ppermute | solution.py:106
  88.1 3.4 %collective-permute-start.2 = (f32[4,64]{1,0:T(4,128)S(1)}, f32[4,64]{1,0:T(4,128)S(1)}, u32[]{:S(2)}, u32[]{:S(2)}) collective-permute-start(f32[4,64]{1,0:T(4,128)S(1)} %pad_maximum_fusion.3), channel_id=1, source_target_pairs={{0,8},{2,10},{4,12},{6,14},{8,0},{10,2},{12,4},{14,6},{1,9},{3,11}... | collective-permute-start | bytes 3080 | tf_op jit(solution)/shard_map/ppermute | solution.py:106
  91.6 2.5 %collective-permute-start.3 = (f32[4,64]{1,0:T(4,128)S(1)}, f32[4,64]{1,0:T(4,128)S(1)}, u32[]{:S(2)}, u32[]{:S(2)}) collective-permute-start(f32[4,64]{1,0:T(4,128)S(1)} %pad_maximum_fusion.4), channel_id=1, source_target_pairs={{0,1},{1,0},{2,3},{3,2},{4,5},{5,4},{6,7},{7,6},{8,9},{9,8},{10,11... | collective-permute-start | bytes 3080 | tf_op jit(solution)/shard_map/ppermute | solution.py:117
  94.1 5.9 %slice-start = ((bf16[64,5248]{1,0:T(8,128)(2,1)}), bf16[64,128]{1,0:T(8,128)(2,1)S(1)}, s32[]{:S(2)}) async-start(bf16[64,5248]{1,0:T(8,128)(2,1)} %copy-done.3), calls=%async_computation.2 | async-start | bytes 32768 | tf_op jit(solution)/shard_map/slice | solution.py:57
  96.3 2.0 %copy-start.2 = (f32[4,32,64,128]{3,1,2,0:T(8,128)}, f32[4,32,64,128]{3,1,2,0:T(8,128)S(1)}, u32[]{:S(2)}) copy-start(f32[4,32,64,128]{3,1,2,0:T(8,128)S(1)} %fusion.1) | copy-start | bytes 12582916
  98.5 21.2 %collective-permute-start.5 = (bf16[2,32,64,128]{3,1,2,0:T(8,128)(2,1)S(1)}, bf16[2,32,64,128]{3,1,2,0:T(8,128)(2,1)S(1)}, u32[]{:S(2)}, u32[]{:S(2)}) collective-permute-start(bf16[2,32,64,128]{3,1,2,0:T(8,128)(2,1)S(1)} %fusion.8), channel_id=1, source_target_pairs={{0,4},{2,6},{4,0},{6,2},{8,12},{10,14},{12,8},{14,10},{1,5},{3,7},... | collective-permute-start | bytes 3145736 | tf_op jit(solution)/shard_map/ppermute | solution.py:105
  119.7 1.0 copy-start.4
  123.8 25.3 %collective-permute-start.6 = (bf16[1,32,64,128]{3,1,2,0:T(8,128)(2,1)}, bf16[1,32,64,128]{3,1,2,0:T(8,128)(2,1)}, u32[]{:S(2)}, u32[]{:S(2)}) collective-permute-start(bf16[1,32,64,128]{3,1,2,0:T(8,128)(2,1)} %fusion.23), channel_id=1, source_target_pairs={{0,8},{2,10},{4,12},{6,14},{8,0},{10,2},{12,4},{14,6},{1,9},{3,11}... | collective-permute-start | bytes 1572872 | tf_op jit(solution)/shard_map/ppermute | solution.py:105

commit v5 on v4

--- a/solution.py
+++ b/solution.py
@@ -83,9 +83,6 @@
     student_local_peak = jnp.max(student_logits, axis=1)
     student_local_total = jnp.sum(jnp.exp(student_logits - student_local_peak[:, None]), axis=1)
 
-    peak, mass = teacher_local_peak, mapped_mass
-    s_peak, s_total = student_local_peak, student_local_total
-
     def merge(stats, other):
         new_peak = jnp.maximum(stats[0], other[0])
         new_s_peak = jnp.maximum(stats[2], other[2])
@@ -97,20 +94,53 @@
         )
         return merged, own, far
 
-    stats = jnp.stack([peak, mass, s_peak, s_total])
-    stage = 1
-    while stage < dp_count:
-        pairs = [(j, j ^ stage) for j in range(dp_count)]
-        halves = held.reshape(held.shape[0] // 2, 2, student_blocks, tokens_all, block_size)
-        arrived = lax.ppermute(halves[:, 1].astype(jnp.bfloat16), "dp", pairs)
-        other = lax.ppermute(stats, "dp", pairs)
-        stats, own, far = merge(stats, other)
-        held = (
-            halves[:, 0] * own[None, None, :, None]
-            + arrived.astype(jnp.float32) * far[None, None, :, None]
-        )
-        stage *= 2
-    column_peak = stats[0]
+    def to_every_peer(stats):
+        spread = jnp.broadcast_to(stats[None], (dp_count,) + stats.shape)
+        return lax.all_to_all(spread, "dp", split_axis=0, concat_axis=0, tiled=True)
+
+    teacher_seen = to_every_peer(jnp.stack([teacher_local_peak, mapped_mass]))
+    column_peak = jnp.max(teacher_seen[:, 0], axis=0)
+    column_scale = jnp.exp(teacher_seen[:, 0] - column_peak[None, :])
+    column_mass = jnp.sum(column_scale * teacher_seen[:, 1], axis=0)
+    student_seen = to_every_peer(jnp.stack([student_local_peak, student_local_total]))
+    column_s_peak = jnp.max(student_seen[:, 0], axis=0)
+    column_s_total = jnp.sum(
+        jnp.exp(student_seen[:, 0] - column_s_peak[None, :]) * student_seen[:, 1], axis=0
+    )
+
+    halves = held.reshape(dp_count // 2, 2, student_blocks, tokens_all, block_size)
+    arrived = lax.ppermute(
+        halves[:, 1].astype(jnp.bfloat16), "dp", [(j, j ^ 1) for j in range(dp_count)]
+    )
+    own = jnp.exp(teacher_local_peak - column_peak)
+    far = jnp.take(column_scale, jnp.bitwise_xor(my_dp, 1), axis=0)
+    held = (
+        halves[:, 0] * own[None, None, :, None]
+        + arrived.astype(jnp.float32) * far[None, None, :, None]
+    )
+
+    def reduce_bits(part, bits, low_first):
+        for bit in bits:
+            pairs = [(j, j ^ (1 << bit)) for j in range(dp_count)]
+            count = part.shape[0] // 2
+            if low_first:
+                split = part.reshape((count, 2) + part.shape[1:])
+                keep, send = split[:, 0], split[:, 1]
+            else:
+                split = part.reshape((2, count) + part.shape[1:])
+                keep, send = split[0], split[1]
+            part = keep + lax.ppermute(send.astype(jnp.bfloat16), "dp", pairs).astype(
+                jnp.float32
+            )
+        return part
+
+    bits = list(range(1, dp_count.bit_length() - 1))
+    half = tokens_all // 2
+    first = reduce_bits(held[:, :, :half], bits, True)
+    second = reduce_bits(held[:, :, half:], bits[::-1], False)
+    held = jnp.concatenate([first, second], axis=2)
+
+    stats = jnp.stack([column_peak, column_mass, column_s_peak, column_s_total])
     stage = 1
     while stage < vocab_count:
         pairs = [(j, j ^ stage) for j in range(vocab_count)]

time: 190 us -> 192 us (1.011)
  blocking collectives: 43.3 us -> 36.4 us
  other arithmetic: 9.09 us -> 13.1 us
  waiting for transfers between devices: 46.8 us -> 50.1 us
    ppermute x6 -> x5, waiting for transfers between devices: 45.5 us -> 36.5 us  [the longest x4 36.5 us: reduce_bits(): lax.ppermute(send.astype(jnp.bfloat16), 'dp', pairs).astype(jnp.float32)]
    all_to_all x0 -> x2, starting transfers between devices: none -> 9 us  [to_every_peer(): return lax.all_to_all(spread, 'dp', split_axis=0, concat_axis=0, tiled=True)]
    ppermute x6 -> x5, starting transfers between devices: 8.22 us -> 0.96 us  [the longest x4 0.58 us: reduce_bits(): lax.ppermute(send.astype(jnp.bfloat16), 'dp', pairs).astype(jnp.float32)]
    all_to_all x1, waiting for transfers between devices: 0.01 us -> 6.69 us  [on_device(): lax.all_to_all(jnp.broadcast_to(student_hidden[None], (dp_count,) + stude...]
    all_to_all x0 -> x2, waiting for transfers between devices: none -> 5.66 us  [to_every_peer(): return lax.all_to_all(spread, 'dp', split_axis=0, concat_axis=0, tiled=True)]
    all_gather x1, blocking collectives: 21.7 us -> 16.8 us  [on_device(): gathered = lax.all_gather(packed, 'dp', axis=0, tiled=True)]
    add x4 -> x3, other arithmetic: 0.07 us -> 3.75 us  [reduce_bits(): keep + lax.ppermute(send.astype(jnp.bfloat16), 'dp', pairs).astype(jnp.fl...]
    all_to_all x1, blocking collectives: 21.6 us -> 19.6 us  [on_device(): lax.all_to_all(partial, ('dp', 'vocab'), split_axis=0, concat_axis=0, til...]
  transfers between devices with their start and end apart: 8 -> 9, of which waited for: 6 -> 7; matrix products, arithmetic and copies ran while one was open for 27% -> 16% of each run, Pallas kernels for 0% -> 0%
where the time goes in v5:
time: 192 us; the launch traced here: 191 us
  matrix products  60.1 us (31%)
  waiting for transfers between devices  50.1 us (26%)
  blocking collectives  36.4 us (19%)
  starting transfers between devices  16 us (8%)
  local copies, waits for them, and re-layouts  15.6 us (8%)
  other arithmetic  13.1 us (7%)
    ppermute x4, waiting for transfers between devices, reduce_bits(): lax.ppermute(send.astype(jnp.bfloat16), 'dp', pairs).astype(jnp.float32)  36.5 us
    dot_general x1, matrix products, on_device(): jnp.dot(teacher_all, teacher_head, preferred_element_type=jnp.float32)  23.4 us
    all_to_all x1, blocking collectives, on_device(): lax.all_to_all(partial, ('dp', 'vocab'), split_axis=0, concat_axis=0, til...  19.6 us
    all_gather x1, blocking collectives, on_device(): gathered = lax.all_gather(packed, 'dp', axis=0, tiled=True)  16.8 us
    dot_general x1, matrix products, on_device(): lax.dot_general(logit_grad, student_head, (((1,), (1,)), ((), ())), prefe...  16.4 us
    dot_general x1, matrix products, on_device(): jnp.dot(student_all, student_head, preferred_element_type=jnp.float32)  13.8 us
    unnamed x23, local copies, waits for them, and re-layouts  10.4 us
    all_to_all x2, starting transfers between devices, to_every_peer(): return lax.all_to_all(spread, 'dp', split_axis=0, concat_axis=0, tiled=True)  9 us
  transfers between devices with their start and end apart: 9, of which 7 were waited for; matrix products, arithmetic and copies ran while one was open for 16% of the time, Pallas kernels for 0%

profile of v5, /device:TPU:1, one launch (start us, length us, event | category | flops | bytes accessed | tf_op | source)
XLA Modules:
  0.0 191.5 jit_solution(14529789385362188451)
XLA Ops:
  0.0 0.7 convert_convert_fusion
  0.7 0.1 fusion.39
  0.7 0.9 pad_maximum_fusion
  1.6 16.8 %all_gather.3 = bf16[64,5248]{1,0:T(8,128)(2,1)S(1)} all-gather(bf16[8,5248]{1,0:T(8,128)(2,1)S(1)} %pad_maximum_fusion), channel_id=1, replica_groups=mesh['groups'=2,'dp'=8,'vocab'=2] {'dp'}, dimensions={0}, use_global_device_ids=true | all-gather | bytes 755712 | tf_op jit(solution)/shard_map/all_gather | solution.py:50
  18.5 23.4 %fusion.54 = (f32[64]{0:T(128)S(1)}, f32[64,6144]{1,0:T(8,128)S(1)}) fusion(bf16[5120,6144]{1,0:T(8,128)(2,1)} %param.9, bf16[64,5248]{1,0:T(8,128)(2,1)S(1)} %all_gather.3), kind=kOutput, calls=%fused_computation.97 | convolution fusion | flops 4026925056 | bytes 65143040 | tf_op jit(solution)/shard_map/dot_general | solution.py:62
  41.9 0.3 fusion.13
  42.2 0.1 copy.60
  42.3 0.0 copy-start.6
  42.3 0.0 copy-start.7
  42.3 4.0 %convert_reduce_fusion = (f32[64]{0:T(128)S(1)}, bf16[48,64,4,128]{3,1,2,0:T(8,128)(2,1)S(1)}) fusion(bf16[48,4,128,128]{3,2,1,0:T(8,128)(2,1)} %param.12, bf16[64,48,128,1]{2,1,0,3:T(8,128)(2,1)S(1)} %bitcast.132), kind=kOutput, calls=%fused_computation | convolution fusion | flops 407371712 | bytes 10223872 | tf_op jit(solution)/shard_map/gkc,krcd->krgd/dot_general | solution.py:66
  46.3 0.7 reshape.219
  47.0 4.8 %all-to-all-start.2 = ((f32[8,1,128]{2,1,0:T(1,128)}), f32[8,1,128]{2,1,0:T(1,128)S(1)}, u32[]{:S(2)}, u32[]{:S(2)}) async-start(f32[8,1,128]{2,1,0:T(1,128)} %reshape.219), calls=%async_computation.2 | async-start | bytes 8192 | tf_op jit(solution)/shard_map/all_to_all | solution.py:99
  51.8 0.1 copy.40
  51.9 0.1 add.79
  52.0 2.8 %copy.83 = bf16[24,8,64,128]{3,1,2,0:T(8,128)(2,1)S(1)} copy(bf16[24,8,64,128]{3,2,1,0:T(8,128)(2,1)S(1)} %bitcast.127) | data formatting | bytes 6291456
  54.9 0.0 copy-start.5
  54.9 0.9 copy.62
  55.8 0.8 all-to-all-done.2
  56.6 0.8 broadcast_in_dim.15
  57.4 4.7 %all-to-all-start = ((bf16[8,8,4096]{2,1,0:T(8,128)(2,1)}), bf16[8,8,4096]{2,1,0:T(8,128)(2,1)}, u32[]{:S(2)}, u32[]{:S(2)}) async-start(bf16[8,8,4096]{2,1,0:T(8,128)(2,1)} %broadcast_in_dim.15), calls=%async_computation | async-start | bytes 1048576 | tf_op jit(solution)/shard_map/all_to_all | solution.py:51
  62.2 2.5 %fusion.2 = f32[4,2,32,64,128]{4,2,3,1,0:T(8,128)S(1)} fusion(bf16[64,128,192,1,1]{1,0,2,4,3:T(8,128)(2,1)S(1)} %bitcast.128, s32[192]{0:T(256)S(1)} %add.79, s32[4,2,32]{2,1,0:T(2,128)S(1)} %multiply_add_fusion), kind=kOutput, calls=%fused_computation.7 | convolution fusion | flops 805355520 | bytes 11536128 | tf_op jit(solution)/shard_map/dot_general | solution.py:76
  64.7 3.2 %copy-done = f32[4,2,32,64,128]{4,2,3,1,0:T(8,128)} copy-done((f32[4,2,32,64,128]{4,2,3,1,0:T(8,128)}, f32[4,2,32,64,128]{4,2,3,1,0:T(8,128)S(1)}, u32[]{:S(2)}) %copy-start) | copy-done | bytes 8388632
  67.9 0.5 fusion.4
  68.4 0.4 collective-permute-start.1
  68.8 0.5 broadcast.123
  69.3 0.6 reduce.3
  69.9 0.1 reshape.220
  70.0 6.7 %all-to-all-done = bf16[8,8,4096]{2,1,0:T(8,128)(2,1)} async-done(((bf16[8,8,4096]{2,1,0:T(8,128)(2,1)}), bf16[8,8,4096]{2,1,0:T(8,128)(2,1)}, u32[]{:S(2)}, u32[]{:S(2)}) %all-to-all-start) | async-done | bytes 524320 | tf_op jit(solution)/shard_map/all_to_all | solution.py:51
  76.7 13.8 %fusion.55 = (f32[64]{0:T(128)S(1)}, f32[64,4096]{1,0:T(8,128)S(1)}) fusion(bf16[4096,4096]{1,0:T(8,128)(2,1)} %param.14, bf16[8,8,4096]{2,1,0:T(8,128)(2,1)} %all-to-all-done), kind=kOutput, calls=%fused_computation.98 | convolution fusion | flops 2147745792 | bytes 35127552 | tf_op jit(solution)/shard_map/dot_general | solution.py:82
  90.5 0.3 exponential_reduce_fusion
  90.9 0.7 reshape.221
  91.6 4.2 %all-to-all-start.1 = ((f32[8,1,128]{2,1,0:T(1,128)}), f32[8,1,128]{2,1,0:T(1,128)S(1)}, u32[]{:S(2)}, u32[]{:S(2)}) async-start(f32[8,1,128]{2,1,0:T(1,128)} %reshape.221), calls=%async_computation.1 | async-start | bytes 8192 | tf_op jit(solution)/shard_map/all_to_all | solution.py:99
  95.8 4.8 %all-to-all-done.1 = f32[8,1,128]{2,1,0:T(1,128)S(1)} async-done(((f32[8,1,128]{2,1,0:T(1,128)}), f32[8,1,128]{2,1,0:T(1,128)S(1)}, u32[]{:S(2)}, u32[]{:S(2)}) %all-to-all-start.1) | async-done | bytes 4128 | tf_op jit(solution)/shard_map/all_to_all | solution.py:99
  100.6 0.6 reduce.4
  101.2 0.1 reshape.222
  101.3 1.3 collective-permute-start
  102.6 1.2 collective-permute-done
  103.8 0.0 collective-permute-done.1
  103.8 3.5 %fusion.1 = f32[4,32,64,128]{3,1,2,0:T(8,128)S(1)} fusion(f32[4,2,32,64,128]{4,2,3,1,0:T(8,128)} %copy-done, bf16[4,32,64,128]{3,1,2,0:T(8,128)(2,1)} %collective-permute-done.1, f32[64]{0:T(128)S(1)} %fusion.43, f32[64]{0:T(128)S(1)} %get-tuple-element.28), kind=kLoop, calls=%fused_computation.5 | loop fusion | flops 4194304 | bytes 10486272 | tf_op jit(solution)/shard_map/add | solution.py:118
  107.3 0.0 slice-start
  107.4 1.0 slice.168
  108.4 0.3 collective-permute-start.4
  108.6 0.8 copy-done.1
  109.4 0.2 slice.122
  109.6 0.9 fusion.18
  110.5 0.3 collective-permute-start.2
  110.8 0.1 convert_add_fusion
  110.9 23.8 %collective-permute-done.4 = bf16[2,32,32,128]{3,1,2,0:T(8,128)(2,1)} collective-permute-done((bf16[2,32,32,128]{3,1,2,0:T(8,128)(2,1)}, bf16[2,32,32,128]{3,1,2,0:T(8,128)(2,1)}, u32[]{:S(2)}, u32[]{:S(2)}) %collective-permute-start.4) | collective-permute-done | bytes 524320 | tf_op jit(solution)/shard_map/ppermute | solution.py:132
  134.7 1.5 slice_add_fusion
  136.2 0.8 slice.169
  137.0 0.0 collective-permute-done.2
  137.0 1.2 fusion.10
  138.3 1.0 copy-done.4
  139.3 0.0 collective-permute-start.3
  139.3 0.1 eq.56
  139.4 6.8 %collective-permute-done.5 = bf16[1,32,32,128]{3,1,2,0:T(8,128)(2,1)S(1)} collective-permute-done((bf16[1,32,32,128]{3,1,2,0:T(8,128)(2,1)}, bf16[1,32,32,128]{3,1,2,0:T(8,128)(2,1)S(1)}, u32[]{:S(2)}, u32[]{:S(2)}) %collective-permute-start.5) | collective-permute-done | bytes 262176 | tf_op jit(solution)/shard_map/ppermute | solution.py:132
  146.2 1.1 slice_add_fusion.1
  147.3 5.9 %collective-permute-done.3 = bf16[1,32,32,128]{3,1,2,0:T(8,128)(2,1)S(1)} collective-permute-done((bf16[1,32,32,128]{3,1,2,0:T(8,128)(2,1)S(1)}, bf16[1,32,32,128]{3,1,2,0:T(8,128)(2,1)S(1)}, u32[]{:S(2)}, u32[]{:S(2)}) %collective-permute-start.3) | collective-permute-done | bytes 262176 | tf_op jit(solution)/shard_map/ppermute | solution.py:132
  153.2 1.1 fusion.19
  154.3 0.1 fusion.11
  154.5 16.4 %convolution_convert_fusion = bf16[64,4096]{1,0:T(8,128)(2,1)S(1)} fusion(bf16[4096,4096]{1,0:T(8,128)(2,1)} %param.14, f32[8,8,32,128]{3,2,1,0:T(8,128)S(1)} %bitcast.131, f32[64,4096]{1,0:T(8,128)S(1)} %get-tuple-element.36, s32[4096]{0:T(1024)S(1)} %iota_add_fusion, f32[64]{0:T(128)S(1)} %get-tuple-element.27, f32[64]{0:T(128)S(1)} %get-tuple-element.23, ...), kind=kOutput, calls=%fused_computation.1 | convolution fusion | flops 2150367232 | bytes 36193280 | tf_op jit(solution)/shard_map/dot_general | solution.py:163
  170.9 0.2 reshape.185
  171.1 19.6 %all_to_all.20 = bf16[16,4,4096]{2,1,0:T(4,128)(2,1)S(1)} all-to-all(bf16[16,4,4096]{2,1,0:T(4,128)(2,1)S(1)} %reshape.185), channel_id=1, replica_groups=mesh['groups'=2,'dp'=8,'vocab'=2] {'dp','vocab'}, dimensions={0} | all-to-all | bytes 1048576 | tf_op jit(solution)/shard_map/all_to_all | solution.py:168
  190.6 0.8 reduce_sum.52
  (30 shorter events, 0.3 us)
Async XLA Ops:
  18.5 23.4 %copy-start.2 = (bf16[64,5248]{1,0:T(8,128)(2,1)}, bf16[64,5248]{1,0:T(8,128)(2,1)S(1)}, u32[]{:S(2)}) copy-start(bf16[64,5248]{1,0:T(8,128)(2,1)S(1)} %all_gather.3) | copy-start | bytes 2015236
  42.3 9.5 %copy-start.6 = (s32[48,4]{0,1:T(4,128)S(1)}, s32[48,4]{0,1:T(4,128)}, u32[]{:S(2)}) copy-start(s32[48,4]{0,1:T(4,128)} %param.11) | copy-start | bytes 2308
  42.3 9.5 %copy-start.7 = (s32[48,4]{0,1:T(4,128)S(1)}, s32[48,4]{0,1:T(4,128)}, u32[]{:S(2)}) copy-start(s32[48,4]{0,1:T(4,128)} %param.10) | copy-start | bytes 2308
  47.0 9.6 %all-to-all-start.2 = ((f32[8,1,128]{2,1,0:T(1,128)}), f32[8,1,128]{2,1,0:T(1,128)S(1)}, u32[]{:S(2)}, u32[]{:S(2)}) async-start(f32[8,1,128]{2,1,0:T(1,128)} %reshape.219), calls=%async_computation.2 | async-start | bytes 8192 | tf_op jit(solution)/shard_map/all_to_all | solution.py:99
  54.9 1.7 copy-start.5
  57.4 19.2 %all-to-all-start = ((bf16[8,8,4096]{2,1,0:T(8,128)(2,1)}), bf16[8,8,4096]{2,1,0:T(8,128)(2,1)}, u32[]{:S(2)}, u32[]{:S(2)}) async-start(bf16[8,8,4096]{2,1,0:T(8,128)(2,1)} %broadcast_in_dim.15), calls=%async_computation | async-start | bytes 1048576 | tf_op jit(solution)/shard_map/all_to_all | solution.py:51
  64.7 3.2 %copy-start = (f32[4,2,32,64,128]{4,2,3,1,0:T(8,128)}, f32[4,2,32,64,128]{4,2,3,1,0:T(8,128)S(1)}, u32[]{:S(2)}) copy-start(f32[4,2,32,64,128]{4,2,3,1,0:T(8,128)S(1)} %fusion.2) | copy-start | bytes 25165828
  68.4 35.4 %collective-permute-start.1 = (bf16[4,32,64,128]{3,1,2,0:T(8,128)(2,1)S(1)}, bf16[4,32,64,128]{3,1,2,0:T(8,128)(2,1)}, u32[]{:S(2)}, u32[]{:S(2)}) collective-permute-start(bf16[4,32,64,128]{3,1,2,0:T(8,128)(2,1)S(1)} %fusion.4), channel_id=1, source_target_pairs={{0,2},{2,0},{4,6},{6,4},{8,10},{10,8},{12,14},{14,12},{1,3},{3,1},... | collective-permute-start | bytes 6291464 | tf_op jit(solution)/shard_map/ppermute | solution.py:112
  91.6 9.0 %all-to-all-start.1 = ((f32[8,1,128]{2,1,0:T(1,128)}), f32[8,1,128]{2,1,0:T(1,128)S(1)}, u32[]{:S(2)}, u32[]{:S(2)}) async-start(f32[8,1,128]{2,1,0:T(1,128)} %reshape.221), calls=%async_computation.1 | async-start | bytes 8192 | tf_op jit(solution)/shard_map/all_to_all | solution.py:99
  101.3 2.5 %collective-permute-start = (f32[4,64]{1,0:T(4,128)S(1)}, f32[4,64]{1,0:T(4,128)S(1)}, u32[]{:S(2)}, u32[]{:S(2)}) collective-permute-start(f32[4,64]{1,0:T(4,128)S(1)} %pad_maximum_fusion.1), channel_id=1, source_target_pairs={{0,1},{1,0},{2,3},{3,2},{4,5},{5,4},{6,7},{7,6},{8,9},{9,8},{10,11... | collective-permute-start | bytes 3080 | tf_op jit(solution)/shard_map/ppermute | solution.py:147
  107.3 2.1 %copy-start.1 = (f32[4,32,64,128]{3,1,2,0:T(8,128)}, f32[4,32,64,128]{3,1,2,0:T(8,128)S(1)}, u32[]{:S(2)}) copy-start(f32[4,32,64,128]{3,1,2,0:T(8,128)S(1)} %fusion.1) | copy-start | bytes 12582916
  107.3 3.4 %slice-start = ((bf16[64,5248]{1,0:T(8,128)(2,1)}), bf16[64,128]{1,0:T(8,128)(2,1)S(1)}, s32[]{:S(2)}) async-start(bf16[64,5248]{1,0:T(8,128)(2,1)} %copy-done.2), calls=%async_computation.4 | async-start | bytes 32768 | tf_op jit(solution)/shard_map/slice | solution.py:57
  108.4 26.3 %collective-permute-start.4 = (bf16[2,32,32,128]{3,1,2,0:T(8,128)(2,1)}, bf16[2,32,32,128]{3,1,2,0:T(8,128)(2,1)}, u32[]{:S(2)}, u32[]{:S(2)}) collective-permute-start(bf16[2,32,32,128]{3,1,2,0:T(8,128)(2,1)} %slice.168), channel_id=1, source_target_pairs={{0,8},{2,10},{4,12},{6,14},{8,0},{10,2},{12,4},{14,6},{1,9},{3,11}... | collective-permute-start | bytes 1572872 | tf_op jit(solution)/shard_map/ppermute | solution.py:132
  110.5 26.6 %collective-permute-start.2 = (bf16[2,32,32,128]{3,1,2,0:T(8,128)(2,1)}, bf16[2,32,32,128]{3,1,2,0:T(8,128)(2,1)}, u32[]{:S(2)}, u32[]{:S(2)}) collective-permute-start(bf16[2,32,32,128]{3,1,2,0:T(8,128)(2,1)} %fusion.18), channel_id=1, source_target_pairs={{0,4},{2,6},{4,0},{6,2},{8,12},{10,14},{12,8},{14,10},{1,5},{3,7},... | collective-permute-start | bytes 1572872 | tf_op jit(solution)/shard_map/ppermute | solution.py:132
  136.2 2.1 %copy-start.3 = (f32[2,32,32,128]{3,1,2,0:T(8,128)}, f32[2,32,32,128]{3,1,2,0:T(8,128)S(1)}, u32[]{:S(2)}) copy-start(f32[2,32,32,128]{3,1,2,0:T(8,128)S(1)} %slice_add_fusion) | copy-start | bytes 3145732
  137.0 9.2 %collective-permute-start.5 = (bf16[1,32,32,128]{3,1,2,0:T(8,128)(2,1)}, bf16[1,32,32,128]{3,1,2,0:T(8,128)(2,1)S(1)}, u32[]{:S(2)}, u32[]{:S(2)}) collective-permute-start(bf16[1,32,32,128]{3,1,2,0:T(8,128)(2,1)} %slice.169), channel_id=1, source_target_pairs={{0,4},{2,6},{4,0},{6,2},{8,12},{10,14},{12,8},{14,10},{1,5},{3,7},... | collective-permute-start | bytes 786440 | tf_op jit(solution)/shard_map/ppermute | solution.py:132
  138.3 1.0 copy-start.4
  139.3 13.9 %collective-permute-start.3 = (bf16[1,32,32,128]{3,1,2,0:T(8,128)(2,1)S(1)}, bf16[1,32,32,128]{3,1,2,0:T(8,128)(2,1)S(1)}, u32[]{:S(2)}, u32[]{:S(2)}) collective-permute-start(bf16[1,32,32,128]{3,1,2,0:T(8,128)(2,1)S(1)} %fusion.31), channel_id=1, source_target_pairs={{0,8},{2,10},{4,12},{6,14},{8,0},{10,2},{12,4},{14,6},{1,9},{3,11}... | collective-permute-start | bytes 786440 | tf_op jit(solution)/shard_map/ppermute | solution.py:132

commit v6 on v4

--- a/solution.py
+++ b/solution.py
@@ -97,19 +97,59 @@
         )
         return merged, own, far
 
+    def code_stats(stats, rows):
+        high = lax.reduce_precision(stats, exponent_bits=8, mantissa_bits=7)
+        rest = stats - high
+        middle = lax.reduce_precision(rest, exponent_bits=8, mantissa_bits=7)
+        low = rest - middle
+        flat = jnp.concatenate([high, middle, low]).astype(jnp.bfloat16).reshape(-1)
+        flat = jnp.pad(flat, (0, rows * block_size - flat.shape[0]))
+        return flat.reshape(1, rows, block_size)
+
+    def decode_stats(coded_block):
+        flat = coded_block.reshape(-1)[: 12 * tokens_all].astype(jnp.float32)
+        pieces = flat.reshape(3, 4, tokens_all)
+        return pieces[0] + pieces[1] + pieces[2]
+
+    def exchange(send, stats, pairs):
+        rows = send.shape[-2]
+        flat = send.reshape((-1, rows, block_size)).astype(jnp.bfloat16)
+        payload = jnp.concatenate([flat, code_stats(stats, rows)], axis=0)
+        arrived = lax.ppermute(payload, "dp", pairs)
+        blocks = arrived[:-1].reshape(send.shape).astype(jnp.float32)
+        return blocks, decode_stats(arrived[-1])
+
+    def combine(keep, stats, blocks, other, token_slice):
+        merged, own, far = merge(stats, other)
+        own, far = own[token_slice], far[token_slice]
+        return keep * own[None, None, :, None] + blocks * far[None, None, :, None], merged
+
     stats = jnp.stack([peak, mass, s_peak, s_total])
-    stage = 1
-    while stage < dp_count:
-        pairs = [(j, j ^ stage) for j in range(dp_count)]
-        halves = held.reshape(held.shape[0] // 2, 2, student_blocks, tokens_all, block_size)
-        arrived = lax.ppermute(halves[:, 1].astype(jnp.bfloat16), "dp", pairs)
-        other = lax.ppermute(stats, "dp", pairs)
-        stats, own, far = merge(stats, other)
-        held = (
-            halves[:, 0] * own[None, None, :, None]
-            + arrived.astype(jnp.float32) * far[None, None, :, None]
-        )
-        stage *= 2
+    every = slice(None)
+    halves = held.reshape(dp_count // 2, 2, student_blocks, tokens_all, block_size)
+    blocks, other = exchange(halves[:, 1], stats, [(j, j ^ 1) for j in range(dp_count)])
+    held, stats = combine(halves[:, 0], stats, blocks, other, every)
+
+    def reduce_bits(part, stats, bits, low_first, token_slice):
+        for bit in bits:
+            pairs = [(j, j ^ (1 << bit)) for j in range(dp_count)]
+            count = part.shape[0] // 2
+            if low_first:
+                split = part.reshape((count, 2) + part.shape[1:])
+                keep, send = split[:, 0], split[:, 1]
+            else:
+                split = part.reshape((2, count) + part.shape[1:])
+                keep, send = split[0], split[1]
+            blocks, other = exchange(send, stats, pairs)
+            part, stats = combine(keep, stats, blocks, other, token_slice)
+        return part, stats
+
+    bits = list(range(1, dp_count.bit_length() - 1))
+    half = tokens_all // 2
+    first, stats_first = reduce_bits(held[:, :, :half], stats, bits, True, slice(0, half))
+    second, _ = reduce_bits(held[:, :, half:], stats, bits[::-1], False, slice(half, None))
+    held = jnp.concatenate([first, second], axis=2)
+    stats = stats_first
     column_peak = stats[0]
     stage = 1
     while stage < vocab_count:

time: 190 us -> 202 us (1.063)
  other arithmetic: 9.09 us -> 23.6 us
  waiting for transfers between devices: 46.8 us -> 36.7 us
  local copies, waits for them, and re-layouts: 13.7 us -> 19.9 us
    add x1 -> x9, other arithmetic: 2.21 us -> 12.2 us  [the longest x5 12.1 us: combine(): keep * own[None, None, :, None] + blocks * far[None, None, :, None]]
    ppermute x6 -> x5, waiting for transfers between devices: 45.5 us -> 36.6 us  [exchange(): arrived = lax.ppermute(payload, 'dp', pairs)]
    slice x0 -> x14, local copies, waits for them, and re-layouts: none -> 8.6 us  [the longest x3 2.32 us: exchange(): blocks = arrived[:-1].reshape(send.shape).astype(jnp.float32)]
    convert_element_type x0 -> x8, other arithmetic: none -> 4.46 us  [the longest x5 2.77 us: decode_stats(): flat = coded_block.reshape(-1)[:12 * tokens_all].astype(jnp.float32)]
    reshape x1 -> x0, other arithmetic: 2.26 us -> none  [on_device(): held.reshape(held.shape[0] // 2, 2, student_blocks, tokens_all, block_size)]
    concatenate x0 -> x8, other arithmetic: none -> 2.14 us  [the longest x4 2.09 us: exchange(): payload = jnp.concatenate([flat, code_stats(stats, rows)], axis=0)]
    unnamed x17 -> x21, local copies, waits for them, and re-layouts: 9.97 us -> 8.26 us
    ppermute x6 -> x5, starting transfers between devices: 8.22 us -> 8.3 us  [exchange(): arrived = lax.ppermute(payload, 'dp', pairs)]
  transfers between devices with their start and end apart: 8 -> 7, of which waited for: 6 -> 5; matrix products, arithmetic and copies ran while one was open for 27% -> 22% of each run, Pallas kernels for 0% -> 0%
where the time goes in v6:
time: 202 us; the launch traced here: 201 us
  matrix products  60.4 us (30%)
  blocking collectives  44 us (22%)
  waiting for transfers between devices  36.7 us (18%)
  other arithmetic  23.6 us (12%)
  local copies, waits for them, and re-layouts  19.9 us (10%)
  starting transfers between devices  16 us (8%)
    ppermute x5, waiting for transfers between devices, exchange(): arrived = lax.ppermute(payload, 'dp', pairs)  36.6 us
    dot_general x1, matrix products, on_device(): jnp.dot(teacher_all, teacher_head, preferred_element_type=jnp.float32)  23.3 us
    all_to_all x1, blocking collectives, on_device(): lax.all_to_all(partial, ('dp', 'vocab'), split_axis=0, concat_axis=0, til...  23.2 us
    all_gather x1, blocking collectives, on_device(): gathered = lax.all_gather(packed, 'dp', axis=0, tiled=True)  20.8 us
    dot_general x1, matrix products, on_device(): lax.dot_general(logit_grad, student_head, (((1,), (1,)), ((), ())), prefe...  16.6 us
    dot_general x1, matrix products, on_device(): jnp.dot(student_all, student_head, preferred_element_type=jnp.float32)  14 us
    add x5, other arithmetic, combine(): keep * own[None, None, :, None] + blocks * far[None, None, :, None]  12.1 us
    ppermute x5, starting transfers between devices, exchange(): arrived = lax.ppermute(payload, 'dp', pairs)  8.3 us
  transfers between devices with their start and end apart: 7, of which 5 were waited for; matrix products, arithmetic and copies ran while one was open for 22% of the time, Pallas kernels for 0%

profile of v6, /device:TPU:1, one launch (start us, length us, event | category | flops | bytes accessed | tf_op | source)
XLA Modules:
  0.0 201.0 jit_solution(5555222502438581129)
XLA Ops:
  0.0 1.7 broadcast_in_dim.2
  1.7 6.4 %all-to-all-start = ((bf16[8,8,4096]{2,1,0:T(8,128)(2,1)}), bf16[8,8,4096]{2,1,0:T(8,128)(2,1)}, u32[]{:S(2)}, u32[]{:S(2)}) async-start(bf16[8,8,4096]{2,1,0:T(8,128)(2,1)} %broadcast_in_dim.2), calls=%async_computation | async-start | bytes 1048576 | tf_op jit(solution)/shard_map/all_to_all | solution.py:51
  8.0 0.7 convert_convert_fusion
  8.7 0.7 multiply_add_fusion.1
  9.4 0.1 copy.10
  9.5 0.1 add.220
  9.7 0.9 pad_maximum_fusion.5
  10.6 20.8 %all_gather.3 = bf16[64,5248]{1,0:T(8,128)(2,1)S(1)} all-gather(bf16[8,5248]{1,0:T(8,128)(2,1)S(1)} %pad_maximum_fusion.5), channel_id=1, replica_groups=mesh['groups'=2,'dp'=8,'vocab'=2] {'dp'}, dimensions={0}, use_global_device_ids=true | all-gather | bytes 755712 | tf_op jit(solution)/shard_map/all_gather | solution.py:50
  31.4 23.3 %fusion.84 = (f32[64]{0:T(128)S(1)}, f32[64,6144]{1,0:T(8,128)S(1)}) fusion(bf16[5120,6144]{1,0:T(8,128)(2,1)} %param.9, bf16[64,5248]{1,0:T(8,128)(2,1)S(1)} %all_gather.3), kind=kOutput, calls=%fused_computation.209 | convolution fusion | flops 4026925056 | bytes 65143040 | tf_op jit(solution)/shard_map/dot_general | solution.py:62
  54.7 0.3 fusion.13
  55.0 0.1 copy.31
  55.1 4.0 %convert_reduce_fusion = (f32[64]{0:T(128)S(1)}, bf16[48,64,4,128]{3,1,2,0:T(8,128)(2,1)S(1)}) fusion(bf16[48,4,128,128]{3,2,1,0:T(8,128)(2,1)} %param.12, bf16[64,48,128,1]{2,1,0,3:T(8,128)(2,1)S(1)} %bitcast.285), kind=kOutput, calls=%fused_computation | convolution fusion | flops 407371712 | bytes 10223872 | tf_op jit(solution)/shard_map/gkc,krcd->krgd/dot_general | solution.py:66
  59.1 2.9 %copy.55 = bf16[24,8,64,128]{3,1,2,0:T(8,128)(2,1)S(1)} copy(bf16[24,8,64,128]{3,2,1,0:T(8,128)(2,1)S(1)} %bitcast.280) | data formatting | bytes 6291456
  61.9 0.9 copy.33
  62.8 2.5 %fusion.2 = f32[4,2,32,64,128]{4,2,3,1,0:T(8,128)S(1)} fusion(bf16[64,128,192,1,1]{1,0,2,4,3:T(8,128)(2,1)S(1)} %bitcast.281, s32[192]{0:T(256)S(1)} %add.220, s32[4,2,32]{2,1,0:T(2,128)S(1)} %multiply_add_fusion), kind=kOutput, calls=%fused_computation.8 | convolution fusion | flops 805355520 | bytes 11536128 | tf_op jit(solution)/shard_map/dot_general | solution.py:76
  65.4 3.2 %copy-done = f32[4,2,32,64,128]{4,2,3,1,0:T(8,128)} copy-done((f32[4,2,32,64,128]{4,2,3,1,0:T(8,128)}, f32[4,2,32,64,128]{4,2,3,1,0:T(8,128)S(1)}, u32[]{:S(2)}) %copy-start) | copy-done | bytes 8388632
  68.6 0.5 slice.540
  69.1 0.8 copy.13
  69.9 14.0 %fusion.85 = (f32[64]{0:T(128)S(1)}, f32[64,4096]{1,0:T(8,128)S(1)}) fusion(bf16[4096,4096]{1,0:T(8,128)(2,1)} %param.14, bf16[8,8,4096]{2,1,0:T(8,128)(2,1)} %all-to-all-done), kind=kOutput, calls=%fused_computation.210 | convolution fusion | flops 2147745792 | bytes 35127552 | tf_op jit(solution)/shard_map/dot_general | solution.py:82
  84.0 0.3 exponential_reduce_fusion
  84.4 0.2 pad_maximum_fusion
  84.6 0.2 collective-permute-start
  84.8 4.0 %collective-permute-done = bf16[129,64,128]{2,1,0:T(8,128)(2,1)S(1)} collective-permute-done((bf16[129,64,128]{2,1,0:T(8,128)(2,1)S(1)}, bf16[129,64,128]{2,1,0:T(8,128)(2,1)S(1)}, u32[]{:S(2)}, u32[]{:S(2)}) %collective-permute-start) | collective-permute-done | bytes 2113568 | tf_op jit(solution)/shard_map/ppermute | solution.py:118
  88.9 0.1 add.224
  89.0 0.2 slice.363
  89.2 0.5 convert.72
  89.6 5.7 %fusion.1 = f32[4,32,64,128]{3,1,2,0:T(8,128)S(1)} fusion(f32[4,2,32,64,128]{4,2,3,1,0:T(8,128)} %copy-done, f32[4,32,64,128]{3,2,1,0:T(8,128)S(1)} %convert.72, f32[64]{0:T(128)S(1)} %fusion.78, f32[64]{0:T(128)S(1)} %get-tuple-element.17), kind=kLoop, calls=%fused_computation.4 | loop fusion | flops 3145728 | bytes 12583424 | tf_op jit(solution)/shard_map/add | solution.py:125
  95.4 1.0 slice.541
  96.4 1.2 copy-done.1
  97.5 0.2 slice.364
  97.9 1.2 copy.19
  99.1 1.2 copy.15
  100.4 1.1 pad_maximum_fusion.2
  101.5 1.6 collective-permute-start.1
  103.1 2.2 %collective-permute-start.4 = (bf16[65,32,128]{2,1,0:T(8,128)(2,1)}, bf16[65,32,128]{2,1,0:T(8,128)(2,1)}, u32[]{:S(2)}, u32[]{:S(2)}) collective-permute-start(bf16[65,32,128]{2,1,0:T(8,128)(2,1)} %get-tuple-element.20), channel_id=1, source_target_pairs={{0,8},{2,10},{4,12},{6,14},{8,0},{10,2},{12,4},{14,6},{1,9},{3,11}... | collective-permute-start | bytes 1597448 | tf_op jit(solution)/shard_map/ppermute | solution.py:118
  105.4 21.1 %collective-permute-done.1 = bf16[65,32,128]{2,1,0:T(8,128)(2,1)} collective-permute-done((bf16[65,32,128]{2,1,0:T(8,128)(2,1)}, bf16[65,32,128]{2,1,0:T(8,128)(2,1)}, u32[]{:S(2)}, u32[]{:S(2)}) %collective-permute-start.1) | collective-permute-done | bytes 532512 | tf_op jit(solution)/shard_map/ppermute | solution.py:118
  126.4 0.7 slice_convert_fusion.8
  127.1 0.1 add.230
  127.2 0.7 slice_convert_fusion.7
  128.0 1.1 slice.368
  129.1 1.1 convert.73
  130.3 0.6 slice.340
  130.9 0.6 slice.338
  131.7 2.0 %fusion.10 = f32[1,2,32,32,128]{4,2,3,1,0:T(8,128)S(1)} fusion(f32[2,2,32,32,128]{4,2,3,1,0:T(8,128)S(1)} %bitcast.279, f32[1,2,32,32,128]{4,3,2,1,0:T(8,128)} %convert.73, f32[32]{0:T(128)S(1)} %bitcast.296, f32[32]{0:T(128)S(1)} %bitcast.295), kind=kLoop, calls=%fused_computation.23 | loop fusion | flops 786432 | bytes 3145984 | tf_op jit(solution)/shard_map/add | solution.py:125
  133.8 2.1 %collective-permute-start.2 = (bf16[33,32,128]{2,0,1:T(8,128)(2,1)S(1)}, bf16[33,32,128]{2,0,1:T(8,128)(2,1)}, u32[]{:S(2)}, u32[]{:S(2)}) collective-permute-start(bf16[33,32,128]{2,0,1:T(8,128)(2,1)S(1)} %pad_maximum_fusion.3), channel_id=1, source_target_pairs={{0,8},{2,10},{4,12},{6,14},{8,0},{10,2},{12,4},{14,6},{1,9},{3,11}... | collective-permute-start | bytes 811016 | tf_op jit(solution)/shard_map/ppermute | solution.py:118
  135.9 1.1 slice.379
  137.0 0.1 convert.74
  137.2 2.2 %fusion.8 = f32[2,32,32,128]{3,1,2,0:T(8,128)S(1)} fusion(f32[4,32,64,128]{3,1,2,0:T(8,128)} %copy-done.1, f32[2,32,32,128]{3,2,1,0:T(8,128)S(1)} %convert.74, f32[32]{0:T(128)S(1)} %copy-done.7, f32[32]{0:T(128)S(1)} %copy-done.8), kind=kLoop, calls=%fused_computation.20 | loop fusion | flops 786432 | bytes 3145984 | tf_op jit(solution)/shard_map/add | solution.py:125
  139.4 0.8 pad_maximum_fusion.4
  140.2 2.2 %collective-permute-start.5 = (bf16[33,32,128]{2,0,1:T(8,128)(2,1)}, bf16[33,32,128]{2,0,1:T(8,128)(2,1)}, u32[]{:S(2)}, u32[]{:S(2)}) collective-permute-start(bf16[33,32,128]{2,0,1:T(8,128)(2,1)} %pad_maximum_fusion.4), channel_id=1, source_target_pairs={{0,4},{2,6},{4,0},{6,2},{8,12},{10,14},{12,8},{14,10},{1,5},{3,7},... | collective-permute-start | bytes 811016 | tf_op jit(solution)/shard_map/ppermute | solution.py:118
  142.5 7.3 %collective-permute-done.2 = bf16[33,32,128]{2,0,1:T(8,128)(2,1)} collective-permute-done((bf16[33,32,128]{2,0,1:T(8,128)(2,1)S(1)}, bf16[33,32,128]{2,0,1:T(8,128)(2,1)}, u32[]{:S(2)}, u32[]{:S(2)}) %collective-permute-start.2) | collective-permute-done | bytes 270368 | tf_op jit(solution)/shard_map/ppermute | solution.py:118
  149.8 0.7 slice_convert_fusion.6
  150.5 4.2 %collective-permute-done.5 = bf16[33,32,128]{2,0,1:T(8,128)(2,1)} collective-permute-done((bf16[33,32,128]{2,0,1:T(8,128)(2,1)}, bf16[33,32,128]{2,0,1:T(8,128)(2,1)}, u32[]{:S(2)}, u32[]{:S(2)}) %collective-permute-start.5) | collective-permute-done | bytes 270368 | tf_op jit(solution)/shard_map/ppermute | solution.py:118
  154.7 0.7 slice_convert_fusion.5
  155.7 1.3 collective-permute-start.3
  157.0 1.1 fusion.20
  158.1 0.1 collective-permute-done.3
  158.2 0.7 fusion.60
  158.9 1.1 fusion.23
  160.0 0.1 fusion.11
  160.2 16.6 %convolution_convert_fusion = bf16[64,4096]{1,0:T(8,128)(2,1)S(1)} fusion(bf16[4096,4096]{1,0:T(8,128)(2,1)} %param.14, f32[8,8,32,128]{3,2,1,0:T(8,128)S(1)} %bitcast.284, f32[64,4096]{1,0:T(8,128)S(1)} %get-tuple-element.68, s32[4096]{0:T(1024)S(1)} %iota_add_fusion, f32[64]{0:T(128)S(1)} %get-tuple-element.21, f32[64]{0:T(128)S(1)} %get-tuple-element.5, ...), kind=kOutput, calls=%fused_computation.1 | convolution fusion | flops 2150367232 | bytes 36193280 | tf_op jit(solution)/shard_map/dot_general | solution.py:173
  176.8 0.2 reshape.530
  177.0 23.2 %all_to_all.10 = bf16[16,4,4096]{2,1,0:T(4,128)(2,1)S(1)} all-to-all(bf16[16,4,4096]{2,1,0:T(4,128)(2,1)S(1)} %reshape.530), channel_id=1, replica_groups=mesh['groups'=2,'dp'=8,'vocab'=2] {'dp','vocab'}, dimensions={0} | all-to-all | bytes 1048576 | tf_op jit(solution)/shard_map/all_to_all | solution.py:178
  200.2 0.8 reduce_sum.32
  (68 shorter events, 1.5 us)
Async XLA Ops:
  1.7 68.2 %all-to-all-start = ((bf16[8,8,4096]{2,1,0:T(8,128)(2,1)}), bf16[8,8,4096]{2,1,0:T(8,128)(2,1)}, u32[]{:S(2)}, u32[]{:S(2)}) async-start(bf16[8,8,4096]{2,1,0:T(8,128)(2,1)} %broadcast_in_dim.2), calls=%async_computation | async-start | bytes 1048576 | tf_op jit(solution)/shard_map/all_to_all | solution.py:51
  31.4 23.3 %copy-start.2 = (bf16[64,5248]{1,0:T(8,128)(2,1)}, bf16[64,5248]{1,0:T(8,128)(2,1)S(1)}, u32[]{:S(2)}) copy-start(bf16[64,5248]{1,0:T(8,128)(2,1)S(1)} %all_gather.3) | copy-start | bytes 2015236
  65.4 3.2 %copy-start = (f32[4,2,32,64,128]{4,2,3,1,0:T(8,128)}, f32[4,2,32,64,128]{4,2,3,1,0:T(8,128)S(1)}, u32[]{:S(2)}) copy-start(f32[4,2,32,64,128]{4,2,3,1,0:T(8,128)S(1)} %fusion.2) | copy-start | bytes 25165828
  84.6 4.2 %collective-permute-start = (bf16[129,64,128]{2,1,0:T(8,128)(2,1)S(1)}, bf16[129,64,128]{2,1,0:T(8,128)(2,1)S(1)}, u32[]{:S(2)}, u32[]{:S(2)}) collective-permute-start(bf16[129,64,128]{2,1,0:T(8,128)(2,1)S(1)} %pad_maximum_fusion), channel_id=1, source_target_pairs={{0,2},{2,0},{4,6},{6,4},{8,10},{10,8},{12,14},{14,12},{1,3},{3,1},... | collective-permute-start | bytes 6340616 | tf_op jit(solution)/shard_map/ppermute | solution.py:118
  95.4 2.1 %copy-start.1 = (f32[4,32,64,128]{3,1,2,0:T(8,128)}, f32[4,32,64,128]{3,1,2,0:T(8,128)S(1)}, u32[]{:S(2)}) copy-start(f32[4,32,64,128]{3,1,2,0:T(8,128)S(1)} %fusion.1) | copy-start | bytes 12582916
  97.7 5.4 %slice-start = ((bf16[64,5248]{1,0:T(8,128)(2,1)}), bf16[64,128]{1,0:T(8,128)(2,1)S(1)}, s32[]{:S(2)}) async-start(bf16[64,5248]{1,0:T(8,128)(2,1)} %copy-done.2), calls=%async_computation.2 | async-start | bytes 32768 | tf_op jit(solution)/shard_map/slice | solution.py:57
  101.5 25.0 %collective-permute-start.1 = (bf16[65,32,128]{2,1,0:T(8,128)(2,1)}, bf16[65,32,128]{2,1,0:T(8,128)(2,1)}, u32[]{:S(2)}, u32[]{:S(2)}) collective-permute-start(bf16[65,32,128]{2,1,0:T(8,128)(2,1)} %get-tuple-element.19), channel_id=1, source_target_pairs={{0,4},{2,6},{4,0},{6,2},{8,12},{10,14},{12,8},{14,10},{1,5},{3,7},... | collective-permute-start | bytes 1597448 | tf_op jit(solution)/shard_map/ppermute | solution.py:118
  103.1 24.1 %collective-permute-start.4 = (bf16[65,32,128]{2,1,0:T(8,128)(2,1)}, bf16[65,32,128]{2,1,0:T(8,128)(2,1)}, u32[]{:S(2)}, u32[]{:S(2)}) collective-permute-start(bf16[65,32,128]{2,1,0:T(8,128)(2,1)} %get-tuple-element.20), channel_id=1, source_target_pairs={{0,8},{2,10},{4,12},{6,14},{8,0},{10,2},{12,4},{14,6},{1,9},{3,11}... | collective-permute-start | bytes 1597448 | tf_op jit(solution)/shard_map/ppermute | solution.py:118
  128.0 3.5 %copy-start.6 = (f32[64]{0:T(128)}, f32[64]{0:T(128)S(1)}, u32[]{:S(2)}) copy-start(f32[64]{0:T(128)S(1)} %get-tuple-element.12) | copy-start | bytes 772
  130.9 8.4 %copy-start.5 = (f32[64]{0:T(128)}, f32[64]{0:T(128)S(1)}, u32[]{:S(2)}) copy-start(f32[64]{0:T(128)S(1)} %fusion.76) | copy-start | bytes 772
  131.5 5.6 %copy-start.7 = (f32[32]{0:T(128)S(1)}, f32[32]{0:T(128)}, u32[]{:S(2)}) copy-start(f32[32]{0:T(128)} %slice.340) | copy-start | bytes 388
  131.5 5.6 %copy-start.8 = (f32[32]{0:T(128)S(1)}, f32[32]{0:T(128)}, u32[]{:S(2)}) copy-start(f32[32]{0:T(128)} %slice.338) | copy-start | bytes 388
  133.7 3.3 %copy-start.3 = (f32[1,2,32,32,128]{4,2,3,1,0:T(8,128)}, f32[1,2,32,32,128]{4,2,3,1,0:T(8,128)S(1)}, u32[]{:S(2)}) copy-start(f32[1,2,32,32,128]{4,2,3,1,0:T(8,128)S(1)} %fusion.10) | copy-start | bytes 3145732
  133.8 16.0 %collective-permute-start.2 = (bf16[33,32,128]{2,0,1:T(8,128)(2,1)S(1)}, bf16[33,32,128]{2,0,1:T(8,128)(2,1)}, u32[]{:S(2)}, u32[]{:S(2)}) collective-permute-start(bf16[33,32,128]{2,0,1:T(8,128)(2,1)S(1)} %pad_maximum_fusion.3), channel_id=1, source_target_pairs={{0,8},{2,10},{4,12},{6,14},{8,0},{10,2},{12,4},{14,6},{1,9},{3,11}... | collective-permute-start | bytes 811016 | tf_op jit(solution)/shard_map/ppermute | solution.py:118
  137.0 21.9 %copy-start.4 = (f32[1,2,32,32,128]{4,2,3,1,0:T(8,128)S(1)}, f32[1,2,32,32,128]{4,2,3,1,0:T(8,128)}, u32[]{:S(2)}) copy-start(f32[1,2,32,32,128]{4,2,3,1,0:T(8,128)} %copy-done.3) | copy-start | bytes 3145732
  140.2 14.5 %collective-permute-start.5 = (bf16[33,32,128]{2,0,1:T(8,128)(2,1)}, bf16[33,32,128]{2,0,1:T(8,128)(2,1)}, u32[]{:S(2)}, u32[]{:S(2)}) collective-permute-start(bf16[33,32,128]{2,0,1:T(8,128)(2,1)} %pad_maximum_fusion.4), channel_id=1, source_target_pairs={{0,4},{2,6},{4,0},{6,2},{8,12},{10,14},{12,8},{14,10},{1,5},{3,7},... | collective-permute-start | bytes 811016 | tf_op jit(solution)/shard_map/ppermute | solution.py:118
  155.7 2.5 %collective-permute-start.3 = (f32[4,64]{1,0:T(4,128)S(1)}, f32[4,64]{1,0:T(4,128)S(1)}, u32[]{:S(2)}, u32[]{:S(2)}) collective-permute-start(f32[4,64]{1,0:T(4,128)S(1)} %pad_maximum_fusion.13), channel_id=1, source_target_pairs={{0,1},{1,0},{2,3},{3,2},{4,5},{5,4},{6,7},{7,6},{8,9},{9,8},{10,11... | collective-permute-start | bytes 3080 | tf_op jit(solution)/shard_map/ppermute | solution.py:157

commit v7 on v4

--- a/solution.py
+++ b/solution.py
@@ -88,36 +88,32 @@
 
     def merge(stats, other):
         new_peak = jnp.maximum(stats[0], other[0])
-        new_s_peak = jnp.maximum(stats[2], other[2])
         own, far = jnp.exp(stats[0] - new_peak), jnp.exp(other[0] - new_peak)
-        s_own, s_far = jnp.exp(stats[2] - new_s_peak), jnp.exp(other[2] - new_s_peak)
-        merged = jnp.stack(
-            [new_peak, stats[1] * own + other[1] * far, new_s_peak,
-             stats[3] * s_own + other[3] * s_far]
-        )
-        return merged, own, far
+        return jnp.stack([new_peak, stats[1] * own + other[1] * far]), own, far
 
-    stats = jnp.stack([peak, mass, s_peak, s_total])
+    teacher_stats = jnp.stack([peak, mass])
+    student_stats = jnp.stack([s_peak, s_total])
     stage = 1
     while stage < dp_count:
         pairs = [(j, j ^ stage) for j in range(dp_count)]
         halves = held.reshape(held.shape[0] // 2, 2, student_blocks, tokens_all, block_size)
         arrived = lax.ppermute(halves[:, 1].astype(jnp.bfloat16), "dp", pairs)
-        other = lax.ppermute(stats, "dp", pairs)
-        stats, own, far = merge(stats, other)
+        teacher_stats, own, far = merge(teacher_stats, lax.ppermute(teacher_stats, "dp", pairs))
+        student_stats = merge(student_stats, lax.ppermute(student_stats, "dp", pairs))[0]
         held = (
             halves[:, 0] * own[None, None, :, None]
             + arrived.astype(jnp.float32) * far[None, None, :, None]
         )
         stage *= 2
-    column_peak = stats[0]
+    column_peak = teacher_stats[0]
     stage = 1
     while stage < vocab_count:
         pairs = [(j, j ^ stage) for j in range(vocab_count)]
-        stats = merge(stats, lax.ppermute(stats, "vocab", pairs))[0]
+        teacher_stats = merge(teacher_stats, lax.ppermute(teacher_stats, "vocab", pairs))[0]
+        student_stats = merge(student_stats, lax.ppermute(student_stats, "vocab", pairs))[0]
         stage *= 2
-    teacher_peak, target_total = stats[0], stats[1]
-    student_peak, student_total = stats[2], stats[3]
+    teacher_peak, target_total = teacher_stats[0], teacher_stats[1]
+    student_peak, student_total = student_stats[0], student_stats[1]
     mapped = jnp.transpose(
         held[0] * jnp.exp(column_peak - teacher_peak)[None, :, None], (1, 0, 2)
     ).reshape(tokens_all, student_cols)

time: 190 us -> 185 us (0.974)
  blocking collectives: 43.3 us -> 36.2 us
  starting transfers between devices: 15.9 us -> 20 us
  local copies, waits for them, and re-layouts: 13.7 us -> 9.84 us
  waiting for transfers between devices: 46.8 us -> 50.4 us
    ppermute x4 -> x8, waiting for transfers between devices: 4.27 us -> 28.8 us  [the longest x3 23.9 us: on_device(): lax.ppermute(student_stats, 'dp', pairs)]
    ppermute x3, waiting for transfers between devices: 42.5 us -> 21.6 us  [on_device(): arrived = lax.ppermute(halves[:, 1].astype(jnp.bfloat16), 'dp', pairs)]
    ppermute x4 -> x8, starting transfers between devices: 5.53 us -> 11.7 us  [the longest x3 5.61 us: on_device(): lax.ppermute(teacher_stats, 'dp', pairs)]
    all_gather x1, blocking collectives: 21.7 us -> 16.8 us  [on_device(): gathered = lax.all_gather(packed, 'dp', axis=0, tiled=True)]
    unnamed x17, local copies, waits for them, and re-layouts: 9.97 us -> 7.7 us
    all_to_all x1, blocking collectives: 21.6 us -> 19.4 us  [on_device(): lax.all_to_all(partial, ('dp', 'vocab'), split_axis=0, concat_axis=0, til...]
  transfers between devices with their start and end apart: 8 -> 12, of which waited for: 6 -> 5; matrix products, arithmetic and copies ran while one was open for 27% -> 13% of each run, Pallas kernels for 0% -> 0%
where the time goes in v7:
time: 185 us
  matrix products  60.5 us (33%)
  waiting for transfers between devices  50.4 us (27%)
  blocking collectives  36.2 us (20%)
  starting transfers between devices  20 us (11%)
  local copies, waits for them, and re-layouts  9.84 us (5%)
  other arithmetic  7.79 us (4%)
    ppermute x3, waiting for transfers between devices, on_device(): lax.ppermute(student_stats, 'dp', pairs)  23.9 us
    dot_general x1, matrix products, on_device(): jnp.dot(teacher_all, teacher_head, preferred_element_type=jnp.float32)  23.4 us
    ppermute x3, waiting for transfers between devices, on_device(): arrived = lax.ppermute(halves[:, 1].astype(jnp.bfloat16), 'dp', pairs)  21.6 us
    all_to_all x1, blocking collectives, on_device(): lax.all_to_all(partial, ('dp', 'vocab'), split_axis=0, concat_axis=0, til...  19.4 us
    all_gather x1, blocking collectives, on_device(): gathered = lax.all_gather(packed, 'dp', axis=0, tiled=True)  16.8 us
    dot_general x1, matrix products, on_device(): lax.dot_general(logit_grad, student_head, (((1,), (1,)), ((), ())), prefe...  16.6 us
    dot_general x1, matrix products, on_device(): jnp.dot(student_all, student_head, preferred_element_type=jnp.float32)  14 us
    unnamed x17, local copies, waits for them, and re-layouts  7.7 us
  transfers between devices with their start and end apart: 12, of which 5 were waited for; matrix products, arithmetic and copies ran while one was open for 13% of the time, Pallas kernels for 0%

profile of v7, /device:TPU:1, one launch (start us, length us, event | category | flops | bytes accessed | tf_op | source)
XLA Modules:
  0.0 185.0 jit_solution(10286098093655619350)
XLA Ops:
  0.0 0.7 convert_convert_fusion
  0.7 0.1 fusion.42
  0.7 0.9 pad_maximum_fusion
  1.6 16.8 %all_gather.3 = bf16[64,5248]{1,0:T(8,128)(2,1)S(1)} all-gather(bf16[8,5248]{1,0:T(8,128)(2,1)S(1)} %pad_maximum_fusion), channel_id=1, replica_groups=mesh['groups'=2,'dp'=8,'vocab'=2] {'dp'}, dimensions={0}, use_global_device_ids=true | all-gather | bytes 755712 | tf_op jit(solution)/shard_map/all_gather | solution.py:50
  18.5 23.4 %fusion.75 = (f32[64]{0:T(128)S(1)}, f32[64,6144]{1,0:T(8,128)S(1)}) fusion(bf16[5120,6144]{1,0:T(8,128)(2,1)} %param.9, bf16[64,5248]{1,0:T(8,128)(2,1)S(1)} %all_gather.3), kind=kOutput, calls=%fused_computation.143 | convolution fusion | flops 4026925056 | bytes 65143040 | tf_op jit(solution)/shard_map/dot_general | solution.py:62
  41.9 0.0 copy-done.3
  41.9 0.3 fusion.18
  42.2 0.1 copy.29
  42.3 0.0 copy-start.4
  42.3 0.0 copy-start.5
  42.3 0.0 copy-start.6
  42.3 4.0 %convert_reduce_fusion = (f32[64]{0:T(128)S(1)}, bf16[48,64,4,128]{3,1,2,0:T(8,128)(2,1)S(1)}) fusion(bf16[48,4,128,128]{3,2,1,0:T(8,128)(2,1)} %param.12, bf16[64,48,128,1]{2,1,0,3:T(8,128)(2,1)S(1)} %bitcast.254), kind=kOutput, calls=%fused_computation | convolution fusion | flops 407371712 | bytes 10223872 | tf_op jit(solution)/shard_map/gkc,krcd->krgd/dot_general | solution.py:66
  46.3 0.2 collective-permute-start.4
  46.5 0.0 copy-done.4
  46.5 0.8 broadcast_in_dim.2
  47.4 5.0 %all-to-all-start = ((bf16[8,8,4096]{2,1,0:T(8,128)(2,1)}), bf16[8,8,4096]{2,1,0:T(8,128)(2,1)}, u32[]{:S(2)}, u32[]{:S(2)}) async-start(bf16[8,8,4096]{2,1,0:T(8,128)(2,1)} %broadcast_in_dim.2), calls=%async_computation | async-start | bytes 1048576 | tf_op jit(solution)/shard_map/all_to_all | solution.py:51
  52.4 0.0 copy-done.5
  52.4 0.0 copy-done.6
  52.4 0.0 collective-permute-done.4
  52.4 1.4 collective-permute-start.6
  53.9 2.8 %copy.54 = bf16[24,8,64,128]{3,1,2,0:T(8,128)(2,1)S(1)} copy(bf16[24,8,64,128]{3,2,1,0:T(8,128)(2,1)S(1)} %bitcast.251) | data formatting | bytes 6291456
  56.7 0.9 copy.31
  57.6 0.1 copy.13
  57.7 0.1 add.140
  57.8 3.6 %collective-permute-done.6 = f32[2,64]{1,0:T(2,128)S(1)} collective-permute-done((f32[2,64]{1,0:T(2,128)S(1)}, f32[2,64]{1,0:T(2,128)S(1)}, u32[]{:S(2)}, u32[]{:S(2)}) %collective-permute-start.6) | collective-permute-done | bytes 544 | tf_op jit(solution)/shard_map/ppermute | solution.py:101
  61.5 4.0 %collective-permute-start.8 = (f32[2,64]{1,0:T(2,128)S(1)}, f32[2,64]{1,0:T(2,128)S(1)}, u32[]{:S(2)}, u32[]{:S(2)}) collective-permute-start(f32[2,64]{1,0:T(2,128)S(1)} %pad_maximum_fusion.7), channel_id=1, source_target_pairs={{0,8},{2,10},{4,12},{6,14},{8,0},{10,2},{12,4},{14,6},{1,9},{3,11}... | collective-permute-start | bytes 1544 | tf_op jit(solution)/shard_map/ppermute | solution.py:101
  65.4 2.5 %fusion.2 = f32[4,2,32,64,128]{4,2,3,1,0:T(8,128)S(1)} fusion(bf16[64,128,192,1,1]{1,0,2,4,3:T(8,128)(2,1)S(1)} %bitcast.252, s32[192]{0:T(256)S(1)} %add.140, s32[4,2,32]{2,1,0:T(2,128)S(1)} %multiply_add_fusion), kind=kOutput, calls=%fused_computation.7 | convolution fusion | flops 805355520 | bytes 11536128 | tf_op jit(solution)/shard_map/dot_general | solution.py:76
  67.9 0.0 copy-start
  68.0 0.0 slice-start
  68.0 0.0 collective-permute-done.8
  68.0 1.3 collective-permute-start.10
  69.3 1.9 %copy-done = f32[4,2,32,64,128]{4,2,3,1,0:T(8,128)} copy-done((f32[4,2,32,64,128]{4,2,3,1,0:T(8,128)}, f32[4,2,32,64,128]{4,2,3,1,0:T(8,128)S(1)}, u32[]{:S(2)}) %copy-start) | copy-done | bytes 8388632
  71.2 0.5 fusion.4
  71.7 1.2 collective-permute-start.5
  72.9 0.0 slice-done
  72.9 0.0 collective-permute-done.10
  72.9 0.0 all-to-all-done
  73.0 14.0 %fusion.76 = (f32[64]{0:T(128)S(1)}, f32[64,4096]{1,0:T(8,128)S(1)}) fusion(bf16[4096,4096]{1,0:T(8,128)(2,1)} %param.14, bf16[8,8,4096]{2,1,0:T(8,128)(2,1)} %all-to-all-done), kind=kOutput, calls=%fused_computation.144 | convolution fusion | flops 2147745792 | bytes 35127552 | tf_op jit(solution)/shard_map/dot_general | solution.py:82
  87.0 0.3 exponential_reduce_fusion
  87.3 0.1 collective-permute-start
  87.4 0.0 collective-permute-done.5
  87.4 2.2 %fusion.1 = f32[4,32,64,128]{3,1,2,0:T(8,128)S(1)} fusion(f32[4,2,32,64,128]{4,2,3,1,0:T(8,128)S(1)} %copy-done.1, bf16[4,32,64,128]{3,1,2,0:T(8,128)(2,1)} %collective-permute-done.5, f32[64]{0:T(128)S(1)} %get-tuple-element.16, f32[64]{0:T(128)S(1)} %get-tuple-element.15), kind=kLoop, calls=%fused_computation.5 | loop fusion | flops 4194304 | bytes 10486272 | tf_op jit(solution)/shard_map/add | solution.py:104
  89.6 1.9 %copy-done.2 = f32[4,32,64,128]{3,1,2,0:T(8,128)} copy-done((f32[4,32,64,128]{3,1,2,0:T(8,128)}, f32[4,32,64,128]{3,1,2,0:T(8,128)S(1)}, u32[]{:S(2)}) %copy-start.2) | copy-done | bytes 4194328
  91.6 0.2 fusion.8
  91.8 0.1 collective-permute-start.7
  91.9 0.0 collective-permute-done
  91.9 1.5 collective-permute-start.1
  93.4 0.1 convert_add_fusion
  93.5 22.6 %collective-permute-done.1 = f32[2,64]{1,0:T(2,128)S(1)} collective-permute-done((f32[2,64]{1,0:T(2,128)S(1)}, f32[2,64]{1,0:T(2,128)S(1)}, u32[]{:S(2)}, u32[]{:S(2)}) %collective-permute-start.1) | collective-permute-done | bytes 544 | tf_op jit(solution)/shard_map/ppermute | solution.py:102
  116.2 2.0 %collective-permute-start.2 = (f32[2,64]{1,0:T(2,128)S(1)}, f32[2,64]{1,0:T(2,128)S(1)}, u32[]{:S(2)}, u32[]{:S(2)}) collective-permute-start(f32[2,64]{1,0:T(2,128)S(1)} %pad_maximum_fusion.3), channel_id=1, source_target_pairs={{0,8},{2,10},{4,12},{6,14},{8,0},{10,2},{12,4},{14,6},{1,9},{3,11}... | collective-permute-start | bytes 1544 | tf_op jit(solution)/shard_map/ppermute | solution.py:102
  118.2 0.1 eq.56
  118.2 1.3 collective-permute-done.2
  119.6 0.0 collective-permute-done.7
  119.6 1.9 %fusion.7 = f32[1,2,32,64,128]{4,2,3,1,0:T(8,128)S(1)} fusion(bf16[2,32,64,128]{3,1,2,0:T(8,128)(2,1)S(1)} %collective-permute-done.7, f32[64]{0:T(128)S(1)} %get-tuple-element.13, f32[64]{0:T(128)S(1)} %get-tuple-element.12, f32[2,2,32,64,128]{4,2,3,1,0:T(8,128)} %bitcast.250), kind=kLoop, calls=%fused_computation.15 | loop fusion | flops 2097152 | bytes 5243392 | tf_op jit(solution)/shard_map/reshape | solution.py:99
  121.5 0.1 fusion.23
  121.6 2.0 %collective-permute-start.9 = (bf16[1,32,64,128]{3,1,2,0:T(8,128)(2,1)S(1)}, bf16[1,32,64,128]{3,1,2,0:T(8,128)(2,1)S(1)}, u32[]{:S(2)}, u32[]{:S(2)}) collective-permute-start(bf16[1,32,64,128]{3,1,2,0:T(8,128)(2,1)S(1)} %fusion.23), channel_id=1, source_target_pairs={{0,8},{2,10},{4,12},{6,14},{8,0},{10,2},{12,4},{14,6},{1,9},{3,11}... | collective-permute-start | bytes 1572872 | tf_op jit(solution)/shard_map/ppermute | solution.py:100
  123.6 1.2 collective-permute-start.3
  124.8 1.2 collective-permute-done.3
  126.1 21.6 %collective-permute-done.9 = bf16[1,32,64,128]{3,1,2,0:T(8,128)(2,1)S(1)} collective-permute-done((bf16[1,32,64,128]{3,1,2,0:T(8,128)(2,1)S(1)}, bf16[1,32,64,128]{3,1,2,0:T(8,128)(2,1)S(1)}, u32[]{:S(2)}, u32[]{:S(2)}) %collective-permute-start.9) | collective-permute-done | bytes 524320 | tf_op jit(solution)/shard_map/ppermute | solution.py:100
  147.7 0.3 fusion.16
  147.9 16.6 %convolution_convert_fusion = bf16[64,4096]{1,0:T(8,128)(2,1)S(1)} fusion(bf16[4096,4096]{1,0:T(8,128)(2,1)} %param.14, f32[8,8,32,128]{3,2,1,0:T(8,128)S(1)} %bitcast.253, f32[64,4096]{1,0:T(8,128)S(1)} %get-tuple-element.35, s32[4096]{0:T(1024)S(1)} %iota_add_fusion, f32[64]{0:T(128)S(1)} %get-tuple-element.11, f32[64]{0:T(128)S(1)} %get-tuple-element.5, ...), kind=kOutput, calls=%fused_computation.1 | convolution fusion | flops 2150367232 | bytes 36193280 | tf_op jit(solution)/shard_map/dot_general | solution.py:129
  164.5 0.2 reshape.406
  164.7 19.4 %all_to_all.10 = bf16[16,4,4096]{2,1,0:T(4,128)(2,1)S(1)} all-to-all(bf16[16,4,4096]{2,1,0:T(4,128)(2,1)S(1)} %reshape.406), channel_id=1, replica_groups=mesh['groups'=2,'dp'=8,'vocab'=2] {'dp','vocab'}, dimensions={0} | all-to-all | bytes 1048576 | tf_op jit(solution)/shard_map/all_to_all | solution.py:134
  184.2 0.8 reduce_sum.32
  (25 shorter events, 0.2 us)
Async XLA Ops:
  18.5 23.4 %copy-start.3 = (bf16[64,5248]{1,0:T(8,128)(2,1)}, bf16[64,5248]{1,0:T(8,128)(2,1)S(1)}, u32[]{:S(2)}) copy-start(bf16[64,5248]{1,0:T(8,128)(2,1)S(1)} %all_gather.3) | copy-start | bytes 2015236
  42.3 4.3 %copy-start.4 = (bf16[8,4096]{1,0:T(8,128)(2,1)S(1)}, bf16[8,4096]{1,0:T(8,128)(2,1)}, u32[]{:S(2)}) copy-start(bf16[8,4096]{1,0:T(8,128)(2,1)} %param.13) | copy-start | bytes 196612
  42.3 10.1 %copy-start.5 = (s32[48,4]{0,1:T(4,128)S(1)}, s32[48,4]{0,1:T(4,128)}, u32[]{:S(2)}) copy-start(s32[48,4]{0,1:T(4,128)} %param.11) | copy-start | bytes 2308
  42.3 10.1 %copy-start.6 = (s32[48,4]{0,1:T(4,128)S(1)}, s32[48,4]{0,1:T(4,128)}, u32[]{:S(2)}) copy-start(s32[48,4]{0,1:T(4,128)} %param.10) | copy-start | bytes 2308
  46.3 6.1 %collective-permute-start.4 = (f32[2,64]{1,0:T(2,128)S(1)}, f32[2,64]{1,0:T(2,128)S(1)}, u32[]{:S(2)}, u32[]{:S(2)}) collective-permute-start(f32[2,64]{1,0:T(2,128)S(1)} %pad_maximum_fusion.5), channel_id=1, source_target_pairs={{0,2},{2,0},{4,6},{6,4},{8,10},{10,8},{12,14},{14,12},{1,3},{3,1},... | collective-permute-start | bytes 1544 | tf_op jit(solution)/shard_map/ppermute | solution.py:101
  47.4 25.6 %all-to-all-start = ((bf16[8,8,4096]{2,1,0:T(8,128)(2,1)}), bf16[8,8,4096]{2,1,0:T(8,128)(2,1)}, u32[]{:S(2)}, u32[]{:S(2)}) async-start(bf16[8,8,4096]{2,1,0:T(8,128)(2,1)} %broadcast_in_dim.2), calls=%async_computation | async-start | bytes 1048576 | tf_op jit(solution)/shard_map/all_to_all | solution.py:51
  52.4 9.0 %collective-permute-start.6 = (f32[2,64]{1,0:T(2,128)S(1)}, f32[2,64]{1,0:T(2,128)S(1)}, u32[]{:S(2)}, u32[]{:S(2)}) collective-permute-start(f32[2,64]{1,0:T(2,128)S(1)} %pad_maximum_fusion.6), channel_id=1, source_target_pairs={{0,4},{2,6},{4,0},{6,2},{8,12},{10,14},{12,8},{14,10},{1,5},{3,7},... | collective-permute-start | bytes 1544 | tf_op jit(solution)/shard_map/ppermute | solution.py:101
  61.5 6.5 %collective-permute-start.8 = (f32[2,64]{1,0:T(2,128)S(1)}, f32[2,64]{1,0:T(2,128)S(1)}, u32[]{:S(2)}, u32[]{:S(2)}) collective-permute-start(f32[2,64]{1,0:T(2,128)S(1)} %pad_maximum_fusion.7), channel_id=1, source_target_pairs={{0,8},{2,10},{4,12},{6,14},{8,0},{10,2},{12,4},{14,6},{1,9},{3,11}... | collective-permute-start | bytes 1544 | tf_op jit(solution)/shard_map/ppermute | solution.py:101
  67.9 3.2 %copy-start = (f32[4,2,32,64,128]{4,2,3,1,0:T(8,128)}, f32[4,2,32,64,128]{4,2,3,1,0:T(8,128)S(1)}, u32[]{:S(2)}) copy-start(f32[4,2,32,64,128]{4,2,3,1,0:T(8,128)S(1)} %fusion.2) | copy-start | bytes 25165828
  68.0 4.9 %slice-start = ((bf16[64,5248]{1,0:T(8,128)(2,1)}), bf16[64,128]{1,0:T(8,128)(2,1)S(1)}, s32[]{:S(2)}) async-start(bf16[64,5248]{1,0:T(8,128)(2,1)} %copy-done.3), calls=%async_computation.2 | async-start | bytes 32768 | tf_op jit(solution)/shard_map/slice | solution.py:57
  68.0 4.9 %collective-permute-start.10 = (f32[2,64]{1,0:T(2,128)S(1)}, f32[2,64]{1,0:T(2,128)S(1)}, u32[]{:S(2)}, u32[]{:S(2)}) collective-permute-start(f32[2,64]{1,0:T(2,128)S(1)} %pad_maximum_fusion.8), channel_id=1, source_target_pairs={{0,1},{1,0},{2,3},{3,2},{4,5},{5,4},{6,7},{7,6},{8,9},{9,8},{10,11... | collective-permute-start | bytes 1544 | tf_op jit(solution)/shard_map/ppermute | solution.py:112
  71.7 15.7 %collective-permute-start.5 = (bf16[4,32,64,128]{3,1,2,0:T(8,128)(2,1)S(1)}, bf16[4,32,64,128]{3,1,2,0:T(8,128)(2,1)}, u32[]{:S(2)}, u32[]{:S(2)}) collective-permute-start(bf16[4,32,64,128]{3,1,2,0:T(8,128)(2,1)S(1)} %fusion.4), channel_id=1, source_target_pairs={{0,2},{2,0},{4,6},{6,4},{8,10},{10,8},{12,14},{14,12},{1,3},{3,1},... | collective-permute-start | bytes 6291464 | tf_op jit(solution)/shard_map/ppermute | solution.py:100
  73.0 14.5 %copy-start.1 = (f32[4,2,32,64,128]{4,2,3,1,0:T(8,128)S(1)}, f32[4,2,32,64,128]{4,2,3,1,0:T(8,128)}, u32[]{:S(2)}) copy-start(f32[4,2,32,64,128]{4,2,3,1,0:T(8,128)} %copy-done) | copy-start | bytes 25165828
  87.3 4.6 %collective-permute-start = (f32[2,64]{1,0:T(2,128)S(1)}, f32[2,64]{1,0:T(2,128)S(1)}, u32[]{:S(2)}, u32[]{:S(2)}) collective-permute-start(f32[2,64]{1,0:T(2,128)S(1)} %pad_maximum_fusion.1), channel_id=1, source_target_pairs={{0,2},{2,0},{4,6},{6,4},{8,10},{10,8},{12,14},{14,12},{1,3},{3,1},... | collective-permute-start | bytes 1544 | tf_op jit(solution)/shard_map/ppermute | solution.py:102
  89.6 1.9 %copy-start.2 = (f32[4,32,64,128]{3,1,2,0:T(8,128)}, f32[4,32,64,128]{3,1,2,0:T(8,128)S(1)}, u32[]{:S(2)}) copy-start(f32[4,32,64,128]{3,1,2,0:T(8,128)S(1)} %fusion.1) | copy-start | bytes 12582916
  91.8 27.8 %collective-permute-start.7 = (bf16[2,32,64,128]{3,1,2,0:T(8,128)(2,1)S(1)}, bf16[2,32,64,128]{3,1,2,0:T(8,128)(2,1)S(1)}, u32[]{:S(2)}, u32[]{:S(2)}) collective-permute-start(bf16[2,32,64,128]{3,1,2,0:T(8,128)(2,1)S(1)} %fusion.8), channel_id=1, source_target_pairs={{0,4},{2,6},{4,0},{6,2},{8,12},{10,14},{12,8},{14,10},{1,5},{3,7},... | collective-permute-start | bytes 3145736 | tf_op jit(solution)/shard_map/ppermute | solution.py:100
  91.9 24.2 %collective-permute-start.1 = (f32[2,64]{1,0:T(2,128)S(1)}, f32[2,64]{1,0:T(2,128)S(1)}, u32[]{:S(2)}, u32[]{:S(2)}) collective-permute-start(f32[2,64]{1,0:T(2,128)S(1)} %pad_maximum_fusion.2), channel_id=1, source_target_pairs={{0,4},{2,6},{4,0},{6,2},{8,12},{10,14},{12,8},{14,10},{1,5},{3,7},... | collective-permute-start | bytes 1544 | tf_op jit(solution)/shard_map/ppermute | solution.py:102
  116.2 3.4 %collective-permute-start.2 = (f32[2,64]{1,0:T(2,128)S(1)}, f32[2,64]{1,0:T(2,128)S(1)}, u32[]{:S(2)}, u32[]{:S(2)}) collective-permute-start(f32[2,64]{1,0:T(2,128)S(1)} %pad_maximum_fusion.3), channel_id=1, source_target_pairs={{0,8},{2,10},{4,12},{6,14},{8,0},{10,2},{12,4},{14,6},{1,9},{3,11}... | collective-permute-start | bytes 1544 | tf_op jit(solution)/shard_map/ppermute | solution.py:102
  121.6 26.0 %collective-permute-start.9 = (bf16[1,32,64,128]{3,1,2,0:T(8,128)(2,1)S(1)}, bf16[1,32,64,128]{3,1,2,0:T(8,128)(2,1)S(1)}, u32[]{:S(2)}, u32[]{:S(2)}) collective-permute-start(bf16[1,32,64,128]{3,1,2,0:T(8,128)(2,1)S(1)} %fusion.23), channel_id=1, source_target_pairs={{0,8},{2,10},{4,12},{6,14},{8,0},{10,2},{12,4},{14,6},{1,9},{3,11}... | collective-permute-start | bytes 1572872 | tf_op jit(solution)/shard_map/ppermute | solution.py:100
  123.6 2.4 %collective-permute-start.3 = (f32[2,64]{1,0:T(2,128)S(1)}, f32[2,64]{1,0:T(2,128)S(1)}, u32[]{:S(2)}, u32[]{:S(2)}) collective-permute-start(f32[2,64]{1,0:T(2,128)S(1)} %pad_maximum_fusion.4), channel_id=1, source_target_pairs={{0,1},{1,0},{2,3},{3,2},{4,5},{5,4},{6,7},{7,6},{8,9},{9,8},{10,11... | collective-permute-start | bytes 1544 | tf_op jit(solution)/shard_map/ppermute | solution.py:113

commit v8 on v7

--- a/solution.py
+++ b/solution.py
@@ -96,16 +96,34 @@
     stage = 1
     while stage < dp_count:
         pairs = [(j, j ^ stage) for j in range(dp_count)]
-        halves = held.reshape(held.shape[0] // 2, 2, student_blocks, tokens_all, block_size)
-        arrived = lax.ppermute(halves[:, 1].astype(jnp.bfloat16), "dp", pairs)
-        teacher_stats, own, far = merge(teacher_stats, lax.ppermute(teacher_stats, "dp", pairs))
+        teacher_stats = merge(teacher_stats, lax.ppermute(teacher_stats, "dp", pairs))[0]
         student_stats = merge(student_stats, lax.ppermute(student_stats, "dp", pairs))[0]
-        held = (
-            halves[:, 0] * own[None, None, :, None]
-            + arrived.astype(jnp.float32) * far[None, None, :, None]
-        )
         stage *= 2
     column_peak = teacher_stats[0]
+    held = held * jnp.exp(teacher_local_peak - column_peak)[None, None, :, None]
+
+    def reduce_bits(part, bits, low_first):
+        for bit in bits:
+            pairs = [(j, j ^ (1 << bit)) for j in range(dp_count)]
+            count = part.shape[0] // 2
+            if low_first:
+                split = part.reshape((count, 2) + part.shape[1:])
+                keep, send = split[:, 0], split[:, 1]
+            else:
+                split = part.reshape((2, count) + part.shape[1:])
+                keep, send = split[0], split[1]
+            part = keep + lax.ppermute(send.astype(jnp.bfloat16), "dp", pairs).astype(
+                jnp.float32
+            )
+        return part
+
+    held = reduce_bits(held, [0], True)
+    bits = list(range(1, dp_count.bit_length() - 1))
+    half = tokens_all // 2
+    first = reduce_bits(held[:, :, :half], bits, True)
+    second = reduce_bits(held[:, :, half:], bits[::-1], False)
+    held = jnp.concatenate([first, second], axis=2)
+
     stage = 1
     while stage < vocab_count:
         pairs = [(j, j ^ stage) for j in range(vocab_count)]

time: 185 us -> 180 us (0.973)
  blocking collectives: 36.2 us -> 39.3 us
  local copies, waits for them, and re-layouts: 9.84 us -> 6.98 us
  waiting for transfers between devices: 50.4 us -> 48.2 us
  starting transfers between devices: 20 us -> 17.9 us
    ppermute x3, waiting for transfers between devices: 23.9 us -> 3.39 us  [on_device(): lax.ppermute(student_stats, 'dp', pairs)]
    ppermute x3, waiting for transfers between devices: 3.64 us -> 13.2 us  [on_device(): lax.ppermute(teacher_stats, 'dp', pairs)]
    ppermute x3 -> x5, waiting for transfers between devices: 21.6 us -> 30.6 us  [reduce_bits(): lax.ppermute(send.astype(jnp.bfloat16), 'dp', pairs).astype(jnp.float32)]
    unnamed x17 -> x11, local copies, waits for them, and re-layouts: 7.7 us -> 3.36 us
    ppermute x3 -> x5, starting transfers between devices: 3.27 us -> 6.77 us  [reduce_bits(): lax.ppermute(send.astype(jnp.bfloat16), 'dp', pairs).astype(jnp.float32)]
    ppermute x3, starting transfers between devices: 3.59 us -> 0.21 us  [on_device(): lax.ppermute(student_stats, 'dp', pairs)]
    all_to_all x1, blocking collectives: 19.4 us -> 22.5 us  [on_device(): lax.all_to_all(partial, ('dp', 'vocab'), split_axis=0, concat_axis=0, til...]
  transfers between devices with their start and end apart: 12 -> 14, of which waited for: 5 -> 7; matrix products, arithmetic and copies ran while one was open for 13% -> 13% of each run, Pallas kernels for 0% -> 0%
where the time goes in v8:
time: 180 us
  matrix products  60.1 us (33%)
  waiting for transfers between devices  48.2 us (27%)
  blocking collectives  39.3 us (22%)
  starting transfers between devices  17.9 us (10%)
  local copies, waits for them, and re-layouts  6.98 us (4%)
  other arithmetic  6.91 us (4%)
    ppermute x5, waiting for transfers between devices, reduce_bits(): lax.ppermute(send.astype(jnp.bfloat16), 'dp', pairs).astype(jnp.float32)  30.6 us
    dot_general x1, matrix products, on_device(): jnp.dot(teacher_all, teacher_head, preferred_element_type=jnp.float32)  23.4 us
    all_to_all x1, blocking collectives, on_device(): lax.all_to_all(partial, ('dp', 'vocab'), split_axis=0, concat_axis=0, til...  22.5 us
    all_gather x1, blocking collectives, on_device(): gathered = lax.all_gather(packed, 'dp', axis=0, tiled=True)  16.8 us
    dot_general x1, matrix products, on_device(): lax.dot_general(logit_grad, student_head, (((1,), (1,)), ((), ())), prefe...  16.4 us
    dot_general x1, matrix products, on_device(): jnp.dot(student_all, student_head, preferred_element_type=jnp.float32)  13.8 us
    ppermute x3, waiting for transfers between devices, on_device(): lax.ppermute(teacher_stats, 'dp', pairs)  13.2 us
    ppermute x5, starting transfers between devices, reduce_bits(): lax.ppermute(send.astype(jnp.bfloat16), 'dp', pairs).astype(jnp.float32)  6.77 us
  transfers between devices with their start and end apart: 14, of which 7 were waited for; matrix products, arithmetic and copies ran while one was open for 13% of the time, Pallas kernels for 0%

profile of v8, /device:TPU:1, one launch (start us, length us, event | category | flops | bytes accessed | tf_op | source)
XLA Modules:
  0.0 179.7 jit_solution(5000186134460024794)
XLA Ops:
  0.0 0.7 convert_convert_fusion
  0.7 0.1 fusion.37
  0.7 0.9 pad_maximum_fusion
  1.6 16.8 %all_gather.3 = bf16[64,5248]{1,0:T(8,128)(2,1)S(1)} all-gather(bf16[8,5248]{1,0:T(8,128)(2,1)S(1)} %pad_maximum_fusion), channel_id=1, replica_groups=mesh['groups'=2,'dp'=8,'vocab'=2] {'dp'}, dimensions={0}, use_global_device_ids=true | all-gather | bytes 755712 | tf_op jit(solution)/shard_map/all_gather | solution.py:50
  18.5 23.4 %fusion.68 = (f32[64]{0:T(128)S(1)}, f32[64,6144]{1,0:T(8,128)S(1)}) fusion(bf16[5120,6144]{1,0:T(8,128)(2,1)} %param.9, bf16[64,5248]{1,0:T(8,128)(2,1)S(1)} %all_gather.3), kind=kOutput, calls=%fused_computation.143 | convolution fusion | flops 4026925056 | bytes 65143040 | tf_op jit(solution)/shard_map/dot_general | solution.py:62
  41.9 0.3 fusion.11
  42.2 0.1 copy.30
  42.3 0.0 copy-start.2
  42.3 0.0 copy-start.3
  42.3 0.0 copy-start.4
  42.3 0.0 slice-start
  42.3 4.0 %convert_reduce_fusion = (f32[64]{0:T(128)S(1)}, bf16[48,64,4,128]{3,1,2,0:T(8,128)(2,1)S(1)}) fusion(bf16[48,4,128,128]{3,2,1,0:T(8,128)(2,1)} %param.12, bf16[64,48,128,1]{2,1,0,3:T(8,128)(2,1)S(1)} %bitcast.240), kind=kOutput, calls=%fused_computation | convolution fusion | flops 407371712 | bytes 10223872 | tf_op jit(solution)/shard_map/gkc,krcd->krgd/dot_general | solution.py:66
  46.3 0.2 collective-permute-start.4
  46.6 1.0 collective-permute-done.4
  47.6 1.3 collective-permute-start.5
  48.8 0.8 broadcast_in_dim.2
  49.7 4.5 %all-to-all-start = ((bf16[8,8,4096]{2,1,0:T(8,128)(2,1)}), bf16[8,8,4096]{2,1,0:T(8,128)(2,1)}, u32[]{:S(2)}, u32[]{:S(2)}) async-start(bf16[8,8,4096]{2,1,0:T(8,128)(2,1)} %broadcast_in_dim.2), calls=%async_computation | async-start | bytes 1048576 | tf_op jit(solution)/shard_map/all_to_all | solution.py:51
  54.2 0.0 collective-permute-done.5
  54.2 2.3 %collective-permute-start.6 = (f32[2,64]{1,0:T(2,128)S(1)}, f32[2,64]{1,0:T(2,128)S(1)}, u32[]{:S(2)}, u32[]{:S(2)}) collective-permute-start(f32[2,64]{1,0:T(2,128)S(1)} %pad_maximum_fusion.7), channel_id=1, source_target_pairs={{0,8},{2,10},{4,12},{6,14},{8,0},{10,2},{12,4},{14,6},{1,9},{3,11}... | collective-permute-start | bytes 1544 | tf_op jit(solution)/shard_map/ppermute | solution.py:99
  56.5 0.0 copy-done.3
  56.5 12.2 %collective-permute-done.6 = f32[2,64]{1,0:T(2,128)S(1)} collective-permute-done((f32[2,64]{1,0:T(2,128)S(1)}, f32[2,64]{1,0:T(2,128)S(1)}, u32[]{:S(2)}, u32[]{:S(2)}) %collective-permute-start.6) | collective-permute-done | bytes 544 | tf_op jit(solution)/shard_map/ppermute | solution.py:99
  68.7 1.3 collective-permute-start.12
  70.0 0.1 copy.14
  70.1 0.1 add.142
  70.2 1.0 collective-permute-done.12
  71.3 2.5 %broadcast_multiply_fusion = f32[8,32,64,128]{3,1,2,0:T(8,128)S(1)} fusion(f32[64]{0:T(128)S(1)} %get-tuple-element.22, s32[192]{0:T(256)S(1)} %add.142, s32[8,32]{1,0:T(8,128)S(1)} %multiply_add_fusion, bf16[24,8,64,128]{3,2,1,0:T(8,128)(2,1)S(1)} %bitcast.236), kind=kOutput, calls=%fused_computation.5 | convolution fusion | flops 807452672 | bytes 11536384 | tf_op jit(solution)/shard_map/dot_general | solution.py:76
  73.8 3.2 %copy-done = f32[8,32,64,128]{3,1,2,0:T(8,128)} copy-done((f32[8,32,64,128]{3,1,2,0:T(8,128)}, f32[8,32,64,128]{3,1,2,0:T(8,128)S(1)}, u32[]{:S(2)}) %copy-start) | copy-done | bytes 8388632
  77.0 1.9 %fusion.2 = bf16[4,32,64,128]{3,1,2,0:T(8,128)(2,1)} fusion(f32[4,2,32,64,128]{4,2,3,1,0:T(8,128)S(1)} %bitcast.234), kind=kLoop, calls=%fused_computation.10 | loop fusion | bytes 4194304 | tf_op jit(solution)/shard_map/convert_element_type | solution.py:115
  78.9 2.1 %collective-permute-start.7 = (bf16[4,32,64,128]{3,1,2,0:T(8,128)(2,1)}, bf16[4,32,64,128]{3,1,2,0:T(8,128)(2,1)S(1)}, u32[]{:S(2)}, u32[]{:S(2)}) collective-permute-start(bf16[4,32,64,128]{3,1,2,0:T(8,128)(2,1)} %fusion.2), channel_id=1, source_target_pairs={{0,2},{2,0},{4,6},{6,4},{8,10},{10,8},{12,14},{14,12},{1,3},{3,1},... | collective-permute-start | bytes 6291464 | tf_op jit(solution)/shard_map/ppermute | solution.py:115
  81.0 0.0 all-to-all-done
  81.0 13.8 %fusion.69 = (f32[64]{0:T(128)S(1)}, f32[64,4096]{1,0:T(8,128)S(1)}) fusion(bf16[4096,4096]{1,0:T(8,128)(2,1)} %param.14, bf16[8,8,4096]{2,1,0:T(8,128)(2,1)} %all-to-all-done), kind=kOutput, calls=%fused_computation.144 | convolution fusion | flops 2147745792 | bytes 35127552 | tf_op jit(solution)/shard_map/dot_general | solution.py:82
  94.9 0.3 exponential_reduce_fusion
  95.2 0.1 collective-permute-start
  95.3 0.1 convert_add_fusion
  95.4 1.1 collective-permute-done
  96.5 0.1 collective-permute-start.1
  96.6 0.1 eq.47
  96.6 2.3 %collective-permute-done.1 = f32[2,64]{1,0:T(2,128)S(1)} collective-permute-done((f32[2,64]{1,0:T(2,128)S(1)}, f32[2,64]{1,0:T(2,128)S(1)}, u32[]{:S(2)}, u32[]{:S(2)}) %collective-permute-start.1) | collective-permute-done | bytes 544 | tf_op jit(solution)/shard_map/ppermute | solution.py:100
  99.0 0.1 collective-permute-start.2
  99.1 0.0 collective-permute-done.7
  99.1 2.9 %fusion = f32[4,32,64,128]{3,1,2,0:T(8,128)S(1)} fusion(bf16[4,32,64,128]{3,1,2,0:T(8,128)(2,1)S(1)} %collective-permute-done.7, f32[4,2,32,64,128]{4,2,3,1,0:T(8,128)} %bitcast.235), kind=kLoop, calls=%fused_computation.4 | loop fusion | flops 2097152 | bytes 10485760 | tf_op jit(solution)/shard_map/add | solution.py:115
  102.0 0.1 slice.221
  102.1 0.2 slice.147
  102.3 2.4 %collective-permute-start.10 = (bf16[2,32,32,128]{3,1,2,0:T(8,128)(2,1)S(1)}, bf16[2,32,32,128]{3,1,2,0:T(8,128)(2,1)S(1)}, u32[]{:S(2)}, u32[]{:S(2)}) collective-permute-start(bf16[2,32,32,128]{3,1,2,0:T(8,128)(2,1)S(1)} %slice.221), channel_id=1, source_target_pairs={{0,8},{2,10},{4,12},{6,14},{8,0},{10,2},{12,4},{14,6},{1,9},{3,11}... | collective-permute-start | bytes 1572872 | tf_op jit(solution)/shard_map/ppermute | solution.py:115
  104.7 0.1 fusion.16
  104.8 0.1 collective-permute-start.8
  104.8 0.0 collective-permute-done.2
  104.9 1.3 collective-permute-start.3
  106.2 21.2 %collective-permute-done.10 = bf16[2,32,32,128]{3,1,2,0:T(8,128)(2,1)S(1)} collective-permute-done((bf16[2,32,32,128]{3,1,2,0:T(8,128)(2,1)S(1)}, bf16[2,32,32,128]{3,1,2,0:T(8,128)(2,1)S(1)}, u32[]{:S(2)}, u32[]{:S(2)}) %collective-permute-start.10) | collective-permute-done | bytes 524320 | tf_op jit(solution)/shard_map/ppermute | solution.py:115
  127.4 0.2 slice_add_fusion
  127.6 0.1 collective-permute-start.11
  127.7 0.0 collective-permute-done.8
  127.7 0.2 fusion.8
  127.9 2.1 %collective-permute-start.9 = (bf16[1,32,32,128]{3,1,2,0:T(8,128)(2,1)S(1)}, bf16[1,32,32,128]{3,1,2,0:T(8,128)(2,1)S(1)}, u32[]{:S(2)}, u32[]{:S(2)}) collective-permute-start(bf16[1,32,32,128]{3,1,2,0:T(8,128)(2,1)S(1)} %fusion.29), channel_id=1, source_target_pairs={{0,8},{2,10},{4,12},{6,14},{8,0},{10,2},{12,4},{14,6},{1,9},{3,11}... | collective-permute-start | bytes 786440 | tf_op jit(solution)/shard_map/ppermute | solution.py:115
  130.1 0.0 collective-permute-done.3
  130.1 9.4 %collective-permute-done.11 = bf16[1,32,32,128]{3,1,2,0:T(8,128)(2,1)S(1)} collective-permute-done((bf16[1,32,32,128]{3,1,2,0:T(8,128)(2,1)S(1)}, bf16[1,32,32,128]{3,1,2,0:T(8,128)(2,1)S(1)}, u32[]{:S(2)}, u32[]{:S(2)}) %collective-permute-start.11) | collective-permute-done | bytes 262176 | tf_op jit(solution)/shard_map/ppermute | solution.py:115
  139.5 0.1 slice_add_fusion.1
  139.6 0.0 collective-permute-done.9
  139.6 0.1 fusion.17
  139.7 0.1 fusion.9
  139.8 16.4 %convolution_convert_fusion = bf16[64,4096]{1,0:T(8,128)(2,1)S(1)} fusion(bf16[4096,4096]{1,0:T(8,128)(2,1)} %param.14, f32[8,8,32,128]{3,2,1,0:T(8,128)S(1)} %bitcast.239, f32[64,4096]{1,0:T(8,128)S(1)} %get-tuple-element.30, s32[4096]{0:T(1024)S(1)} %iota_add_fusion, f32[64]{0:T(128)S(1)} %get-tuple-element.11, f32[64]{0:T(128)S(1)} %get-tuple-element.5, ...), kind=kOutput, calls=%fused_computation.1 | convolution fusion | flops 2150367232 | bytes 36193280 | tf_op jit(solution)/shard_map/dot_general | solution.py:147
  156.2 0.2 reshape.347
  156.4 22.5 %all_to_all.10 = bf16[16,4,4096]{2,1,0:T(4,128)(2,1)S(1)} all-to-all(bf16[16,4,4096]{2,1,0:T(4,128)(2,1)S(1)} %reshape.347), channel_id=1, replica_groups=mesh['groups'=2,'dp'=8,'vocab'=2] {'dp','vocab'}, dimensions={0} | all-to-all | bytes 1048576 | tf_op jit(solution)/shard_map/all_to_all | solution.py:152
  178.9 0.8 reduce_sum.32
  (29 shorter events, 0.3 us)
Async XLA Ops:
  18.5 23.4 %copy-start.1 = (bf16[64,5248]{1,0:T(8,128)(2,1)}, bf16[64,5248]{1,0:T(8,128)(2,1)S(1)}, u32[]{:S(2)}) copy-start(bf16[64,5248]{1,0:T(8,128)(2,1)S(1)} %all_gather.3) | copy-start | bytes 2015236
  42.3 6.6 %copy-start.2 = (bf16[8,4096]{1,0:T(8,128)(2,1)S(1)}, bf16[8,4096]{1,0:T(8,128)(2,1)}, u32[]{:S(2)}) copy-start(bf16[8,4096]{1,0:T(8,128)(2,1)} %param.13) | copy-start | bytes 196612
  42.3 14.2 %copy-start.3 = (s32[48,4]{0,1:T(4,128)S(1)}, s32[48,4]{0,1:T(4,128)}, u32[]{:S(2)}) copy-start(s32[48,4]{0,1:T(4,128)} %param.11) | copy-start | bytes 2308
  42.3 14.2 %copy-start.4 = (s32[48,4]{0,1:T(4,128)S(1)}, s32[48,4]{0,1:T(4,128)}, u32[]{:S(2)}) copy-start(s32[48,4]{0,1:T(4,128)} %param.10) | copy-start | bytes 2308
  42.3 27.9 %slice-start = ((bf16[64,5248]{1,0:T(8,128)(2,1)}), bf16[64,128]{1,0:T(8,128)(2,1)S(1)}, s32[]{:S(2)}) async-start(bf16[64,5248]{1,0:T(8,128)(2,1)} %copy-done.1), calls=%async_computation.2 | async-start | bytes 32768 | tf_op jit(solution)/shard_map/slice | solution.py:57
  46.3 1.2 collective-permute-start.4
  47.6 6.6 %collective-permute-start.5 = (f32[2,64]{1,0:T(2,128)S(1)}, f32[2,64]{1,0:T(2,128)S(1)}, u32[]{:S(2)}, u32[]{:S(2)}) collective-permute-start(f32[2,64]{1,0:T(2,128)S(1)} %pad_maximum_fusion.6), channel_id=1, source_target_pairs={{0,4},{2,6},{4,0},{6,2},{8,12},{10,14},{12,8},{14,10},{1,5},{3,7},... | collective-permute-start | bytes 1544 | tf_op jit(solution)/shard_map/ppermute | solution.py:99
  49.7 31.3 %all-to-all-start = ((bf16[8,8,4096]{2,1,0:T(8,128)(2,1)}), bf16[8,8,4096]{2,1,0:T(8,128)(2,1)}, u32[]{:S(2)}, u32[]{:S(2)}) async-start(bf16[8,8,4096]{2,1,0:T(8,128)(2,1)} %broadcast_in_dim.2), calls=%async_computation | async-start | bytes 1048576 | tf_op jit(solution)/shard_map/all_to_all | solution.py:51
  54.2 14.5 %collective-permute-start.6 = (f32[2,64]{1,0:T(2,128)S(1)}, f32[2,64]{1,0:T(2,128)S(1)}, u32[]{:S(2)}, u32[]{:S(2)}) collective-permute-start(f32[2,64]{1,0:T(2,128)S(1)} %pad_maximum_fusion.7), channel_id=1, source_target_pairs={{0,8},{2,10},{4,12},{6,14},{8,0},{10,2},{12,4},{14,6},{1,9},{3,11}... | collective-permute-start | bytes 1544 | tf_op jit(solution)/shard_map/ppermute | solution.py:99
  68.7 2.5 %collective-permute-start.12 = (f32[2,64]{1,0:T(2,128)S(1)}, f32[2,64]{1,0:T(2,128)S(1)}, u32[]{:S(2)}, u32[]{:S(2)}) collective-permute-start(f32[2,64]{1,0:T(2,128)S(1)} %pad_maximum_fusion.8), channel_id=1, source_target_pairs={{0,1},{1,0},{2,3},{3,2},{4,5},{5,4},{6,7},{7,6},{8,9},{9,8},{10,11... | collective-permute-start | bytes 1544 | tf_op jit(solution)/shard_map/ppermute | solution.py:130
  73.8 3.2 %copy-start = (f32[8,32,64,128]{3,1,2,0:T(8,128)}, f32[8,32,64,128]{3,1,2,0:T(8,128)S(1)}, u32[]{:S(2)}) copy-start(f32[8,32,64,128]{3,1,2,0:T(8,128)S(1)} %broadcast_multiply_fusion) | copy-start | bytes 25165828
  78.9 20.2 %collective-permute-start.7 = (bf16[4,32,64,128]{3,1,2,0:T(8,128)(2,1)}, bf16[4,32,64,128]{3,1,2,0:T(8,128)(2,1)S(1)}, u32[]{:S(2)}, u32[]{:S(2)}) collective-permute-start(bf16[4,32,64,128]{3,1,2,0:T(8,128)(2,1)} %fusion.2), channel_id=1, source_target_pairs={{0,2},{2,0},{4,6},{6,4},{8,10},{10,8},{12,14},{14,12},{1,3},{3,1},... | collective-permute-start | bytes 6291464 | tf_op jit(solution)/shard_map/ppermute | solution.py:115
  95.2 1.2 collective-permute-start
  96.5 2.5 %collective-permute-start.1 = (f32[2,64]{1,0:T(2,128)S(1)}, f32[2,64]{1,0:T(2,128)S(1)}, u32[]{:S(2)}, u32[]{:S(2)}) collective-permute-start(f32[2,64]{1,0:T(2,128)S(1)} %pad_maximum_fusion.2), channel_id=1, source_target_pairs={{0,4},{2,6},{4,0},{6,2},{8,12},{10,14},{12,8},{14,10},{1,5},{3,7},... | collective-permute-start | bytes 1544 | tf_op jit(solution)/shard_map/ppermute | solution.py:100
  99.0 5.9 %collective-permute-start.2 = (f32[2,64]{1,0:T(2,128)S(1)}, f32[2,64]{1,0:T(2,128)S(1)}, u32[]{:S(2)}, u32[]{:S(2)}) collective-permute-start(f32[2,64]{1,0:T(2,128)S(1)} %pad_maximum_fusion.3), channel_id=1, source_target_pairs={{0,8},{2,10},{4,12},{6,14},{8,0},{10,2},{12,4},{14,6},{1,9},{3,11}... | collective-permute-start | bytes 1544 | tf_op jit(solution)/shard_map/ppermute | solution.py:100
  102.3 25.1 %collective-permute-start.10 = (bf16[2,32,32,128]{3,1,2,0:T(8,128)(2,1)S(1)}, bf16[2,32,32,128]{3,1,2,0:T(8,128)(2,1)S(1)}, u32[]{:S(2)}, u32[]{:S(2)}) collective-permute-start(bf16[2,32,32,128]{3,1,2,0:T(8,128)(2,1)S(1)} %slice.221), channel_id=1, source_target_pairs={{0,8},{2,10},{4,12},{6,14},{8,0},{10,2},{12,4},{14,6},{1,9},{3,11}... | collective-permute-start | bytes 1572872 | tf_op jit(solution)/shard_map/ppermute | solution.py:115
  104.8 22.9 %collective-permute-start.8 = (bf16[2,32,32,128]{3,1,2,0:T(8,128)(2,1)S(1)}, bf16[2,32,32,128]{3,1,2,0:T(8,128)(2,1)S(1)}, u32[]{:S(2)}, u32[]{:S(2)}) collective-permute-start(bf16[2,32,32,128]{3,1,2,0:T(8,128)(2,1)S(1)} %fusion.16), channel_id=1, source_target_pairs={{0,4},{2,6},{4,0},{6,2},{8,12},{10,14},{12,8},{14,10},{1,5},{3,7},... | collective-permute-start | bytes 1572872 | tf_op jit(solution)/shard_map/ppermute | solution.py:115
  104.9 25.2 %collective-permute-start.3 = (f32[2,64]{1,0:T(2,128)S(1)}, f32[2,64]{1,0:T(2,128)S(1)}, u32[]{:S(2)}, u32[]{:S(2)}) collective-permute-start(f32[2,64]{1,0:T(2,128)S(1)} %pad_maximum_fusion.4), channel_id=1, source_target_pairs={{0,1},{1,0},{2,3},{3,2},{4,5},{5,4},{6,7},{7,6},{8,9},{9,8},{10,11... | collective-permute-start | bytes 1544 | tf_op jit(solution)/shard_map/ppermute | solution.py:131
  127.6 11.9 %collective-permute-start.11 = (bf16[1,32,32,128]{3,1,2,0:T(8,128)(2,1)S(1)}, bf16[1,32,32,128]{3,1,2,0:T(8,128)(2,1)S(1)}, u32[]{:S(2)}, u32[]{:S(2)}) collective-permute-start(bf16[1,32,32,128]{3,1,2,0:T(8,128)(2,1)S(1)} %slice.222), channel_id=1, source_target_pairs={{0,4},{2,6},{4,0},{6,2},{8,12},{10,14},{12,8},{14,10},{1,5},{3,7},... | collective-permute-start | bytes 786440 | tf_op jit(solution)/shard_map/ppermute | solution.py:115
  127.9 11.6 %collective-permute-start.9 = (bf16[1,32,32,128]{3,1,2,0:T(8,128)(2,1)S(1)}, bf16[1,32,32,128]{3,1,2,0:T(8,128)(2,1)S(1)}, u32[]{:S(2)}, u32[]{:S(2)}) collective-permute-start(bf16[1,32,32,128]{3,1,2,0:T(8,128)(2,1)S(1)} %fusion.29), channel_id=1, source_target_pairs={{0,8},{2,10},{4,12},{6,14},{8,0},{10,2},{12,4},{14,6},{1,9},{3,11}... | collective-permute-start | bytes 786440 | tf_op jit(solution)/shard_map/ppermute | solution.py:115

commit v9 on v8

--- a/solution.py
+++ b/solution.py
@@ -45,16 +45,15 @@
     extra_width = -(-extra_width // 128) * 128
     coded = jnp.pad(coded, (0, extra_width * local_tokens - coded.shape[0]))
     packed = jnp.concatenate(
-        [teacher_hidden, coded.reshape(local_tokens, extra_width)], axis=1
+        [teacher_hidden, student_hidden, coded.reshape(local_tokens, extra_width)], axis=1
     )
     gathered = lax.all_gather(packed, "dp", axis=0, tiled=True)
-    student_all = lax.all_to_all(
-        jnp.broadcast_to(student_hidden[None], (dp_count,) + student_hidden.shape),
-        "dp", split_axis=0, concat_axis=0, tiled=True,
-    ).reshape(dp_count * local_tokens, student_width)
     tokens_all = gathered.shape[0]
     teacher_all = gathered[:, :teacher_width]
-    extra_all = gathered[:, teacher_width:].reshape(dp_count, local_tokens * extra_width)
+    student_all = gathered[:, teacher_width : teacher_width + student_width]
+    extra_all = gathered[:, teacher_width + student_width :].reshape(
+        dp_count, local_tokens * extra_width
+    )
     t_hi = _decode(extra_all[:, :local_tokens])
     t_lo = _decode(extra_all[:, local_tokens : 2 * local_tokens])
     all_targets = (t_hi * 256 + t_lo).reshape(tokens_all)

time: 180 us -> 191 us (1.061)
  waiting for transfers between devices: 48.2 us -> 65.1 us
  blocking collectives: 39.3 us -> 22.6 us
  between operations: 0.34 us -> 13.7 us
  starting transfers between devices: 17.9 us -> 15.7 us
    all_gather x0 -> x1, waiting for transfers between devices: none -> 25.5 us  [on_device(): gathered = lax.all_gather(packed, 'dp', axis=0, tiled=True)]
    all_gather x1 -> x0, blocking collectives: 16.8 us -> none  [on_device(): gathered = lax.all_gather(packed, 'dp', axis=0, tiled=True)]
    ppermute x3, waiting for transfers between devices: 13.2 us -> 4.16 us  [on_device(): lax.ppermute(teacher_stats, 'dp', pairs)]
    all_to_all x1 -> x0, starting transfers between devices: 4.48 us -> none  [on_device(): lax.all_to_all(jnp.broadcast_to(student_hidden[None], (dp_count,) + stude...]
    ppermute x3, starting transfers between devices: 0.21 us -> 2.66 us  [on_device(): lax.ppermute(student_stats, 'dp', pairs)]
  transfers between devices with their start and end apart: 14 -> 14, of which waited for: 7 -> 9; matrix products, arithmetic and copies ran while one was open for 13% -> 10% of each run, Pallas kernels for 0% -> 0%
where the time goes in v9:
time: 191 us
  waiting for transfers between devices  65.1 us (34%)
  matrix products  60 us (31%)
  blocking collectives  22.6 us (12%)
  starting transfers between devices  15.7 us (8%)
  between operations  13.7 us (7%)
  other arithmetic  7.61 us (4%)
  local copies, waits for them, and re-layouts  6.14 us (3%)
    ppermute x5, waiting for transfers between devices, reduce_bits(): lax.ppermute(send.astype(jnp.bfloat16), 'dp', pairs).astype(jnp.float32)  31.9 us
    all_gather x1, waiting for transfers between devices, on_device(): gathered = lax.all_gather(packed, 'dp', axis=0, tiled=True)  25.5 us
    dot_general x1, matrix products, on_device(): jnp.dot(teacher_all, teacher_head, preferred_element_type=jnp.float32)  23.2 us
    all_to_all x1, blocking collectives, on_device(): lax.all_to_all(partial, ('dp', 'vocab'), split_axis=0, concat_axis=0, til...  22.6 us
    dot_general x1, matrix products, on_device(): lax.dot_general(logit_grad, student_head, (((1,), (1,)), ((), ())), prefe...  16.4 us
    dot_general x1, matrix products, on_device(): jnp.dot(student_all, student_head, preferred_element_type=jnp.float32)  13.9 us
    ppermute x5, starting transfers between devices, reduce_bits(): lax.ppermute(send.astype(jnp.bfloat16), 'dp', pairs).astype(jnp.float32)  7.74 us
    ppermute x3, waiting for transfers between devices, on_device(): lax.ppermute(teacher_stats, 'dp', pairs)  4.16 us
  transfers between devices with their start and end apart: 14, of which 9 were waited for; matrix products, arithmetic and copies ran while one was open for 10% of the time, Pallas kernels for 0%

profile of v9, /device:TPU:1, one launch (start us, length us, event | category | flops | bytes accessed | tf_op | source)
XLA Modules:
  0.0 190.8 jit_solution(17350286868551371705)
XLA Ops:
  6.5 0.0 all-gather.2.cloned.1.call-start
  6.5 0.7 convert_convert_fusion
  7.2 0.1 fusion.37
  7.3 1.6 pad_maximum_fusion
  8.9 0.0 all-gather.2.cloned.1.call-update
  8.9 25.5 %all-gather.2.cloned.1.call-done = bf16[64,9344]{1,0:T(8,128)(2,1)} async-done(((bf16[8,9344]{1,0:T(8,128)(2,1)}), bf16[64,9344]{1,0:T(8,128)(2,1)}) %all-gather.2.cloned.1.call-update) | async-done | bytes 1196048 | tf_op jit(solution)/shard_map/all_gather | solution.py:50
  34.4 23.2 %fusion.68 = (f32[64]{0:T(128)S(1)}, f32[64,6144]{1,0:T(8,128)S(1)}) fusion(bf16[5120,6144]{1,0:T(8,128)(2,1)} %param.9, bf16[64,9344]{1,0:T(8,128)(2,1)} %all-gather.2.cloned.1.call-done), kind=kOutput, calls=%fused_computation.143 | convolution fusion | flops 4026925056 | bytes 65143040 | tf_op jit(solution)/shard_map/dot_general | solution.py:61
  57.6 0.3 fusion.11
  57.9 0.1 copy.30
  58.0 0.0 copy-start.2
  58.0 0.0 copy-start.3
  58.0 4.0 %convert_reduce_fusion = (f32[64]{0:T(128)S(1)}, bf16[48,64,4,128]{3,1,2,0:T(8,128)(2,1)S(1)}) fusion(bf16[48,4,128,128]{3,2,1,0:T(8,128)(2,1)} %param.12, bf16[64,48,128,1]{2,1,0,3:T(8,128)(2,1)S(1)} %bitcast.235), kind=kOutput, calls=%fused_computation | convolution fusion | flops 407371712 | bytes 10223872 | tf_op jit(solution)/shard_map/gkc,krcd->krgd/dot_general | solution.py:65
  62.0 0.4 collective-permute-start.4
  62.4 0.9 collective-permute-done.4
  63.3 1.0 collective-permute-start.5
  64.3 1.5 collective-permute-done.5
  65.8 1.5 collective-permute-start.6
  67.3 0.0 copy-done.2
  67.3 0.0 copy-done.3
  67.4 1.8 collective-permute-done.6
  69.2 1.1 collective-permute-start.12
  70.3 0.1 copy.14
  70.4 0.1 add.143
  70.5 1.2 collective-permute-done.12
  71.7 2.5 %broadcast_multiply_fusion = f32[8,32,64,128]{3,1,2,0:T(8,128)S(1)} fusion(f32[64]{0:T(128)S(1)} %get-tuple-element.22, s32[192]{0:T(256)S(1)} %add.143, s32[8,32]{1,0:T(8,128)S(1)} %multiply_add_fusion, bf16[24,8,64,128]{3,2,1,0:T(8,128)(2,1)S(1)} %bitcast.231), kind=kOutput, calls=%fused_computation.5 | convolution fusion | flops 807452672 | bytes 11536384 | tf_op jit(solution)/shard_map/dot_general | solution.py:75
  74.3 0.0 copy-start
  74.3 0.0 copy-start.1
  74.3 3.2 %copy-done = f32[8,32,64,128]{3,1,2,0:T(8,128)} copy-done((f32[8,32,64,128]{3,1,2,0:T(8,128)}, f32[8,32,64,128]{3,1,2,0:T(8,128)S(1)}, u32[]{:S(2)}) %copy-start) | copy-done | bytes 8388632
  77.5 1.9 fusion.2
  79.4 3.7 %collective-permute-start.7 = (bf16[4,32,64,128]{3,1,2,0:T(8,128)(2,1)}, bf16[4,32,64,128]{3,1,2,0:T(8,128)(2,1)S(1)}, u32[]{:S(2)}, u32[]{:S(2)}) collective-permute-start(bf16[4,32,64,128]{3,1,2,0:T(8,128)(2,1)} %fusion.2), channel_id=1, source_target_pairs={{0,2},{2,0},{4,6},{6,4},{8,10},{10,8},{12,14},{14,12},{1,3},{3,1},... | collective-permute-start | bytes 6291464 | tf_op jit(solution)/shard_map/ppermute | solution.py:114
  83.1 13.9 %fusion.69 = (f32[64]{0:T(128)S(1)}, f32[64,4096]{1,0:T(8,128)S(1)}) fusion(bf16[4096,4096]{1,0:T(8,128)(2,1)} %param.14, bf16[64,9344]{1,0:T(8,128)(2,1)S(1)} %copy-done.1), kind=kOutput, calls=%fused_computation.144 | convolution fusion | flops 2147745792 | bytes 35127552 | tf_op jit(solution)/shard_map/dot_general | solution.py:81
  97.1 0.3 exponential_reduce_fusion
  97.4 0.1 collective-permute-start
  97.5 1.1 collective-permute-done
  98.7 1.0 collective-permute-start.1
  99.7 0.1 convert_add_fusion
  99.8 0.1 eq.47
  99.9 1.3 collective-permute-done.1
  101.2 1.6 collective-permute-start.2
  102.7 0.0 collective-permute-done.7
  102.7 2.9 %fusion = f32[4,32,64,128]{3,1,2,0:T(8,128)S(1)} fusion(bf16[4,32,64,128]{3,1,2,0:T(8,128)(2,1)S(1)} %collective-permute-done.7, f32[4,2,32,64,128]{4,2,3,1,0:T(8,128)} %bitcast.230), kind=kLoop, calls=%fused_computation.4 | loop fusion | flops 2097152 | bytes 10485760 | tf_op jit(solution)/shard_map/add | solution.py:114
  105.7 0.1 slice.228
  105.8 0.2 slice.152
  105.9 0.9 collective-permute-start.10
  106.9 0.1 fusion.16
  107.0 1.0 collective-permute-start.8
  108.0 0.0 collective-permute-done.2
  108.0 1.2 collective-permute-start.3
  109.3 22.4 %collective-permute-done.10 = bf16[2,32,32,128]{3,1,2,0:T(8,128)(2,1)S(1)} collective-permute-done((bf16[2,32,32,128]{3,1,2,0:T(8,128)(2,1)S(1)}, bf16[2,32,32,128]{3,1,2,0:T(8,128)(2,1)S(1)}, u32[]{:S(2)}, u32[]{:S(2)}) %collective-permute-start.10) | collective-permute-done | bytes 524320 | tf_op jit(solution)/shard_map/ppermute | solution.py:114
  131.7 0.2 slice_add_fusion
  131.9 0.1 collective-permute-start.11
  132.0 0.0 collective-permute-done.8
  132.0 0.2 fusion.8
  132.2 2.0 %collective-permute-start.9 = (bf16[1,32,32,128]{3,1,2,0:T(8,128)(2,1)S(1)}, bf16[1,32,32,128]{3,1,2,0:T(8,128)(2,1)S(1)}, u32[]{:S(2)}, u32[]{:S(2)}) collective-permute-start(bf16[1,32,32,128]{3,1,2,0:T(8,128)(2,1)S(1)} %fusion.29), channel_id=1, source_target_pairs={{0,8},{2,10},{4,12},{6,14},{8,0},{10,2},{12,4},{14,6},{1,9},{3,11}... | collective-permute-start | bytes 786440 | tf_op jit(solution)/shard_map/ppermute | solution.py:114
  134.2 0.0 collective-permute-done.3
  134.2 9.5 %collective-permute-done.11 = bf16[1,32,32,128]{3,1,2,0:T(8,128)(2,1)S(1)} collective-permute-done((bf16[1,32,32,128]{3,1,2,0:T(8,128)(2,1)S(1)}, bf16[1,32,32,128]{3,1,2,0:T(8,128)(2,1)S(1)}, u32[]{:S(2)}, u32[]{:S(2)}) %collective-permute-start.11) | collective-permute-done | bytes 262176 | tf_op jit(solution)/shard_map/ppermute | solution.py:114
  143.7 0.1 slice_add_fusion.1
  143.8 0.0 collective-permute-done.9
  143.8 0.1 fusion.17
  143.9 0.1 fusion.9
  144.0 16.4 %convolution_convert_fusion = bf16[64,4096]{1,0:T(8,128)(2,1)S(1)} fusion(bf16[4096,4096]{1,0:T(8,128)(2,1)} %param.14, f32[8,8,32,128]{3,2,1,0:T(8,128)S(1)} %bitcast.234, f32[64,4096]{1,0:T(8,128)S(1)} %get-tuple-element.30, s32[4096]{0:T(1024)S(1)} %iota_add_fusion, f32[64]{0:T(128)S(1)} %get-tuple-element.11, f32[64]{0:T(128)S(1)} %get-tuple-element.5, ...), kind=kOutput, calls=%fused_computation.1 | convolution fusion | flops 2150367232 | bytes 36193280 | tf_op jit(solution)/shard_map/dot_general | solution.py:146
  160.4 0.2 reshape.342
  160.6 22.6 %all_to_all.5 = bf16[16,4,4096]{2,1,0:T(4,128)(2,1)S(1)} all-to-all(bf16[16,4,4096]{2,1,0:T(4,128)(2,1)S(1)} %reshape.342), channel_id=1, replica_groups=mesh['groups'=2,'dp'=8,'vocab'=2] {'dp','vocab'}, dimensions={0} | all-to-all | bytes 1048576 | tf_op jit(solution)/shard_map/all_to_all | solution.py:151
  183.2 0.8 reduce_sum.32
  (26 shorter events, 0.3 us)
Async XLA Ops:
  6.5 27.8 %all-gather.2.cloned.1.call-start = ((), (), s32[]{:S(2)}) async-start(), calls=%async_computation.1 | async-start | bytes 1345536 | tf_op jit(solution)/shard_map/all_gather | solution.py:50
  58.0 9.3 %copy-start.2 = (s32[48,4]{0,1:T(4,128)S(1)}, s32[48,4]{0,1:T(4,128)}, u32[]{:S(2)}) copy-start(s32[48,4]{0,1:T(4,128)} %param.11) | copy-start | bytes 2308
  58.0 9.3 %copy-start.3 = (s32[48,4]{0,1:T(4,128)S(1)}, s32[48,4]{0,1:T(4,128)}, u32[]{:S(2)}) copy-start(s32[48,4]{0,1:T(4,128)} %param.10) | copy-start | bytes 2308
  62.0 1.2 collective-permute-start.4
  63.3 2.5 %collective-permute-start.5 = (f32[2,64]{1,0:T(2,128)S(1)}, f32[2,64]{1,0:T(2,128)S(1)}, u32[]{:S(2)}, u32[]{:S(2)}) collective-permute-start(f32[2,64]{1,0:T(2,128)S(1)} %pad_maximum_fusion.6), channel_id=1, source_target_pairs={{0,4},{2,6},{4,0},{6,2},{8,12},{10,14},{12,8},{14,10},{1,5},{3,7},... | collective-permute-start | bytes 1544 | tf_op jit(solution)/shard_map/ppermute | solution.py:98
  65.8 3.4 %collective-permute-start.6 = (f32[2,64]{1,0:T(2,128)S(1)}, f32[2,64]{1,0:T(2,128)S(1)}, u32[]{:S(2)}, u32[]{:S(2)}) collective-permute-start(f32[2,64]{1,0:T(2,128)S(1)} %pad_maximum_fusion.7), channel_id=1, source_target_pairs={{0,8},{2,10},{4,12},{6,14},{8,0},{10,2},{12,4},{14,6},{1,9},{3,11}... | collective-permute-start | bytes 1544 | tf_op jit(solution)/shard_map/ppermute | solution.py:98
  69.2 2.5 %collective-permute-start.12 = (f32[2,64]{1,0:T(2,128)S(1)}, f32[2,64]{1,0:T(2,128)S(1)}, u32[]{:S(2)}, u32[]{:S(2)}) collective-permute-start(f32[2,64]{1,0:T(2,128)S(1)} %pad_maximum_fusion.8), channel_id=1, source_target_pairs={{0,1},{1,0},{2,3},{3,2},{4,5},{5,4},{6,7},{7,6},{8,9},{9,8},{10,11... | collective-permute-start | bytes 1544 | tf_op jit(solution)/shard_map/ppermute | solution.py:129
  74.3 3.2 %copy-start = (f32[8,32,64,128]{3,1,2,0:T(8,128)}, f32[8,32,64,128]{3,1,2,0:T(8,128)S(1)}, u32[]{:S(2)}) copy-start(f32[8,32,64,128]{3,1,2,0:T(8,128)S(1)} %broadcast_multiply_fusion) | copy-start | bytes 25165828
  74.3 8.8 %copy-start.1 = (bf16[64,9344]{1,0:T(8,128)(2,1)S(1)}, bf16[64,9344]{1,0:T(8,128)(2,1)}, u32[]{:S(2)}) copy-start(bf16[64,9344]{1,0:T(8,128)(2,1)} %all-gather.2.cloned.1.call-done) | copy-start | bytes 3588100
  79.4 18.1 %slice-start = ((bf16[64,9344]{1,0:T(8,128)(2,1)}), bf16[64,128]{1,0:T(8,128)(2,1)S(1)}, s32[]{:S(2)}) async-start(bf16[64,9344]{1,0:T(8,128)(2,1)} %all-gather.2.cloned.1.call-done), calls=%async_computation.2 | async-start | bytes 32768 | tf_op jit(solution)/shard_map/slice | solution.py:54
  79.4 23.4 %collective-permute-start.7 = (bf16[4,32,64,128]{3,1,2,0:T(8,128)(2,1)}, bf16[4,32,64,128]{3,1,2,0:T(8,128)(2,1)S(1)}, u32[]{:S(2)}, u32[]{:S(2)}) collective-permute-start(bf16[4,32,64,128]{3,1,2,0:T(8,128)(2,1)} %fusion.2), channel_id=1, source_target_pairs={{0,2},{2,0},{4,6},{6,4},{8,10},{10,8},{12,14},{14,12},{1,3},{3,1},... | collective-permute-start | bytes 6291464 | tf_op jit(solution)/shard_map/ppermute | solution.py:114
  97.4 1.2 collective-permute-start
  98.7 2.5 %collective-permute-start.1 = (f32[2,64]{1,0:T(2,128)S(1)}, f32[2,64]{1,0:T(2,128)S(1)}, u32[]{:S(2)}, u32[]{:S(2)}) collective-permute-start(f32[2,64]{1,0:T(2,128)S(1)} %pad_maximum_fusion.2), channel_id=1, source_target_pairs={{0,4},{2,6},{4,0},{6,2},{8,12},{10,14},{12,8},{14,10},{1,5},{3,7},... | collective-permute-start | bytes 1544 | tf_op jit(solution)/shard_map/ppermute | solution.py:99
  101.2 6.8 %collective-permute-start.2 = (f32[2,64]{1,0:T(2,128)S(1)}, f32[2,64]{1,0:T(2,128)S(1)}, u32[]{:S(2)}, u32[]{:S(2)}) collective-permute-start(f32[2,64]{1,0:T(2,128)S(1)} %pad_maximum_fusion.3), channel_id=1, source_target_pairs={{0,8},{2,10},{4,12},{6,14},{8,0},{10,2},{12,4},{14,6},{1,9},{3,11}... | collective-permute-start | bytes 1544 | tf_op jit(solution)/shard_map/ppermute | solution.py:99
  105.9 25.8 %collective-permute-start.10 = (bf16[2,32,32,128]{3,1,2,0:T(8,128)(2,1)S(1)}, bf16[2,32,32,128]{3,1,2,0:T(8,128)(2,1)S(1)}, u32[]{:S(2)}, u32[]{:S(2)}) collective-permute-start(bf16[2,32,32,128]{3,1,2,0:T(8,128)(2,1)S(1)} %slice.228), channel_id=1, source_target_pairs={{0,8},{2,10},{4,12},{6,14},{8,0},{10,2},{12,4},{14,6},{1,9},{3,11}... | collective-permute-start | bytes 1572872 | tf_op jit(solution)/shard_map/ppermute | solution.py:114
  107.0 25.0 %collective-permute-start.8 = (bf16[2,32,32,128]{3,1,2,0:T(8,128)(2,1)S(1)}, bf16[2,32,32,128]{3,1,2,0:T(8,128)(2,1)S(1)}, u32[]{:S(2)}, u32[]{:S(2)}) collective-permute-start(bf16[2,32,32,128]{3,1,2,0:T(8,128)(2,1)S(1)} %fusion.16), channel_id=1, source_target_pairs={{0,4},{2,6},{4,0},{6,2},{8,12},{10,14},{12,8},{14,10},{1,5},{3,7},... | collective-permute-start | bytes 1572872 | tf_op jit(solution)/shard_map/ppermute | solution.py:114
  108.0 26.2 %collective-permute-start.3 = (f32[2,64]{1,0:T(2,128)S(1)}, f32[2,64]{1,0:T(2,128)S(1)}, u32[]{:S(2)}, u32[]{:S(2)}) collective-permute-start(f32[2,64]{1,0:T(2,128)S(1)} %pad_maximum_fusion.4), channel_id=1, source_target_pairs={{0,1},{1,0},{2,3},{3,2},{4,5},{5,4},{6,7},{7,6},{8,9},{9,8},{10,11... | collective-permute-start | bytes 1544 | tf_op jit(solution)/shard_map/ppermute | solution.py:130
  131.9 11.8 %collective-permute-start.11 = (bf16[1,32,32,128]{3,1,2,0:T(8,128)(2,1)S(1)}, bf16[1,32,32,128]{3,1,2,0:T(8,128)(2,1)S(1)}, u32[]{:S(2)}, u32[]{:S(2)}) collective-permute-start(bf16[1,32,32,128]{3,1,2,0:T(8,128)(2,1)S(1)} %slice.229), channel_id=1, source_target_pairs={{0,4},{2,6},{4,0},{6,2},{8,12},{10,14},{12,8},{14,10},{1,5},{3,7},... | collective-permute-start | bytes 786440 | tf_op jit(solution)/shard_map/ppermute | solution.py:114
  132.2 11.6 %collective-permute-start.9 = (bf16[1,32,32,128]{3,1,2,0:T(8,128)(2,1)S(1)}, bf16[1,32,32,128]{3,1,2,0:T(8,128)(2,1)S(1)}, u32[]{:S(2)}, u32[]{:S(2)}) collective-permute-start(bf16[1,32,32,128]{3,1,2,0:T(8,128)(2,1)S(1)} %fusion.29), channel_id=1, source_target_pairs={{0,8},{2,10},{4,12},{6,14},{8,0},{10,2},{12,4},{14,6},{1,9},{3,11}... | collective-permute-start | bytes 786440 | tf_op jit(solution)/shard_map/ppermute | solution.py:114
Sparse Core Ops, SparseCore 0:
  9.0 25.3 all-gather.1

commit v10 on v8

--- a/solution.py
+++ b/solution.py
@@ -79,12 +79,7 @@
         preferred_element_type=jnp.float32,
     ).reshape(dp_count, student_blocks, tokens_all, block_size)
 
-    student_logits = jnp.dot(student_all, student_head, preferred_element_type=jnp.float32)
-    student_local_peak = jnp.max(student_logits, axis=1)
-    student_local_total = jnp.sum(jnp.exp(student_logits - student_local_peak[:, None]), axis=1)
-
     peak, mass = teacher_local_peak, mapped_mass
-    s_peak, s_total = student_local_peak, student_local_total
 
     def merge(stats, other):
         new_peak = jnp.maximum(stats[0], other[0])
@@ -92,12 +87,10 @@
         return jnp.stack([new_peak, stats[1] * own + other[1] * far]), own, far
 
     teacher_stats = jnp.stack([peak, mass])
-    student_stats = jnp.stack([s_peak, s_total])
     stage = 1
     while stage < dp_count:
         pairs = [(j, j ^ stage) for j in range(dp_count)]
         teacher_stats = merge(teacher_stats, lax.ppermute(teacher_stats, "dp", pairs))[0]
-        student_stats = merge(student_stats, lax.ppermute(student_stats, "dp", pairs))[0]
         stage *= 2
     column_peak = teacher_stats[0]
     held = held * jnp.exp(teacher_local_peak - column_peak)[None, None, :, None]
@@ -118,6 +111,16 @@
         return part
 
     held = reduce_bits(held, [0], True)
+    held, student_all = lax.optimization_barrier((held, student_all))
+    student_logits = jnp.dot(student_all, student_head, preferred_element_type=jnp.float32)
+    student_local_peak = jnp.max(student_logits, axis=1)
+    student_local_total = jnp.sum(jnp.exp(student_logits - student_local_peak[:, None]), axis=1)
+    student_stats = jnp.stack([student_local_peak, student_local_total])
+    stage = 1
+    while stage < dp_count:
+        pairs = [(j, j ^ stage) for j in range(dp_count)]
+        student_stats = merge(student_stats, lax.ppermute(student_stats, "dp", pairs))[0]
+        stage *= 2
     bits = list(range(1, dp_count.bit_length() - 1))
     half = tokens_all // 2
     first = reduce_bits(held[:, :, :half], bits, True)

time: 180 us -> 184 us (1.022)
  waiting for transfers between devices: 48.2 us -> 41.6 us
  other arithmetic: 6.91 us -> 11.2 us
  local copies, waits for them, and re-layouts: 6.98 us -> 11.2 us
  starting transfers between devices: 17.9 us -> 21.1 us
    ppermute x5, waiting for transfers between devices: 30.6 us -> 9.41 us  [reduce_bits(): lax.ppermute(send.astype(jnp.bfloat16), 'dp', pairs).astype(jnp.float32)]
    ppermute x3, waiting for transfers between devices: 3.39 us -> 22 us  [on_device(): lax.ppermute(student_stats, 'dp', pairs)]
    ppermute x3, waiting for transfers between devices: 13.2 us -> 3.59 us  [on_device(): lax.ppermute(teacher_stats, 'dp', pairs)]
    all_to_all x1, waiting for transfers between devices: 0.01 us -> 5.58 us  [on_device(): lax.all_to_all(jnp.broadcast_to(student_hidden[None], (dp_count,) + stude...]
    add x4, other arithmetic: 3.22 us -> 7.66 us  [reduce_bits(): keep + lax.ppermute(send.astype(jnp.bfloat16), 'dp', pairs).astype(jnp.fl...]
    slice x0 -> x2, local copies, waits for them, and re-layouts: none -> 3.14 us  [reduce_bits(): keep, send = (split[:, 0], split[:, 1])]
    ppermute x3, starting transfers between devices: 0.21 us -> 2.26 us  [on_device(): lax.ppermute(student_stats, 'dp', pairs)]
    convert_element_type x3 -> x2, local copies, waits for them, and re-layouts: 2.01 us -> 0.13 us  [reduce_bits(): send.astype(jnp.bfloat16)]
  transfers between devices with their start and end apart: 14 -> 14, of which waited for: 7 -> 8; matrix products, arithmetic and copies ran while one was open for 13% -> 8% of each run, Pallas kernels for 0% -> 0%
where the time goes in v10:
time: 184 us; the launch traced here: 183 us
  matrix products  59.4 us (32%)
  waiting for transfers between devices  41.6 us (23%)
  blocking collectives  38.4 us (21%)
  starting transfers between devices  21.1 us (11%)
  other arithmetic  11.2 us (6%)
  local copies, waits for them, and re-layouts  11.2 us (6%)
    dot_general x1, matrix products, on_device(): jnp.dot(teacher_all, teacher_head, preferred_element_type=jnp.float32)  23.4 us
    ppermute x3, waiting for transfers between devices, on_device(): lax.ppermute(student_stats, 'dp', pairs)  22 us
    all_to_all x1, blocking collectives, on_device(): lax.all_to_all(partial, ('dp', 'vocab'), split_axis=0, concat_axis=0, til...  21.6 us
    all_gather x1, blocking collectives, on_device(): gathered = lax.all_gather(packed, 'dp', axis=0, tiled=True)  16.8 us
    dot_general x1, matrix products, on_device(): lax.dot_general(logit_grad, student_head, (((1,), (1,)), ((), ())), prefe...  15.8 us
    dot_general x1, matrix products, on_device(): jnp.dot(student_all, student_head, preferred_element_type=jnp.float32)  13.7 us
    ppermute x5, waiting for transfers between devices, reduce_bits(): lax.ppermute(send.astype(jnp.bfloat16), 'dp', pairs).astype(jnp.float32)  9.41 us
    ppermute x5, starting transfers between devices, reduce_bits(): lax.ppermute(send.astype(jnp.bfloat16), 'dp', pairs).astype(jnp.float32)  8.02 us
  transfers between devices with their start and end apart: 14, of which 8 were waited for; matrix products, arithmetic and copies ran while one was open for 8% of the time, Pallas kernels for 0%

profile of v10, /device:TPU:1, one launch (start us, length us, event | category | flops | bytes accessed | tf_op | source)
XLA Modules:
  0.0 183.3 jit_solution(1490640882447708258)
XLA Ops:
  0.0 0.7 convert_convert_fusion
  0.7 0.1 fusion.36
  0.7 0.9 pad_maximum_fusion
  1.6 16.8 %all_gather.3 = bf16[64,5248]{1,0:T(8,128)(2,1)S(1)} all-gather(bf16[8,5248]{1,0:T(8,128)(2,1)S(1)} %pad_maximum_fusion), channel_id=1, replica_groups=mesh['groups'=2,'dp'=8,'vocab'=2] {'dp'}, dimensions={0}, use_global_device_ids=true | all-gather | bytes 755712 | tf_op jit(solution)/shard_map/all_gather | solution.py:50
  18.5 23.4 %fusion.67 = (f32[64]{0:T(128)S(1)}, f32[64,6144]{1,0:T(8,128)S(1)}) fusion(bf16[5120,6144]{1,0:T(8,128)(2,1)} %param.9, bf16[64,5248]{1,0:T(8,128)(2,1)S(1)} %all_gather.3), kind=kOutput, calls=%fused_computation.142 | convolution fusion | flops 4026925056 | bytes 65143040 | tf_op jit(solution)/shard_map/dot_general | solution.py:62
  41.9 0.3 fusion.12
  42.2 0.1 copy.27
  42.3 0.0 copy-start.3
  42.3 0.0 copy-start.4
  42.3 4.0 %convert_reduce_fusion = (f32[64]{0:T(128)S(1)}, bf16[48,64,4,128]{3,1,2,0:T(8,128)(2,1)S(1)}) fusion(bf16[48,4,128,128]{3,2,1,0:T(8,128)(2,1)} %param.12, bf16[64,48,128,1]{2,1,0,3:T(8,128)(2,1)S(1)} %bitcast.246), kind=kOutput, calls=%fused_computation | convolution fusion | flops 407371712 | bytes 10223872 | tf_op jit(solution)/shard_map/gkc,krcd->krgd/dot_general | solution.py:66
  46.3 0.2 collective-permute-start
  46.5 1.0 collective-permute-done
  47.5 1.3 collective-permute-start.1
  48.8 1.2 collective-permute-done.1
  50.0 2.0 %collective-permute-start.2 = (f32[2,64]{1,0:T(2,128)S(1)}, f32[2,64]{1,0:T(2,128)S(1)}, u32[]{:S(2)}, u32[]{:S(2)}) collective-permute-start(f32[2,64]{1,0:T(2,128)S(1)} %pad_maximum_fusion.3), channel_id=1, source_target_pairs={{0,8},{2,10},{4,12},{6,14},{8,0},{10,2},{12,4},{14,6},{1,9},{3,11}... | collective-permute-start | bytes 1544 | tf_op jit(solution)/shard_map/ppermute | solution.py:93
  52.1 1.4 collective-permute-done.2
  53.5 1.3 collective-permute-start.12
  54.7 0.1 copy.11
  54.8 0.1 add.135
  54.9 1.0 collective-permute-done.12
  56.0 2.5 %broadcast_multiply_fusion = f32[8,32,64,128]{3,1,2,0:T(8,128)S(1)} fusion(f32[64]{0:T(128)S(1)} %get-tuple-element.26, s32[192]{0:T(256)S(1)} %add.135, s32[8,32]{1,0:T(8,128)S(1)} %multiply_add_fusion, bf16[24,8,64,128]{3,2,1,0:T(8,128)(2,1)S(1)} %bitcast.243), kind=kOutput, calls=%fused_computation.5 | convolution fusion | flops 807452672 | bytes 11536384 | tf_op jit(solution)/shard_map/dot_general | solution.py:76
  58.5 0.0 copy-start.2
  58.5 0.0 slice-start
  58.6 0.5 slice.146
  59.1 2.6 %copy.50 = bf16[4,1,32,64,128]{4,3,2,0,1:T(8,128)(2,1)} copy(bf16[4,1,32,64,128]{4,2,3,1,0:T(8,128)(2,1)S(1)} %slice.146) | data formatting | bytes 4194304
  61.7 0.7 copy-done
  62.4 3.6 %collective-permute-start.3 = (bf16[4,32,64,128]{3,2,1,0:T(8,128)(2,1)}, bf16[4,32,64,128]{3,2,1,0:T(8,128)(2,1)}, u32[]{:S(2)}, u32[]{:S(2)}) collective-permute-start(bf16[4,32,64,128]{3,2,1,0:T(8,128)(2,1)} %bitcast.240), channel_id=1, source_target_pairs={{0,2},{2,0},{4,6},{6,4},{8,10},{10,8},{12,14},{14,12},{1,3},{3,1},... | collective-permute-start | bytes 6291464 | tf_op jit(solution)/shard_map/ppermute | solution.py:108
  66.0 0.8 broadcast_in_dim.2
  66.8 4.8 %all-to-all-start = ((bf16[8,8,4096]{2,1,0:T(8,128)(2,1)}), bf16[8,8,4096]{2,1,0:T(8,128)(2,1)S(1)}, u32[]{:S(2)}, u32[]{:S(2)}) async-start(bf16[8,8,4096]{2,1,0:T(8,128)(2,1)} %broadcast_in_dim.2), calls=%async_computation | async-start | bytes 1048576 | tf_op jit(solution)/shard_map/all_to_all | solution.py:51
  71.6 2.6 %slice.145 = f32[4,1,32,64,128]{4,2,3,1,0:T(8,128)S(1)} slice(f32[4,2,32,64,128]{4,2,3,1,0:T(8,128)} %bitcast.242), slice={[0:4], [0:1], [0:32], [0:64], [0:128]} | slice | bytes 8388608 | tf_op jit(solution)/shard_map/slice | solution.py:104
  74.3 0.0 collective-permute-done.3
  74.3 6.1 %fusion = f32[4,32,64,128]{3,2,1,0:T(8,128)} fusion(f32[4,1,32,64,128]{4,2,3,1,0:T(8,128)S(1)} %slice.145, bf16[4,32,64,128]{3,2,1,0:T(8,128)(2,1)} %collective-permute-done.3), kind=kLoop, calls=%fused_computation.4 | loop fusion | flops 2097152 | bytes 10485760 | tf_op jit(solution)/shard_map/add | solution.py:108
  80.4 5.6 %all-to-all-done = bf16[8,8,4096]{2,1,0:T(8,128)(2,1)S(1)} async-done(((bf16[8,8,4096]{2,1,0:T(8,128)(2,1)}), bf16[8,8,4096]{2,1,0:T(8,128)(2,1)S(1)}, u32[]{:S(2)}, u32[]{:S(2)}) %all-to-all-start) | async-done | bytes 524320 | tf_op jit(solution)/shard_map/all_to_all | solution.py:51
  86.0 13.7 %fusion.68 = (f32[64]{0:T(128)S(1)}, f32[64,4096]{1,0:T(8,128)S(1)}) fusion(bf16[64,4096]{1,0:T(8,128)(2,1)S(1)} %bitcast.247, bf16[4096,4096]{1,0:T(8,128)(2,1)} %param.14), kind=kOutput, calls=%fused_computation.143 | convolution fusion | flops 2147745792 | bytes 35127552 | tf_op jit(solution)/shard_map/dot_general | solution.py:115
  99.7 0.3 exponential_reduce_fusion
  100.0 1.0 collective-permute-start.4
  101.1 0.1 convert_add_fusion.1
  101.1 0.7 collective-permute-done.4
  101.9 0.1 collective-permute-start.5
  102.0 0.1 eq.47
  102.1 1.3 slice.227
  103.4 1.8 slice.129
  105.3 1.3 collective-permute-start.10
  106.6 0.0 collective-permute-done.5
  106.6 1.2 collective-permute-start.6
  107.8 0.1 fusion.17
  107.9 1.5 collective-permute-start.8
  109.4 21.3 %collective-permute-done.6 = f32[2,64]{1,0:T(2,128)S(1)} collective-permute-done((f32[2,64]{1,0:T(2,128)S(1)}, f32[2,64]{1,0:T(2,128)S(1)}, u32[]{:S(2)}, u32[]{:S(2)}) %collective-permute-start.6) | collective-permute-done | bytes 544 | tf_op jit(solution)/shard_map/ppermute | solution.py:122
  130.7 1.3 collective-permute-start.7
  132.0 0.0 collective-permute-done.10
  132.0 1.4 convert_add_fusion
  133.4 0.1 collective-permute-start.11
  133.5 0.0 collective-permute-done.8
  133.5 0.2 fusion.8
  133.8 1.5 collective-permute-start.9
  135.3 0.0 collective-permute-done.7
  135.3 9.4 %collective-permute-done.11 = bf16[1,32,32,128]{3,2,1,0:T(8,128)(2,1)S(1)} collective-permute-done((bf16[1,32,32,128]{3,2,1,0:T(8,128)(2,1)S(1)}, bf16[1,32,32,128]{3,2,1,0:T(8,128)(2,1)S(1)}, u32[]{:S(2)}, u32[]{:S(2)}) %collective-permute-start.11) | collective-permute-done | bytes 262176 | tf_op jit(solution)/shard_map/ppermute | solution.py:108
  144.7 0.1 slice_add_fusion
  144.8 0.0 collective-permute-done.9
  144.8 0.1 fusion.18
  144.8 15.8 %convolution_convert_fusion = bf16[64,4096]{1,0:T(8,128)(2,1)S(1)} fusion(bf16[4096,4096]{1,0:T(8,128)(2,1)} %param.14, f32[64,4096]{1,0:T(8,128)S(1)} %get-tuple-element.34, s32[4096]{0:T(1024)S(1)} %iota_add_fusion, f32[64]{0:T(128)S(1)} %get-tuple-element.15, f32[64]{0:T(128)S(1)} %get-tuple-element.9, f32[64]{0:T(128)S(1)} %get-tuple-element.10, ...), kind=kOutput, calls=%fused_computation.1 | convolution fusion | flops 2150891520 | bytes 36193536 | tf_op jit(solution)/shard_map/dot_general | solution.py:150
  160.6 0.2 reshape.347
  160.8 21.6 %all_to_all.10 = bf16[16,4,4096]{2,1,0:T(4,128)(2,1)S(1)} all-to-all(bf16[16,4,4096]{2,1,0:T(4,128)(2,1)S(1)} %reshape.347), channel_id=1, replica_groups=mesh['groups'=2,'dp'=8,'vocab'=2] {'dp','vocab'}, dimensions={0} | all-to-all | bytes 1048576 | tf_op jit(solution)/shard_map/all_to_all | solution.py:155
  182.4 0.8 reduce_sum.32
  (30 shorter events, 0.3 us)
Async XLA Ops:
  18.5 23.4 %copy-start.1 = (bf16[64,5248]{1,0:T(8,128)(2,1)}, bf16[64,5248]{1,0:T(8,128)(2,1)S(1)}, u32[]{:S(2)}) copy-start(bf16[64,5248]{1,0:T(8,128)(2,1)S(1)} %all_gather.3) | copy-start | bytes 2015236
  42.3 9.8 %copy-start.3 = (s32[48,4]{0,1:T(4,128)S(1)}, s32[48,4]{0,1:T(4,128)}, u32[]{:S(2)}) copy-start(s32[48,4]{0,1:T(4,128)} %param.11) | copy-start | bytes 2308
  42.3 9.8 %copy-start.4 = (s32[48,4]{0,1:T(4,128)S(1)}, s32[48,4]{0,1:T(4,128)}, u32[]{:S(2)}) copy-start(s32[48,4]{0,1:T(4,128)} %param.10) | copy-start | bytes 2308
  46.3 1.2 collective-permute-start
  47.5 2.5 %collective-permute-start.1 = (f32[2,64]{1,0:T(2,128)S(1)}, f32[2,64]{1,0:T(2,128)S(1)}, u32[]{:S(2)}, u32[]{:S(2)}) collective-permute-start(f32[2,64]{1,0:T(2,128)S(1)} %pad_maximum_fusion.2), channel_id=1, source_target_pairs={{0,4},{2,6},{4,0},{6,2},{8,12},{10,14},{12,8},{14,10},{1,5},{3,7},... | collective-permute-start | bytes 1544 | tf_op jit(solution)/shard_map/ppermute | solution.py:93
  50.0 3.4 %collective-permute-start.2 = (f32[2,64]{1,0:T(2,128)S(1)}, f32[2,64]{1,0:T(2,128)S(1)}, u32[]{:S(2)}, u32[]{:S(2)}) collective-permute-start(f32[2,64]{1,0:T(2,128)S(1)} %pad_maximum_fusion.3), channel_id=1, source_target_pairs={{0,8},{2,10},{4,12},{6,14},{8,0},{10,2},{12,4},{14,6},{1,9},{3,11}... | collective-permute-start | bytes 1544 | tf_op jit(solution)/shard_map/ppermute | solution.py:93
  53.5 2.5 %collective-permute-start.12 = (f32[2,64]{1,0:T(2,128)S(1)}, f32[2,64]{1,0:T(2,128)S(1)}, u32[]{:S(2)}, u32[]{:S(2)}) collective-permute-start(f32[2,64]{1,0:T(2,128)S(1)} %pad_maximum_fusion.8), channel_id=1, source_target_pairs={{0,1},{1,0},{2,3},{3,2},{4,5},{5,4},{6,7},{7,6},{8,9},{9,8},{10,11... | collective-permute-start | bytes 1544 | tf_op jit(solution)/shard_map/ppermute | solution.py:133
  58.5 3.9 %copy-start = (f32[8,32,64,128]{3,1,2,0:T(8,128)}, f32[8,32,64,128]{3,1,2,0:T(8,128)S(1)}, u32[]{:S(2)}) copy-start(f32[8,32,64,128]{3,1,2,0:T(8,128)S(1)} %broadcast_multiply_fusion) | copy-start | bytes 25165828
  58.5 7.5 %copy-start.2 = (bf16[8,4096]{1,0:T(8,128)(2,1)S(1)}, bf16[8,4096]{1,0:T(8,128)(2,1)}, u32[]{:S(2)}) copy-start(bf16[8,4096]{1,0:T(8,128)(2,1)} %param.13) | copy-start | bytes 196612
  58.5 13.1 %slice-start = ((bf16[64,5248]{1,0:T(8,128)(2,1)}), bf16[64,128]{1,0:T(8,128)(2,1)S(1)}, s32[]{:S(2)}) async-start(bf16[64,5248]{1,0:T(8,128)(2,1)} %copy-done.1), calls=%async_computation.2 | async-start | bytes 32768 | tf_op jit(solution)/shard_map/slice | solution.py:57
  62.4 11.9 %collective-permute-start.3 = (bf16[4,32,64,128]{3,2,1,0:T(8,128)(2,1)}, bf16[4,32,64,128]{3,2,1,0:T(8,128)(2,1)}, u32[]{:S(2)}, u32[]{:S(2)}) collective-permute-start(bf16[4,32,64,128]{3,2,1,0:T(8,128)(2,1)} %bitcast.240), channel_id=1, source_target_pairs={{0,2},{2,0},{4,6},{6,4},{8,10},{10,8},{12,14},{14,12},{1,3},{3,1},... | collective-permute-start | bytes 6291464 | tf_op jit(solution)/shard_map/ppermute | solution.py:108
  66.8 19.1 %all-to-all-start = ((bf16[8,8,4096]{2,1,0:T(8,128)(2,1)}), bf16[8,8,4096]{2,1,0:T(8,128)(2,1)S(1)}, u32[]{:S(2)}, u32[]{:S(2)}) async-start(bf16[8,8,4096]{2,1,0:T(8,128)(2,1)} %broadcast_in_dim.2), calls=%async_computation | async-start | bytes 1048576 | tf_op jit(solution)/shard_map/all_to_all | solution.py:51
  100.0 1.9 %collective-permute-start.4 = (f32[2,64]{1,0:T(2,128)S(1)}, f32[2,64]{1,0:T(2,128)S(1)}, u32[]{:S(2)}, u32[]{:S(2)}) collective-permute-start(f32[2,64]{1,0:T(2,128)S(1)} %pad_maximum_fusion.4), channel_id=1, source_target_pairs={{0,2},{2,0},{4,6},{6,4},{8,10},{10,8},{12,14},{14,12},{1,3},{3,1},... | collective-permute-start | bytes 1544 | tf_op jit(solution)/shard_map/ppermute | solution.py:122
  101.9 4.7 %collective-permute-start.5 = (f32[2,64]{1,0:T(2,128)S(1)}, f32[2,64]{1,0:T(2,128)S(1)}, u32[]{:S(2)}, u32[]{:S(2)}) collective-permute-start(f32[2,64]{1,0:T(2,128)S(1)} %pad_maximum_fusion.5), channel_id=1, source_target_pairs={{0,4},{2,6},{4,0},{6,2},{8,12},{10,14},{12,8},{14,10},{1,5},{3,7},... | collective-permute-start | bytes 1544 | tf_op jit(solution)/shard_map/ppermute | solution.py:122
  105.3 26.7 %collective-permute-start.10 = (bf16[2,32,32,128]{3,2,1,0:T(8,128)(2,1)S(1)}, bf16[2,32,32,128]{3,2,1,0:T(8,128)(2,1)S(1)}, u32[]{:S(2)}, u32[]{:S(2)}) collective-permute-start(bf16[2,32,32,128]{3,2,1,0:T(8,128)(2,1)S(1)} %slice.227), channel_id=1, source_target_pairs={{0,8},{2,10},{4,12},{6,14},{8,0},{10,2},{12,4},{14,6},{1,9},{3,11}... | collective-permute-start | bytes 1572872 | tf_op jit(solution)/shard_map/ppermute | solution.py:108
  106.6 24.1 %collective-permute-start.6 = (f32[2,64]{1,0:T(2,128)S(1)}, f32[2,64]{1,0:T(2,128)S(1)}, u32[]{:S(2)}, u32[]{:S(2)}) collective-permute-start(f32[2,64]{1,0:T(2,128)S(1)} %pad_maximum_fusion.6), channel_id=1, source_target_pairs={{0,8},{2,10},{4,12},{6,14},{8,0},{10,2},{12,4},{14,6},{1,9},{3,11}... | collective-permute-start | bytes 1544 | tf_op jit(solution)/shard_map/ppermute | solution.py:122
  107.9 25.7 %collective-permute-start.8 = (bf16[2,32,32,128]{3,2,1,0:T(8,128)(2,1)S(1)}, bf16[2,32,32,128]{3,2,1,0:T(8,128)(2,1)S(1)}, u32[]{:S(2)}, u32[]{:S(2)}) collective-permute-start(bf16[2,32,32,128]{3,2,1,0:T(8,128)(2,1)S(1)} %fusion.17), channel_id=1, source_target_pairs={{0,4},{2,6},{4,0},{6,2},{8,12},{10,14},{12,8},{14,10},{1,5},{3,7},... | collective-permute-start | bytes 1572872 | tf_op jit(solution)/shard_map/ppermute | solution.py:108
  130.7 4.6 %collective-permute-start.7 = (f32[2,64]{1,0:T(2,128)S(1)}, f32[2,64]{1,0:T(2,128)S(1)}, u32[]{:S(2)}, u32[]{:S(2)}) collective-permute-start(f32[2,64]{1,0:T(2,128)S(1)} %pad_maximum_fusion.7), channel_id=1, source_target_pairs={{0,1},{1,0},{2,3},{3,2},{4,5},{5,4},{6,7},{7,6},{8,9},{9,8},{10,11... | collective-permute-start | bytes 1544 | tf_op jit(solution)/shard_map/ppermute | solution.py:134
  133.4 11.2 %collective-permute-start.11 = (bf16[1,32,32,128]{3,2,1,0:T(8,128)(2,1)S(1)}, bf16[1,32,32,128]{3,2,1,0:T(8,128)(2,1)S(1)}, u32[]{:S(2)}, u32[]{:S(2)}) collective-permute-start(bf16[1,32,32,128]{3,2,1,0:T(8,128)(2,1)S(1)} %slice.228), channel_id=1, source_target_pairs={{0,4},{2,6},{4,0},{6,2},{8,12},{10,14},{12,8},{14,10},{1,5},{3,7},... | collective-permute-start | bytes 786440 | tf_op jit(solution)/shard_map/ppermute | solution.py:108
  133.8 11.0 %collective-permute-start.9 = (bf16[1,32,32,128]{3,2,1,0:T(8,128)(2,1)S(1)}, bf16[1,32,32,128]{3,2,1,0:T(8,128)(2,1)S(1)}, u32[]{:S(2)}, u32[]{:S(2)}) collective-permute-start(bf16[1,32,32,128]{3,2,1,0:T(8,128)(2,1)S(1)} %fusion.28), channel_id=1, source_target_pairs={{0,8},{2,10},{4,12},{6,14},{8,0},{10,2},{12,4},{14,6},{1,9},{3,11}... | collective-permute-start | bytes 786440 | tf_op jit(solution)/shard_map/ppermute | solution.py:108

commit v11 on v8

--- a/solution.py
+++ b/solution.py
@@ -100,7 +100,7 @@
         student_stats = merge(student_stats, lax.ppermute(student_stats, "dp", pairs))[0]
         stage *= 2
     column_peak = teacher_stats[0]
-    held = held * jnp.exp(teacher_local_peak - column_peak)[None, None, :, None]
+    to_column = jnp.exp(teacher_local_peak - column_peak)[None, None, :, None]
 
     def reduce_bits(part, bits, low_first):
         for bit in bits:
@@ -117,7 +117,11 @@
             )
         return part
 
-    held = reduce_bits(held, [0], True)
+    pair = held.reshape((held.shape[0] // 2, 2) + held.shape[1:])
+    arrived = lax.ppermute(
+        (pair[:, 1] * to_column).astype(jnp.bfloat16), "dp", [(j, j ^ 1) for j in range(dp_count)]
+    )
+    held = pair[:, 0] * to_column + arrived.astype(jnp.float32)
     bits = list(range(1, dp_count.bit_length() - 1))
     half = tokens_all // 2
     first = reduce_bits(held[:, :, :half], bits, True)

time: 180 us -> 180 us (level)
  waiting for transfers between devices: 48.2 us -> 43.8 us
  matrix products: 60.1 us -> 63.5 us
  other arithmetic: 6.91 us -> 9.95 us
    ppermute x3, waiting for transfers between devices: 13.2 us -> 7.61 us  [on_device(): lax.ppermute(teacher_stats, 'dp', pairs)]
    add x0 -> x1, other arithmetic: none -> 3.34 us  [on_device(): held = pair[:, 0] * to_column + arrived.astype(jnp.float32)]
    ppermute x5 -> x4, starting transfers between devices: 6.77 us -> 3.61 us  [reduce_bits(): lax.ppermute(send.astype(jnp.bfloat16), 'dp', pairs).astype(jnp.float32)]
    dot_general x1, matrix products: 2.53 us -> 5.69 us  [on_device(): jnp.dot(placement, mapped_terms.reshape(item_count, tokens_all * block_si...]
    add x4 -> x3, other arithmetic: 3.22 us -> 0.32 us  [reduce_bits(): keep + lax.ppermute(send.astype(jnp.bfloat16), 'dp', pairs).astype(jnp.fl...]
    convert_element_type x0 -> x1, other arithmetic: none -> 2.6 us  [on_device(): (pair[:, 1] * to_column).astype(jnp.bfloat16)]
    ppermute x5 -> x4, waiting for transfers between devices: 30.6 us -> 32.8 us  [reduce_bits(): lax.ppermute(send.astype(jnp.bfloat16), 'dp', pairs).astype(jnp.float32)]
    convert_element_type x3 -> x2, local copies, waits for them, and re-layouts: 2.01 us -> 0.13 us  [reduce_bits(): send.astype(jnp.bfloat16)]
  transfers between devices with their start and end apart: 14 -> 14, of which waited for: 7 -> 5; matrix products, arithmetic and copies ran while one was open for 13% -> 18% of each run, Pallas kernels for 0% -> 0%
where the time goes in v11:
time: 180 us; the launch traced here: 179 us
  matrix products  63.5 us (35%)
  waiting for transfers between devices  43.8 us (24%)
  blocking collectives  38.3 us (21%)
  starting transfers between devices  17.8 us (10%)
  other arithmetic  9.95 us (6%)
  local copies, waits for them, and re-layouts  5.6 us (3%)
    ppermute x4, waiting for transfers between devices, reduce_bits(): lax.ppermute(send.astype(jnp.bfloat16), 'dp', pairs).astype(jnp.float32)  32.8 us
    dot_general x1, matrix products, on_device(): jnp.dot(teacher_all, teacher_head, preferred_element_type=jnp.float32)  23.4 us
    all_to_all x1, blocking collectives, on_device(): lax.all_to_all(partial, ('dp', 'vocab'), split_axis=0, concat_axis=0, til...  21.5 us
    all_gather x1, blocking collectives, on_device(): gathered = lax.all_gather(packed, 'dp', axis=0, tiled=True)  16.8 us
    dot_general x1, matrix products, on_device(): lax.dot_general(logit_grad, student_head, (((1,), (1,)), ((), ())), prefe...  16.6 us
    dot_general x1, matrix products, on_device(): jnp.dot(student_all, student_head, preferred_element_type=jnp.float32)  13.8 us
    ppermute x3, waiting for transfers between devices, on_device(): lax.ppermute(teacher_stats, 'dp', pairs)  7.61 us
    dot_general x1, matrix products, on_device(): jnp.dot(placement, mapped_terms.reshape(item_count, tokens_all * block_si...  5.69 us
  transfers between devices with their start and end apart: 14, of which 5 were waited for; matrix products, arithmetic and copies ran while one was open for 18% of the time, Pallas kernels for 0%

profile of v11, /device:TPU:1, one launch (start us, length us, event | category | flops | bytes accessed | tf_op | source)
XLA Modules:
  0.0 179.3 jit_solution(302252906935269404)
XLA Ops:
  0.0 0.7 convert_convert_fusion
  0.7 0.1 fusion.40
  0.7 0.9 pad_maximum_fusion
  1.6 16.8 %all_gather.3 = bf16[64,5248]{1,0:T(8,128)(2,1)S(1)} all-gather(bf16[8,5248]{1,0:T(8,128)(2,1)S(1)} %pad_maximum_fusion), channel_id=1, replica_groups=mesh['groups'=2,'dp'=8,'vocab'=2] {'dp'}, dimensions={0}, use_global_device_ids=true | all-gather | bytes 755712 | tf_op jit(solution)/shard_map/all_gather | solution.py:50
  18.5 23.4 %fusion.71 = (f32[64]{0:T(128)S(1)}, f32[64,6144]{1,0:T(8,128)S(1)}) fusion(bf16[5120,6144]{1,0:T(8,128)(2,1)} %param.9, bf16[64,5248]{1,0:T(8,128)(2,1)S(1)} %all_gather.3), kind=kOutput, calls=%fused_computation.144 | convolution fusion | flops 4026925056 | bytes 65143040 | tf_op jit(solution)/shard_map/dot_general | solution.py:62
  41.9 0.3 fusion.14
  42.2 0.1 copy.30
  42.3 0.0 copy-start.1
  42.3 0.0 copy-start.2
  42.3 0.0 copy-start.3
  42.3 4.0 %convert_reduce_fusion = (f32[64]{0:T(128)S(1)}, bf16[48,64,4,128]{3,1,2,0:T(8,128)(2,1)S(1)}) fusion(bf16[48,4,128,128]{3,2,1,0:T(8,128)(2,1)} %param.12, bf16[64,48,128,1]{2,1,0,3:T(8,128)(2,1)S(1)} %bitcast.245), kind=kOutput, calls=%fused_computation | convolution fusion | flops 407371712 | bytes 10223872 | tf_op jit(solution)/shard_map/gkc,krcd->krgd/dot_general | solution.py:66
  46.3 0.2 collective-permute-start.4
  46.5 0.8 broadcast_in_dim.2
  47.4 5.0 %all-to-all-start = ((bf16[8,8,4096]{2,1,0:T(8,128)(2,1)}), bf16[8,8,4096]{2,1,0:T(8,128)(2,1)}, u32[]{:S(2)}, u32[]{:S(2)}) async-start(bf16[8,8,4096]{2,1,0:T(8,128)(2,1)} %broadcast_in_dim.2), calls=%async_computation | async-start | bytes 1048576 | tf_op jit(solution)/shard_map/all_to_all | solution.py:51
  52.4 0.0 collective-permute-done.4
  52.4 1.4 collective-permute-start.5
  53.8 0.0 copy-done.2
  53.8 7.6 %collective-permute-done.5 = f32[2,64]{1,0:T(2,128)S(1)} collective-permute-done((f32[2,64]{1,0:T(2,128)S(1)}, f32[2,64]{1,0:T(2,128)S(1)}, u32[]{:S(2)}, u32[]{:S(2)}) %collective-permute-start.5) | collective-permute-done | bytes 544 | tf_op jit(solution)/shard_map/ppermute | solution.py:99
  61.5 4.0 %collective-permute-start.6 = (f32[2,64]{1,0:T(2,128)S(1)}, f32[2,64]{1,0:T(2,128)S(1)}, u32[]{:S(2)}, u32[]{:S(2)}) collective-permute-start(f32[2,64]{1,0:T(2,128)S(1)} %pad_maximum_fusion.7), channel_id=1, source_target_pairs={{0,8},{2,10},{4,12},{6,14},{8,0},{10,2},{12,4},{14,6},{1,9},{3,11}... | collective-permute-start | bytes 1544 | tf_op jit(solution)/shard_map/ppermute | solution.py:99
  65.4 2.8 %copy.53 = bf16[24,8,64,128]{3,1,2,0:T(8,128)(2,1)S(1)} copy(bf16[24,8,64,128]{3,2,1,0:T(8,128)(2,1)S(1)} %bitcast.240) | data formatting | bytes 6291456
  68.3 0.9 copy.32
  69.2 0.1 copy.11
  69.2 0.1 add.146
  69.4 0.0 collective-permute-done.6
  69.4 1.3 collective-permute-start.12
  70.7 5.7 %fusion.4 = f32[4,2,32,64,128]{4,2,3,1,0:T(8,128)} fusion(bf16[64,128,192,1,1]{1,0,2,4,3:T(8,128)(2,1)S(1)} %bitcast.241, s32[192]{0:T(256)S(1)} %add.146, s32[4,2,32]{2,1,0:T(2,128)S(1)} %multiply_add_fusion), kind=kOutput, calls=%fused_computation.9 | convolution fusion | flops 805355520 | bytes 11536128 | tf_op jit(solution)/shard_map/dot_general | solution.py:76
  76.4 0.0 collective-permute-done.12
  76.4 2.6 %fusion.1 = bf16[4,32,64,128]{3,1,2,0:T(8,128)(2,1)S(1)} fusion(f32[4,2,32,64,128]{4,2,3,1,0:T(8,128)} %fusion.4, f32[64]{0:T(128)S(1)} %get-tuple-element.22), kind=kLoop, calls=%fused_computation.4 | loop fusion | flops 2097152 | bytes 6291712 | tf_op jit(solution)/shard_map/convert_element_type | solution.py:122
  79.0 1.5 collective-permute-start.7
  80.5 0.0 all-to-all-done
  80.5 13.8 %fusion.72 = (f32[64]{0:T(128)S(1)}, f32[64,4096]{1,0:T(8,128)S(1)}) fusion(bf16[4096,4096]{1,0:T(8,128)(2,1)} %param.14, bf16[8,8,4096]{2,1,0:T(8,128)(2,1)} %all-to-all-done), kind=kOutput, calls=%fused_computation.145 | convolution fusion | flops 2147745792 | bytes 35127552 | tf_op jit(solution)/shard_map/dot_general | solution.py:82
  94.4 0.3 exponential_reduce_fusion
  94.7 0.1 collective-permute-start
  94.8 0.1 convert_add_fusion
  94.9 1.1 collective-permute-done
  96.0 0.1 collective-permute-start.1
  96.1 0.1 eq.56
  96.2 2.3 %collective-permute-done.1 = f32[2,64]{1,0:T(2,128)S(1)} collective-permute-done((f32[2,64]{1,0:T(2,128)S(1)}, f32[2,64]{1,0:T(2,128)S(1)}, u32[]{:S(2)}, u32[]{:S(2)}) %collective-permute-start.1) | collective-permute-done | bytes 544 | tf_op jit(solution)/shard_map/ppermute | solution.py:100
  98.5 0.3 collective-permute-start.2
  98.8 0.0 collective-permute-done.7
  98.8 3.3 %fusion.3 = f32[4,32,64,128]{3,1,2,0:T(8,128)S(1)} fusion(f32[4,2,32,64,128]{4,2,3,1,0:T(8,128)} %fusion.4, bf16[4,32,64,128]{3,1,2,0:T(8,128)(2,1)} %collective-permute-done.7, f32[64]{0:T(128)S(1)} %get-tuple-element.22), kind=kLoop, calls=%fused_computation.7 | loop fusion | flops 3145728 | bytes 10486016 | tf_op jit(solution)/shard_map/add | solution.py:124
  102.2 0.1 slice.230
  102.3 0.2 slice.146
  102.4 2.2 %collective-permute-start.10 = (bf16[2,32,32,128]{3,1,2,0:T(8,128)(2,1)S(1)}, bf16[2,32,32,128]{3,1,2,0:T(8,128)(2,1)S(1)}, u32[]{:S(2)}, u32[]{:S(2)}) collective-permute-start(bf16[2,32,32,128]{3,1,2,0:T(8,128)(2,1)S(1)} %slice.230), channel_id=1, source_target_pairs={{0,8},{2,10},{4,12},{6,14},{8,0},{10,2},{12,4},{14,6},{1,9},{3,11}... | collective-permute-start | bytes 1572872 | tf_op jit(solution)/shard_map/ppermute | solution.py:115
  104.6 0.1 fusion.19
  104.7 0.1 collective-permute-start.8
  104.8 0.0 collective-permute-done.2
  104.9 0.3 collective-permute-start.3
  105.2 23.1 %collective-permute-done.10 = bf16[2,32,32,128]{3,1,2,0:T(8,128)(2,1)S(1)} collective-permute-done((bf16[2,32,32,128]{3,1,2,0:T(8,128)(2,1)S(1)}, bf16[2,32,32,128]{3,1,2,0:T(8,128)(2,1)S(1)}, u32[]{:S(2)}, u32[]{:S(2)}) %collective-permute-start.10) | collective-permute-done | bytes 524320 | tf_op jit(solution)/shard_map/ppermute | solution.py:115
  128.3 0.2 slice_add_fusion
  128.5 0.1 collective-permute-start.11
  128.6 0.0 collective-permute-done.8
  128.6 0.2 fusion.11
  128.9 1.3 collective-permute-start.9
  130.1 0.0 collective-permute-done.3
  130.1 9.7 %collective-permute-done.11 = bf16[1,32,32,128]{3,1,2,0:T(8,128)(2,1)S(1)} collective-permute-done((bf16[1,32,32,128]{3,1,2,0:T(8,128)(2,1)S(1)}, bf16[1,32,32,128]{3,1,2,0:T(8,128)(2,1)S(1)}, u32[]{:S(2)}, u32[]{:S(2)}) %collective-permute-start.11) | collective-permute-done | bytes 262176 | tf_op jit(solution)/shard_map/ppermute | solution.py:115
  139.9 0.1 slice_add_fusion.1
  139.9 0.0 collective-permute-done.9
  139.9 0.1 fusion.20
  140.0 0.1 fusion.12
  140.2 16.6 %convolution_convert_fusion = bf16[64,4096]{1,0:T(8,128)(2,1)S(1)} fusion(bf16[4096,4096]{1,0:T(8,128)(2,1)} %param.14, f32[8,8,32,128]{3,2,1,0:T(8,128)S(1)} %bitcast.244, f32[64,4096]{1,0:T(8,128)S(1)} %get-tuple-element.30, s32[4096]{0:T(1024)S(1)} %iota_add_fusion, f32[64]{0:T(128)S(1)} %get-tuple-element.11, f32[64]{0:T(128)S(1)} %get-tuple-element.5, ...), kind=kOutput, calls=%fused_computation.1 | convolution fusion | flops 2150367232 | bytes 36193280 | tf_op jit(solution)/shard_map/dot_general | solution.py:151
  156.8 0.2 reshape.345
  157.0 21.5 %all_to_all.10 = bf16[16,4,4096]{2,1,0:T(4,128)(2,1)S(1)} all-to-all(bf16[16,4,4096]{2,1,0:T(4,128)(2,1)S(1)} %reshape.345), channel_id=1, replica_groups=mesh['groups'=2,'dp'=8,'vocab'=2] {'dp','vocab'}, dimensions={0} | all-to-all | bytes 1048576 | tf_op jit(solution)/shard_map/all_to_all | solution.py:156
  178.5 0.8 reduce_sum.32
  (29 shorter events, 0.3 us)
Async XLA Ops:
  18.5 23.4 %copy-start = (bf16[64,5248]{1,0:T(8,128)(2,1)}, bf16[64,5248]{1,0:T(8,128)(2,1)S(1)}, u32[]{:S(2)}) copy-start(bf16[64,5248]{1,0:T(8,128)(2,1)S(1)} %all_gather.3) | copy-start | bytes 2015236
  42.3 4.3 %copy-start.1 = (bf16[8,4096]{1,0:T(8,128)(2,1)S(1)}, bf16[8,4096]{1,0:T(8,128)(2,1)}, u32[]{:S(2)}) copy-start(bf16[8,4096]{1,0:T(8,128)(2,1)} %param.13) | copy-start | bytes 196612
  42.3 11.5 %copy-start.2 = (s32[48,4]{0,1:T(4,128)S(1)}, s32[48,4]{0,1:T(4,128)}, u32[]{:S(2)}) copy-start(s32[48,4]{0,1:T(4,128)} %param.11) | copy-start | bytes 2308
  42.3 11.5 %copy-start.3 = (s32[48,4]{0,1:T(4,128)S(1)}, s32[48,4]{0,1:T(4,128)}, u32[]{:S(2)}) copy-start(s32[48,4]{0,1:T(4,128)} %param.10) | copy-start | bytes 2308
  46.3 6.1 %collective-permute-start.4 = (f32[2,64]{1,0:T(2,128)S(1)}, f32[2,64]{1,0:T(2,128)S(1)}, u32[]{:S(2)}, u32[]{:S(2)}) collective-permute-start(f32[2,64]{1,0:T(2,128)S(1)} %pad_maximum_fusion.5), channel_id=1, source_target_pairs={{0,2},{2,0},{4,6},{6,4},{8,10},{10,8},{12,14},{14,12},{1,3},{3,1},... | collective-permute-start | bytes 1544 | tf_op jit(solution)/shard_map/ppermute | solution.py:99
  47.4 33.2 %all-to-all-start = ((bf16[8,8,4096]{2,1,0:T(8,128)(2,1)}), bf16[8,8,4096]{2,1,0:T(8,128)(2,1)}, u32[]{:S(2)}, u32[]{:S(2)}) async-start(bf16[8,8,4096]{2,1,0:T(8,128)(2,1)} %broadcast_in_dim.2), calls=%async_computation | async-start | bytes 1048576 | tf_op jit(solution)/shard_map/all_to_all | solution.py:51
  52.4 9.0 %collective-permute-start.5 = (f32[2,64]{1,0:T(2,128)S(1)}, f32[2,64]{1,0:T(2,128)S(1)}, u32[]{:S(2)}, u32[]{:S(2)}) collective-permute-start(f32[2,64]{1,0:T(2,128)S(1)} %pad_maximum_fusion.6), channel_id=1, source_target_pairs={{0,4},{2,6},{4,0},{6,2},{8,12},{10,14},{12,8},{14,10},{1,5},{3,7},... | collective-permute-start | bytes 1544 | tf_op jit(solution)/shard_map/ppermute | solution.py:99
  61.5 7.9 %collective-permute-start.6 = (f32[2,64]{1,0:T(2,128)S(1)}, f32[2,64]{1,0:T(2,128)S(1)}, u32[]{:S(2)}, u32[]{:S(2)}) collective-permute-start(f32[2,64]{1,0:T(2,128)S(1)} %pad_maximum_fusion.7), channel_id=1, source_target_pairs={{0,8},{2,10},{4,12},{6,14},{8,0},{10,2},{12,4},{14,6},{1,9},{3,11}... | collective-permute-start | bytes 1544 | tf_op jit(solution)/shard_map/ppermute | solution.py:99
  69.4 7.0 %collective-permute-start.12 = (f32[2,64]{1,0:T(2,128)S(1)}, f32[2,64]{1,0:T(2,128)S(1)}, u32[]{:S(2)}, u32[]{:S(2)}) collective-permute-start(f32[2,64]{1,0:T(2,128)S(1)} %pad_maximum_fusion.8), channel_id=1, source_target_pairs={{0,1},{1,0},{2,3},{3,2},{4,5},{5,4},{6,7},{7,6},{8,9},{9,8},{10,11... | collective-permute-start | bytes 1544 | tf_op jit(solution)/shard_map/ppermute | solution.py:134
  70.7 5.7 %slice-start = ((bf16[64,5248]{1,0:T(8,128)(2,1)}), bf16[64,128]{1,0:T(8,128)(2,1)S(1)}, s32[]{:S(2)}) async-start(bf16[64,5248]{1,0:T(8,128)(2,1)} %copy-done), calls=%async_computation.2 | async-start | bytes 32768 | tf_op jit(solution)/shard_map/slice | solution.py:57
  79.0 19.8 %collective-permute-start.7 = (bf16[4,32,64,128]{3,1,2,0:T(8,128)(2,1)S(1)}, bf16[4,32,64,128]{3,1,2,0:T(8,128)(2,1)}, u32[]{:S(2)}, u32[]{:S(2)}) collective-permute-start(bf16[4,32,64,128]{3,1,2,0:T(8,128)(2,1)S(1)} %fusion.1), channel_id=1, source_target_pairs={{0,2},{2,0},{4,6},{6,4},{8,10},{10,8},{12,14},{14,12},{1,3},{3,1},... | collective-permute-start | bytes 6291464 | tf_op jit(solution)/shard_map/ppermute | solution.py:121
  94.7 1.2 collective-permute-start
  96.0 2.5 %collective-permute-start.1 = (f32[2,64]{1,0:T(2,128)S(1)}, f32[2,64]{1,0:T(2,128)S(1)}, u32[]{:S(2)}, u32[]{:S(2)}) collective-permute-start(f32[2,64]{1,0:T(2,128)S(1)} %pad_maximum_fusion.2), channel_id=1, source_target_pairs={{0,4},{2,6},{4,0},{6,2},{8,12},{10,14},{12,8},{14,10},{1,5},{3,7},... | collective-permute-start | bytes 1544 | tf_op jit(solution)/shard_map/ppermute | solution.py:100
  98.5 6.3 %collective-permute-start.2 = (f32[2,64]{1,0:T(2,128)S(1)}, f32[2,64]{1,0:T(2,128)S(1)}, u32[]{:S(2)}, u32[]{:S(2)}) collective-permute-start(f32[2,64]{1,0:T(2,128)S(1)} %pad_maximum_fusion.3), channel_id=1, source_target_pairs={{0,8},{2,10},{4,12},{6,14},{8,0},{10,2},{12,4},{14,6},{1,9},{3,11}... | collective-permute-start | bytes 1544 | tf_op jit(solution)/shard_map/ppermute | solution.py:100
  102.4 25.9 %collective-permute-start.10 = (bf16[2,32,32,128]{3,1,2,0:T(8,128)(2,1)S(1)}, bf16[2,32,32,128]{3,1,2,0:T(8,128)(2,1)S(1)}, u32[]{:S(2)}, u32[]{:S(2)}) collective-permute-start(bf16[2,32,32,128]{3,1,2,0:T(8,128)(2,1)S(1)} %slice.230), channel_id=1, source_target_pairs={{0,8},{2,10},{4,12},{6,14},{8,0},{10,2},{12,4},{14,6},{1,9},{3,11}... | collective-permute-start | bytes 1572872 | tf_op jit(solution)/shard_map/ppermute | solution.py:115
  104.7 23.9 %collective-permute-start.8 = (bf16[2,32,32,128]{3,1,2,0:T(8,128)(2,1)S(1)}, bf16[2,32,32,128]{3,1,2,0:T(8,128)(2,1)S(1)}, u32[]{:S(2)}, u32[]{:S(2)}) collective-permute-start(bf16[2,32,32,128]{3,1,2,0:T(8,128)(2,1)S(1)} %fusion.19), channel_id=1, source_target_pairs={{0,4},{2,6},{4,0},{6,2},{8,12},{10,14},{12,8},{14,10},{1,5},{3,7},... | collective-permute-start | bytes 1572872 | tf_op jit(solution)/shard_map/ppermute | solution.py:115
  104.9 25.3 %collective-permute-start.3 = (f32[2,64]{1,0:T(2,128)S(1)}, f32[2,64]{1,0:T(2,128)S(1)}, u32[]{:S(2)}, u32[]{:S(2)}) collective-permute-start(f32[2,64]{1,0:T(2,128)S(1)} %pad_maximum_fusion.4), channel_id=1, source_target_pairs={{0,1},{1,0},{2,3},{3,2},{4,5},{5,4},{6,7},{7,6},{8,9},{9,8},{10,11... | collective-permute-start | bytes 1544 | tf_op jit(solution)/shard_map/ppermute | solution.py:135
  128.5 11.3 %collective-permute-start.11 = (bf16[1,32,32,128]{3,1,2,0:T(8,128)(2,1)S(1)}, bf16[1,32,32,128]{3,1,2,0:T(8,128)(2,1)S(1)}, u32[]{:S(2)}, u32[]{:S(2)}) collective-permute-start(bf16[1,32,32,128]{3,1,2,0:T(8,128)(2,1)S(1)} %slice.231), channel_id=1, source_target_pairs={{0,4},{2,6},{4,0},{6,2},{8,12},{10,14},{12,8},{14,10},{1,5},{3,7},... | collective-permute-start | bytes 786440 | tf_op jit(solution)/shard_map/ppermute | solution.py:115
  128.9 11.1 %collective-permute-start.9 = (bf16[1,32,32,128]{3,1,2,0:T(8,128)(2,1)S(1)}, bf16[1,32,32,128]{3,1,2,0:T(8,128)(2,1)S(1)}, u32[]{:S(2)}, u32[]{:S(2)}) collective-permute-start(bf16[1,32,32,128]{3,1,2,0:T(8,128)(2,1)S(1)} %fusion.32), channel_id=1, source_target_pairs={{0,8},{2,10},{4,12},{6,14},{8,0},{10,2},{12,4},{14,6},{1,9},{3,11}... | collective-permute-start | bytes 786440 | tf_op jit(solution)/shard_map/ppermute | solution.py:115

commit v12 on v11

--- a/solution.py
+++ b/solution.py
@@ -73,9 +73,10 @@
     placement = (
         jnp.arange(dp_count * student_blocks, dtype=jnp.int32)[:, None] == row[None, :]
     ).astype(jnp.bfloat16)
-    held = jnp.dot(
-        placement,
-        mapped_terms.reshape(item_count, tokens_all * block_size),
+    held = jnp.einsum(
+        "xkr,krgd->xgd",
+        placement.reshape(dp_count * student_blocks, teacher_blocks, fan_count),
+        mapped_terms,
         preferred_element_type=jnp.float32,
     ).reshape(dp_count, student_blocks, tokens_all, block_size)
 

time: 180 us -> 185 us (1.028)
  waiting for transfers between devices: 43.8 us -> 50.6 us
  local copies, waits for them, and re-layouts: 5.6 us -> 1.74 us
  other arithmetic: 9.95 us -> 12.7 us
    ppermute x4, waiting for transfers between devices: 32.8 us -> 38.7 us  [reduce_bits(): lax.ppermute(send.astype(jnp.bfloat16), 'dp', pairs).astype(jnp.float32)]
    unnamed x11, local copies, waits for them, and re-layouts: 3.86 us -> 0.14 us
    ppermute x4, starting transfers between devices: 3.61 us -> 0.57 us  [reduce_bits(): lax.ppermute(send.astype(jnp.bfloat16), 'dp', pairs).astype(jnp.float32)]
    ppermute x3, starting transfers between devices: 0.46 us -> 3.43 us  [on_device(): lax.ppermute(student_stats, 'dp', pairs)]
    all_to_all x1, blocking collectives: 21.5 us -> 18.6 us  [on_device(): lax.all_to_all(partial, ('dp', 'vocab'), split_axis=0, concat_axis=0, til...]
    dot_general x1, matrix products: 5.69 us -> 7.73 us  [on_device(): jnp.einsum('xkr,krgd->xgd', placement.reshape(dp_count * student_blocks,...]
  transfers between devices with their start and end apart: 14 -> 14, of which waited for: 5 -> 7; matrix products, arithmetic and copies ran while one was open for 18% -> 17% of each run, Pallas kernels for 0% -> 0%
where the time goes in v12:
time: 185 us
  matrix products  65.2 us (35%)
  waiting for transfers between devices  50.6 us (27%)
  blocking collectives  36.6 us (20%)
  starting transfers between devices  17.6 us (10%)
  other arithmetic  12.7 us (7%)
    ppermute x4, waiting for transfers between devices, reduce_bits(): lax.ppermute(send.astype(jnp.bfloat16), 'dp', pairs).astype(jnp.float32)  38.7 us
    dot_general x1, matrix products, on_device(): jnp.dot(teacher_all, teacher_head, preferred_element_type=jnp.float32)  24.5 us
    all_to_all x1, blocking collectives, on_device(): lax.all_to_all(partial, ('dp', 'vocab'), split_axis=0, concat_axis=0, til...  18.6 us
    all_gather x1, blocking collectives, on_device(): gathered = lax.all_gather(packed, 'dp', axis=0, tiled=True)  18 us
    dot_general x1, matrix products, on_device(): lax.dot_general(logit_grad, student_head, (((1,), (1,)), ((), ())), prefe...  16.4 us
    dot_general x1, matrix products, on_device(): jnp.dot(student_all, student_head, preferred_element_type=jnp.float32)  13.7 us
    ppermute x3, waiting for transfers between devices, on_device(): lax.ppermute(teacher_stats, 'dp', pairs)  9.05 us
    dot_general x1, matrix products, on_device(): jnp.einsum('xkr,krgd->xgd', placement.reshape(dp_count * student_blocks,...  7.73 us
  transfers between devices with their start and end apart: 14, of which 7 were waited for; matrix products, arithmetic and copies ran while one was open for 17% of the time, Pallas kernels for 0%

profile of v12, /device:TPU:1, one launch (start us, length us, event | category | flops | bytes accessed | tf_op | source)
XLA Modules:
  0.0 184.7 jit_solution(7307727664058485924)
XLA Ops:
  0.0 0.7 convert_convert_fusion
  0.7 0.1 fusion.39
  0.7 0.9 pad_maximum_fusion
  1.6 18.0 %all_gather.3 = bf16[64,5248]{1,0:T(8,128)(2,1)} all-gather(bf16[8,5248]{1,0:T(8,128)(2,1)S(1)} %pad_maximum_fusion), channel_id=1, replica_groups=mesh['groups'=2,'dp'=8,'vocab'=2] {'dp'}, dimensions={0}, use_global_device_ids=true | all-gather | bytes 755712 | tf_op jit(solution)/shard_map/all_gather | solution.py:50
  19.6 24.5 %fusion.70 = (f32[64]{0:T(128)S(1)}, f32[64,6144]{1,0:T(8,128)}) fusion(bf16[5120,6144]{1,0:T(8,128)(2,1)} %param.9, bf16[64,5248]{1,0:T(8,128)(2,1)} %all_gather.3), kind=kOutput, calls=%fused_computation.143 | convolution fusion | flops 4026925056 | bytes 65143040 | tf_op jit(solution)/shard_map/dot_general | solution.py:62
  44.2 1.7 fusion.13
  45.9 0.1 copy.31
  46.0 0.0 slice-done
  46.0 0.0 slice-done.1
  46.0 0.0 copy-start
  46.0 0.0 copy-start.1
  46.1 0.0 copy-start.2
  46.1 2.9 %convert_reduce_fusion = (f32[64]{0:T(128)S(1)}, bf16[48,64,4,128]{3,1,2,0:T(8,128)(2,1)}) fusion(bf16[48,4,128,128]{3,2,1,0:T(8,128)(2,1)S(1)} %bitcast.234, bf16[64,48,128,1]{2,1,0,3:T(8,128)(2,1)S(1)} %bitcast.236), kind=kOutput, calls=%fused_computation | convolution fusion | flops 407371712 | bytes 10223872 | tf_op jit(solution)/shard_map/gkc,krcd->krgd/dot_general | solution.py:66
  49.0 0.2 collective-permute-start.4
  49.2 0.0 copy-done
  49.2 0.9 broadcast_in_dim.2
  50.1 4.9 %all-to-all-start = ((bf16[8,8,4096]{2,1,0:T(8,128)(2,1)}), bf16[8,8,4096]{2,1,0:T(8,128)(2,1)S(1)}, u32[]{:S(2)}, u32[]{:S(2)}) async-start(bf16[8,8,4096]{2,1,0:T(8,128)(2,1)} %broadcast_in_dim.2), calls=%async_computation | async-start | bytes 1048576 | tf_op jit(solution)/shard_map/all_to_all | solution.py:51
  55.0 0.0 collective-permute-done.4
  55.0 1.4 collective-permute-start.5
  56.4 0.0 copy-done.1
  56.4 0.0 copy-done.2
  56.4 7.6 %collective-permute-done.5 = f32[2,64]{1,0:T(2,128)S(1)} collective-permute-done((f32[2,64]{1,0:T(2,128)S(1)}, f32[2,64]{1,0:T(2,128)S(1)}, u32[]{:S(2)}, u32[]{:S(2)}) %collective-permute-start.5) | collective-permute-done | bytes 544 | tf_op jit(solution)/shard_map/ppermute | solution.py:100
  64.0 3.9 %collective-permute-start.6 = (f32[2,64]{1,0:T(2,128)S(1)}, f32[2,64]{1,0:T(2,128)S(1)}, u32[]{:S(2)}, u32[]{:S(2)}) collective-permute-start(f32[2,64]{1,0:T(2,128)S(1)} %pad_maximum_fusion.7), channel_id=1, source_target_pairs={{0,8},{2,10},{4,12},{6,14},{8,0},{10,2},{12,4},{14,6},{1,9},{3,11}... | collective-permute-start | bytes 1544 | tf_op jit(solution)/shard_map/ppermute | solution.py:100
  67.9 1.4 collective-permute-done.6
  69.4 1.3 collective-permute-start.12
  70.7 7.7 %convolution_bitcast_fusion = f32[4,2,32,64,128]{4,2,3,1,0:T(8,128)} fusion(bf16[48,4,64,128,1,1]{3,2,1,0,5,4:T(8,128)(2,1)} %bitcast.237, s32[48,4]{0,1:T(4,128)S(1)} %multiply_add_fusion.1, s32[4,2,32]{2,1,0:T(2,128)S(1)} %multiply_add_fusion), kind=kOutput, calls=%fused_computation.8 | convolution fusion | flops 805355520 | bytes 11536128 | tf_op jit(solution)/shard_map/xkr,krgd->xgd/dot_general | solution.py:76
  78.4 0.0 collective-permute-done.12
  78.5 3.9 %fusion.1 = bf16[4,32,64,128]{3,1,2,0:T(8,128)(2,1)} fusion(f32[4,2,32,64,128]{4,2,3,1,0:T(8,128)} %convolution_bitcast_fusion, f32[64]{0:T(128)S(1)} %get-tuple-element.22), kind=kLoop, calls=%fused_computation.4 | loop fusion | flops 2097152 | bytes 6291712 | tf_op jit(solution)/shard_map/convert_element_type | solution.py:123
  82.4 1.6 collective-permute-start.7
  84.0 0.0 all-to-all-done
  84.0 13.7 %fusion.71 = (f32[64]{0:T(128)S(1)}, f32[64,4096]{1,0:T(8,128)S(1)}) fusion(bf16[4096,4096]{1,0:T(8,128)(2,1)} %param.14, bf16[8,8,4096]{2,1,0:T(8,128)(2,1)S(1)} %all-to-all-done), kind=kOutput, calls=%fused_computation.144 | convolution fusion | flops 2147745792 | bytes 35127552 | tf_op jit(solution)/shard_map/dot_general | solution.py:83
  97.7 0.3 exponential_reduce_fusion
  98.1 0.1 collective-permute-start
  98.1 0.1 convert_add_fusion
  98.2 1.1 collective-permute-done
  99.3 0.6 collective-permute-start.1
  100.0 0.1 eq.53
  100.1 1.8 collective-permute-done.1
  101.8 2.7 %collective-permute-start.2 = (f32[2,64]{1,0:T(2,128)S(1)}, f32[2,64]{1,0:T(2,128)S(1)}, u32[]{:S(2)}, u32[]{:S(2)}) collective-permute-start(f32[2,64]{1,0:T(2,128)S(1)} %pad_maximum_fusion.3), channel_id=1, source_target_pairs={{0,8},{2,10},{4,12},{6,14},{8,0},{10,2},{12,4},{14,6},{1,9},{3,11}... | collective-permute-start | bytes 1544 | tf_op jit(solution)/shard_map/ppermute | solution.py:101
  104.5 0.0 collective-permute-done.7
  104.6 3.3 %fusion.3 = f32[4,32,64,128]{3,1,2,0:T(8,128)S(1)} fusion(f32[4,2,32,64,128]{4,2,3,1,0:T(8,128)} %convolution_bitcast_fusion, bf16[4,32,64,128]{3,1,2,0:T(8,128)(2,1)} %collective-permute-done.7, f32[64]{0:T(128)S(1)} %get-tuple-element.22), kind=kLoop, calls=%fused_computation.7 | loop fusion | flops 3145728 | bytes 10486016 | tf_op jit(solution)/shard_map/add | solution.py:125
  107.9 0.1 slice.230
  108.0 0.2 slice.146
  108.2 0.1 collective-permute-start.10
  108.3 0.1 fusion.18
  108.4 0.3 collective-permute-start.8
  108.7 0.0 collective-permute-done.2
  108.7 0.3 collective-permute-start.3
  109.1 24.9 %collective-permute-done.10 = bf16[2,32,32,128]{3,1,2,0:T(8,128)(2,1)S(1)} collective-permute-done((bf16[2,32,32,128]{3,1,2,0:T(8,128)(2,1)S(1)}, bf16[2,32,32,128]{3,1,2,0:T(8,128)(2,1)S(1)}, u32[]{:S(2)}, u32[]{:S(2)}) %collective-permute-start.10) | collective-permute-done | bytes 524320 | tf_op jit(solution)/shard_map/ppermute | solution.py:116
  134.0 0.2 slice_add_fusion
  134.2 0.1 collective-permute-start.11
  134.3 0.0 collective-permute-done.8
  134.3 0.2 fusion.10
  134.5 0.1 collective-permute-start.9
  134.6 0.0 collective-permute-done.3
  134.6 10.4 %collective-permute-done.11 = bf16[1,32,32,128]{3,1,2,0:T(8,128)(2,1)S(1)} collective-permute-done((bf16[1,32,32,128]{3,1,2,0:T(8,128)(2,1)S(1)}, bf16[1,32,32,128]{3,1,2,0:T(8,128)(2,1)S(1)}, u32[]{:S(2)}, u32[]{:S(2)}) %collective-permute-start.11) | collective-permute-done | bytes 262176 | tf_op jit(solution)/shard_map/ppermute | solution.py:116
  145.1 0.1 slice_add_fusion.1
  145.1 3.4 %collective-permute-done.9 = bf16[1,32,32,128]{3,1,2,0:T(8,128)(2,1)S(1)} collective-permute-done((bf16[1,32,32,128]{3,1,2,0:T(8,128)(2,1)S(1)}, bf16[1,32,32,128]{3,1,2,0:T(8,128)(2,1)S(1)}, u32[]{:S(2)}, u32[]{:S(2)}) %collective-permute-start.9) | collective-permute-done | bytes 262176 | tf_op jit(solution)/shard_map/ppermute | solution.py:116
  148.5 0.1 fusion.19
  148.6 0.1 fusion.11
  148.7 16.4 %convolution_convert_fusion = bf16[64,4096]{1,0:T(8,128)(2,1)S(1)} fusion(bf16[4096,4096]{1,0:T(8,128)(2,1)} %param.14, f32[8,8,32,128]{3,2,1,0:T(8,128)S(1)} %bitcast.235, f32[64,4096]{1,0:T(8,128)S(1)} %get-tuple-element.30, s32[4096]{0:T(1024)S(1)} %iota_add_fusion, f32[64]{0:T(128)S(1)} %get-tuple-element.11, f32[64]{0:T(128)S(1)} %get-tuple-element.5, ...), kind=kOutput, calls=%fused_computation.1 | convolution fusion | flops 2150367232 | bytes 36193280 | tf_op jit(solution)/shard_map/dot_general | solution.py:152
  165.1 0.2 reshape.336
  165.3 18.6 %all_to_all.10 = bf16[16,4,4096]{2,1,0:T(4,128)(2,1)S(1)} all-to-all(bf16[16,4,4096]{2,1,0:T(4,128)(2,1)S(1)} %reshape.336), channel_id=1, replica_groups=mesh['groups'=2,'dp'=8,'vocab'=2] {'dp','vocab'}, dimensions={0} | all-to-all | bytes 1048576 | tf_op jit(solution)/shard_map/all_to_all | solution.py:157
  183.9 0.8 reduce_sum.32
  (28 shorter events, 0.3 us)
Async XLA Ops:
  1.6 44.4 %slice-start = ((s8[6291456]{0:T(1024)(128)(4,1)}), s8[4194304]{0:T(1024)(128)(4,1)S(1)}, s32[]{:S(2)}) async-start(s8[6291456]{0:T(1024)(128)(4,1)} %bitcast.233), calls=%async_computation.2 | async-start | bytes 8388608
  19.6 26.4 %slice-start.1 = ((s8[6291456]{0:T(1024)(128)(4,1)}), s8[2097152]{0:T(1024)(128)(4,1)S(1)}, s32[]{:S(2)}) async-start(s8[6291456]{0:T(1024)(128)(4,1)} %bitcast.233), calls=%async_computation.3 | async-start | bytes 4194304
  46.0 3.2 %copy-start = (bf16[8,4096]{1,0:T(8,128)(2,1)S(1)}, bf16[8,4096]{1,0:T(8,128)(2,1)}, u32[]{:S(2)}) copy-start(bf16[8,4096]{1,0:T(8,128)(2,1)} %param.13) | copy-start | bytes 196612
  46.0 10.4 %copy-start.1 = (s32[48,4]{0,1:T(4,128)S(1)}, s32[48,4]{0,1:T(4,128)}, u32[]{:S(2)}) copy-start(s32[48,4]{0,1:T(4,128)} %param.11) | copy-start | bytes 2308
  46.1 10.3 %copy-start.2 = (s32[48,4]{0,1:T(4,128)S(1)}, s32[48,4]{0,1:T(4,128)}, u32[]{:S(2)}) copy-start(s32[48,4]{0,1:T(4,128)} %param.10) | copy-start | bytes 2308
  49.0 6.0 %collective-permute-start.4 = (f32[2,64]{1,0:T(2,128)S(1)}, f32[2,64]{1,0:T(2,128)S(1)}, u32[]{:S(2)}, u32[]{:S(2)}) collective-permute-start(f32[2,64]{1,0:T(2,128)S(1)} %pad_maximum_fusion.5), channel_id=1, source_target_pairs={{0,2},{2,0},{4,6},{6,4},{8,10},{10,8},{12,14},{14,12},{1,3},{3,1},... | collective-permute-start | bytes 1544 | tf_op jit(solution)/shard_map/ppermute | solution.py:100
  50.1 33.9 %all-to-all-start = ((bf16[8,8,4096]{2,1,0:T(8,128)(2,1)}), bf16[8,8,4096]{2,1,0:T(8,128)(2,1)S(1)}, u32[]{:S(2)}, u32[]{:S(2)}) async-start(bf16[8,8,4096]{2,1,0:T(8,128)(2,1)} %broadcast_in_dim.2), calls=%async_computation | async-start | bytes 1048576 | tf_op jit(solution)/shard_map/all_to_all | solution.py:51
  55.0 9.0 %collective-permute-start.5 = (f32[2,64]{1,0:T(2,128)S(1)}, f32[2,64]{1,0:T(2,128)S(1)}, u32[]{:S(2)}, u32[]{:S(2)}) collective-permute-start(f32[2,64]{1,0:T(2,128)S(1)} %pad_maximum_fusion.6), channel_id=1, source_target_pairs={{0,4},{2,6},{4,0},{6,2},{8,12},{10,14},{12,8},{14,10},{1,5},{3,7},... | collective-permute-start | bytes 1544 | tf_op jit(solution)/shard_map/ppermute | solution.py:100
  64.0 5.3 %collective-permute-start.6 = (f32[2,64]{1,0:T(2,128)S(1)}, f32[2,64]{1,0:T(2,128)S(1)}, u32[]{:S(2)}, u32[]{:S(2)}) collective-permute-start(f32[2,64]{1,0:T(2,128)S(1)} %pad_maximum_fusion.7), channel_id=1, source_target_pairs={{0,8},{2,10},{4,12},{6,14},{8,0},{10,2},{12,4},{14,6},{1,9},{3,11}... | collective-permute-start | bytes 1544 | tf_op jit(solution)/shard_map/ppermute | solution.py:100
  69.4 9.0 %collective-permute-start.12 = (f32[2,64]{1,0:T(2,128)S(1)}, f32[2,64]{1,0:T(2,128)S(1)}, u32[]{:S(2)}, u32[]{:S(2)}) collective-permute-start(f32[2,64]{1,0:T(2,128)S(1)} %pad_maximum_fusion.8), channel_id=1, source_target_pairs={{0,1},{1,0},{2,3},{3,2},{4,5},{5,4},{6,7},{7,6},{8,9},{9,8},{10,11... | collective-permute-start | bytes 1544 | tf_op jit(solution)/shard_map/ppermute | solution.py:135
  70.7 7.7 %slice-start.2 = ((bf16[64,5248]{1,0:T(8,128)(2,1)}), bf16[64,128]{1,0:T(8,128)(2,1)S(1)}, s32[]{:S(2)}) async-start(bf16[64,5248]{1,0:T(8,128)(2,1)} %all_gather.3), calls=%async_computation.4 | async-start | bytes 32768 | tf_op jit(solution)/shard_map/slice | solution.py:57
  82.4 22.2 %collective-permute-start.7 = (bf16[4,32,64,128]{3,1,2,0:T(8,128)(2,1)}, bf16[4,32,64,128]{3,1,2,0:T(8,128)(2,1)}, u32[]{:S(2)}, u32[]{:S(2)}) collective-permute-start(bf16[4,32,64,128]{3,1,2,0:T(8,128)(2,1)} %fusion.1), channel_id=1, source_target_pairs={{0,2},{2,0},{4,6},{6,4},{8,10},{10,8},{12,14},{14,12},{1,3},{3,1},... | collective-permute-start | bytes 6291464 | tf_op jit(solution)/shard_map/ppermute | solution.py:122
  98.1 1.2 collective-permute-start
  99.3 2.5 %collective-permute-start.1 = (f32[2,64]{1,0:T(2,128)S(1)}, f32[2,64]{1,0:T(2,128)S(1)}, u32[]{:S(2)}, u32[]{:S(2)}) collective-permute-start(f32[2,64]{1,0:T(2,128)S(1)} %pad_maximum_fusion.2), channel_id=1, source_target_pairs={{0,4},{2,6},{4,0},{6,2},{8,12},{10,14},{12,8},{14,10},{1,5},{3,7},... | collective-permute-start | bytes 1544 | tf_op jit(solution)/shard_map/ppermute | solution.py:101
  101.8 6.9 %collective-permute-start.2 = (f32[2,64]{1,0:T(2,128)S(1)}, f32[2,64]{1,0:T(2,128)S(1)}, u32[]{:S(2)}, u32[]{:S(2)}) collective-permute-start(f32[2,64]{1,0:T(2,128)S(1)} %pad_maximum_fusion.3), channel_id=1, source_target_pairs={{0,8},{2,10},{4,12},{6,14},{8,0},{10,2},{12,4},{14,6},{1,9},{3,11}... | collective-permute-start | bytes 1544 | tf_op jit(solution)/shard_map/ppermute | solution.py:101
  108.2 25.8 %collective-permute-start.10 = (bf16[2,32,32,128]{3,1,2,0:T(8,128)(2,1)S(1)}, bf16[2,32,32,128]{3,1,2,0:T(8,128)(2,1)S(1)}, u32[]{:S(2)}, u32[]{:S(2)}) collective-permute-start(bf16[2,32,32,128]{3,1,2,0:T(8,128)(2,1)S(1)} %slice.230), channel_id=1, source_target_pairs={{0,8},{2,10},{4,12},{6,14},{8,0},{10,2},{12,4},{14,6},{1,9},{3,11}... | collective-permute-start | bytes 1572872 | tf_op jit(solution)/shard_map/ppermute | solution.py:116
  108.4 25.9 %collective-permute-start.8 = (bf16[2,32,32,128]{3,1,2,0:T(8,128)(2,1)S(1)}, bf16[2,32,32,128]{3,1,2,0:T(8,128)(2,1)S(1)}, u32[]{:S(2)}, u32[]{:S(2)}) collective-permute-start(bf16[2,32,32,128]{3,1,2,0:T(8,128)(2,1)S(1)} %fusion.18), channel_id=1, source_target_pairs={{0,4},{2,6},{4,0},{6,2},{8,12},{10,14},{12,8},{14,10},{1,5},{3,7},... | collective-permute-start | bytes 1572872 | tf_op jit(solution)/shard_map/ppermute | solution.py:116
  108.7 25.8 %collective-permute-start.3 = (f32[2,64]{1,0:T(2,128)S(1)}, f32[2,64]{1,0:T(2,128)S(1)}, u32[]{:S(2)}, u32[]{:S(2)}) collective-permute-start(f32[2,64]{1,0:T(2,128)S(1)} %pad_maximum_fusion.4), channel_id=1, source_target_pairs={{0,1},{1,0},{2,3},{3,2},{4,5},{5,4},{6,7},{7,6},{8,9},{9,8},{10,11... | collective-permute-start | bytes 1544 | tf_op jit(solution)/shard_map/ppermute | solution.py:136
  134.2 10.9 %collective-permute-start.11 = (bf16[1,32,32,128]{3,1,2,0:T(8,128)(2,1)S(1)}, bf16[1,32,32,128]{3,1,2,0:T(8,128)(2,1)S(1)}, u32[]{:S(2)}, u32[]{:S(2)}) collective-permute-start(bf16[1,32,32,128]{3,1,2,0:T(8,128)(2,1)S(1)} %slice.231), channel_id=1, source_target_pairs={{0,4},{2,6},{4,0},{6,2},{8,12},{10,14},{12,8},{14,10},{1,5},{3,7},... | collective-permute-start | bytes 786440 | tf_op jit(solution)/shard_map/ppermute | solution.py:116
  134.5 14.0 %collective-permute-start.9 = (bf16[1,32,32,128]{3,1,2,0:T(8,128)(2,1)S(1)}, bf16[1,32,32,128]{3,1,2,0:T(8,128)(2,1)S(1)}, u32[]{:S(2)}, u32[]{:S(2)}) collective-permute-start(bf16[1,32,32,128]{3,1,2,0:T(8,128)(2,1)S(1)} %fusion.33), channel_id=1, source_target_pairs={{0,8},{2,10},{4,12},{6,14},{8,0},{10,2},{12,4},{14,6},{1,9},{3,11}... | collective-permute-start | bytes 786440 | tf_op jit(solution)/shard_map/ppermute | solution.py:116

commit v13 on v11

--- a/solution.py
+++ b/solution.py
@@ -131,8 +131,9 @@
     stage = 1
     while stage < vocab_count:
         pairs = [(j, j ^ stage) for j in range(vocab_count)]
-        teacher_stats = merge(teacher_stats, lax.ppermute(teacher_stats, "vocab", pairs))[0]
-        student_stats = merge(student_stats, lax.ppermute(student_stats, "vocab", pairs))[0]
+        both = lax.ppermute(jnp.concatenate([teacher_stats, student_stats]), "vocab", pairs)
+        teacher_stats = merge(teacher_stats, both[:2])[0]
+        student_stats = merge(student_stats, both[2:])[0]
         stage *= 2
     teacher_peak, target_total = teacher_stats[0], teacher_stats[1]
     student_peak, student_total = student_stats[0], student_stats[1]

time: 180 us -> 182 us (1.011)
  local copies, waits for them, and re-layouts: 5.6 us -> 9.82 us
  waiting for transfers between devices: 43.8 us -> 40 us
  matrix products: 63.5 us -> 60.3 us
  starting transfers between devices: 17.8 us -> 21 us
  blocking collectives: 38.3 us -> 41 us
    ppermute x3, waiting for transfers between devices: 7.61 us -> 0.01 us  [on_device(): lax.ppermute(teacher_stats, 'dp', pairs)]
    all_gather x1, blocking collectives: 16.8 us -> 21.7 us  [on_device(): gathered = lax.all_gather(packed, 'dp', axis=0, tiled=True)]
    ppermute x1, waiting for transfers between devices: 0.01 us -> 3.79 us  [on_device(): lax.ppermute((pair[:, 1] * to_column).astype(jnp.bfloat16), 'dp', [(j, j...]
    add x3, other arithmetic: 0.32 us -> 3.62 us  [reduce_bits(): keep + lax.ppermute(send.astype(jnp.bfloat16), 'dp', pairs).astype(jnp.fl...]
    dot_general x1, matrix products: 5.69 us -> 2.51 us  [on_device(): jnp.dot(placement, mapped_terms.reshape(item_count, tokens_all * block_si...]
    add x1, other arithmetic: 3.34 us -> 0.54 us  [on_device(): held = pair[:, 0] * to_column + arrived.astype(jnp.float32)]
    ppermute x3, starting transfers between devices: 0.46 us -> 2.92 us  [on_device(): lax.ppermute(student_stats, 'dp', pairs)]
    all_to_all x1, blocking collectives: 21.5 us -> 19.3 us  [on_device(): lax.all_to_all(partial, ('dp', 'vocab'), split_axis=0, concat_axis=0, til...]
  transfers between devices with their start and end apart: 14 -> 13, of which waited for: 5 -> 7; matrix products, arithmetic and copies ran while one was open for 18% -> 31% of each run, Pallas kernels for 0% -> 0%
where the time goes in v13:
time: 182 us
  matrix products  60.3 us (33%)
  blocking collectives  41 us (23%)
  waiting for transfers between devices  40 us (22%)
  starting transfers between devices  21 us (12%)
  local copies, waits for them, and re-layouts  9.82 us (5%)
  other arithmetic  9.29 us (5%)
    ppermute x4, waiting for transfers between devices, reduce_bits(): lax.ppermute(send.astype(jnp.bfloat16), 'dp', pairs).astype(jnp.float32)  33.9 us
    dot_general x1, matrix products, on_device(): jnp.dot(teacher_all, teacher_head, preferred_element_type=jnp.float32)  23.4 us
    all_gather x1, blocking collectives, on_device(): gathered = lax.all_gather(packed, 'dp', axis=0, tiled=True)  21.7 us
    all_to_all x1, blocking collectives, on_device(): lax.all_to_all(partial, ('dp', 'vocab'), split_axis=0, concat_axis=0, til...  19.3 us
    dot_general x1, matrix products, on_device(): lax.dot_general(logit_grad, student_head, (((1,), (1,)), ((), ())), prefe...  16.4 us
    dot_general x1, matrix products, on_device(): jnp.dot(student_all, student_head, preferred_element_type=jnp.float32)  14 us
    all_to_all x1, starting transfers between devices, on_device(): lax.all_to_all(jnp.broadcast_to(student_hidden[None], (dp_count,) + stude...  6.37 us
    unnamed x19, local copies, waits for them, and re-layouts  4.79 us
  transfers between devices with their start and end apart: 13, of which 7 were waited for; matrix products, arithmetic and copies ran while one was open for 31% of the time, Pallas kernels for 0%

profile of v13, /device:TPU:1, one launch (start us, length us, event | category | flops | bytes accessed | tf_op | source)
XLA Modules:
  0.0 181.7 jit_solution(14626081905423966778)
XLA Ops:
  0.0 1.7 broadcast_in_dim.2
  1.7 6.4 %all-to-all-start = ((bf16[8,8,4096]{2,1,0:T(8,128)(2,1)}), bf16[8,8,4096]{2,1,0:T(8,128)(2,1)}, u32[]{:S(2)}, u32[]{:S(2)}) async-start(bf16[8,8,4096]{2,1,0:T(8,128)(2,1)} %broadcast_in_dim.2), calls=%async_computation | async-start | bytes 1048576 | tf_op jit(solution)/shard_map/all_to_all | solution.py:51
  8.0 0.7 convert_convert_fusion
  8.7 0.1 fusion.40
  8.8 0.9 pad_maximum_fusion
  9.7 21.7 %all_gather.3 = bf16[64,5248]{1,0:T(8,128)(2,1)S(1)} all-gather(bf16[8,5248]{1,0:T(8,128)(2,1)S(1)} %pad_maximum_fusion), channel_id=1, replica_groups=mesh['groups'=2,'dp'=8,'vocab'=2] {'dp'}, dimensions={0}, use_global_device_ids=true | all-gather | bytes 755712 | tf_op jit(solution)/shard_map/all_gather | solution.py:50
  31.4 23.4 %fusion.71 = (f32[64]{0:T(128)S(1)}, f32[64,6144]{1,0:T(8,128)S(1)}) fusion(bf16[5120,6144]{1,0:T(8,128)(2,1)} %param.9, bf16[64,5248]{1,0:T(8,128)(2,1)S(1)} %all_gather.3), kind=kOutput, calls=%fused_computation.143 | convolution fusion | flops 4026925056 | bytes 65143040 | tf_op jit(solution)/shard_map/dot_general | solution.py:62
  54.8 0.3 fusion.14
  55.1 0.1 copy.30
  55.2 0.0 copy-start.6
  55.2 0.0 copy-start.7
  55.2 4.0 %convert_reduce_fusion = (f32[64]{0:T(128)S(1)}, bf16[48,64,4,128]{3,1,2,0:T(8,128)(2,1)S(1)}) fusion(bf16[48,4,128,128]{3,2,1,0:T(8,128)(2,1)} %param.12, bf16[64,48,128,1]{2,1,0,3:T(8,128)(2,1)S(1)} %bitcast.245), kind=kOutput, calls=%fused_computation | convolution fusion | flops 407371712 | bytes 10223872 | tf_op jit(solution)/shard_map/gkc,krcd->krgd/dot_general | solution.py:66
  59.2 0.2 collective-permute-start.3
  59.4 0.0 copy-done.6
  59.5 0.1 copy.12
  59.6 0.1 add.150
  59.7 2.8 %copy.53 = bf16[24,8,64,128]{3,1,2,0:T(8,128)(2,1)S(1)} copy(bf16[24,8,64,128]{3,2,1,0:T(8,128)(2,1)S(1)} %bitcast.241) | data formatting | bytes 6291456
  62.5 0.9 copy.32
  63.4 0.0 collective-permute-done.3
  63.4 1.7 collective-permute-start.4
  65.1 0.0 all-to-all-done
  65.1 14.0 %fusion.72 = (f32[64]{0:T(128)S(1)}, f32[64,4096]{1,0:T(8,128)S(1)}) fusion(bf16[4096,4096]{1,0:T(8,128)(2,1)} %param.14, bf16[8,8,4096]{2,1,0:T(8,128)(2,1)} %all-to-all-done), kind=kOutput, calls=%fused_computation.144 | convolution fusion | flops 2147745792 | bytes 35127552 | tf_op jit(solution)/shard_map/dot_general | solution.py:82
  79.2 0.3 exponential_reduce_fusion
  79.5 0.7 collective-permute-start
  80.2 0.0 collective-permute-done.4
  80.2 0.8 collective-permute-done
  81.0 0.1 collective-permute-start.1
  81.1 2.2 %collective-permute-start.5 = (f32[2,64]{1,0:T(2,128)S(1)}, f32[2,64]{1,0:T(2,128)S(1)}, u32[]{:S(2)}, u32[]{:S(2)}) collective-permute-start(f32[2,64]{1,0:T(2,128)S(1)} %pad_maximum_fusion.7), channel_id=1, source_target_pairs={{0,8},{2,10},{4,12},{6,14},{8,0},{10,2},{12,4},{14,6},{1,9},{3,11}... | collective-permute-start | bytes 1544 | tf_op jit(solution)/shard_map/ppermute | solution.py:99
  83.3 0.2 collective-permute-done.1
  83.6 2.2 %collective-permute-start.2 = (f32[2,64]{1,0:T(2,128)S(1)}, f32[2,64]{1,0:T(2,128)S(1)}, u32[]{:S(2)}, u32[]{:S(2)}) collective-permute-start(f32[2,64]{1,0:T(2,128)S(1)} %pad_maximum_fusion.4), channel_id=1, source_target_pairs={{0,8},{2,10},{4,12},{6,14},{8,0},{10,2},{12,4},{14,6},{1,9},{3,11}... | collective-permute-start | bytes 1544 | tf_op jit(solution)/shard_map/ppermute | solution.py:100
  85.7 0.0 collective-permute-done.5
  85.7 1.2 collective-permute-done.2
  87.0 1.3 collective-permute-start.6
  88.3 2.5 %fusion.4 = f32[4,2,32,64,128]{4,2,3,1,0:T(8,128)S(1)} fusion(bf16[64,128,192,1,1]{1,0,2,4,3:T(8,128)(2,1)S(1)} %bitcast.240, s32[192]{0:T(256)S(1)} %add.150, s32[4,2,32]{2,1,0:T(2,128)S(1)} %multiply_add_fusion), kind=kOutput, calls=%fused_computation.9 | convolution fusion | flops 805355520 | bytes 11536128 | tf_op jit(solution)/shard_map/dot_general | solution.py:76
  90.8 0.0 collective-permute-done.6
  90.8 0.4 fusion.1
  91.3 3.0 %collective-permute-start.7 = (bf16[4,32,64,128]{3,1,2,0:T(8,128)(2,1)S(1)}, bf16[4,32,64,128]{3,1,2,0:T(8,128)(2,1)S(1)}, u32[]{:S(2)}, u32[]{:S(2)}) collective-permute-start(bf16[4,32,64,128]{3,1,2,0:T(8,128)(2,1)S(1)} %fusion.1), channel_id=1, source_target_pairs={{0,2},{2,0},{4,6},{6,4},{8,10},{10,8},{12,14},{14,12},{1,3},{3,1},... | collective-permute-start | bytes 6291464 | tf_op jit(solution)/shard_map/ppermute | solution.py:121
  94.3 3.8 %collective-permute-done.7 = bf16[4,32,64,128]{3,1,2,0:T(8,128)(2,1)S(1)} collective-permute-done((bf16[4,32,64,128]{3,1,2,0:T(8,128)(2,1)S(1)}, bf16[4,32,64,128]{3,1,2,0:T(8,128)(2,1)S(1)}, u32[]{:S(2)}, u32[]{:S(2)}) %collective-permute-start.7) | collective-permute-done | bytes 2097184 | tf_op jit(solution)/shard_map/ppermute | solution.py:121
  98.0 0.5 fusion.3
  98.6 0.0 slice-start
  98.6 1.0 slice.236
  99.6 2.1 %collective-permute-start.10 = (bf16[2,32,32,128]{3,1,2,0:T(8,128)(2,1)}, bf16[2,32,32,128]{3,1,2,0:T(8,128)(2,1)S(1)}, u32[]{:S(2)}, u32[]{:S(2)}) collective-permute-start(bf16[2,32,32,128]{3,1,2,0:T(8,128)(2,1)} %slice.236), channel_id=1, source_target_pairs={{0,8},{2,10},{4,12},{6,14},{8,0},{10,2},{12,4},{14,6},{1,9},{3,11}... | collective-permute-start | bytes 1572872 | tf_op jit(solution)/shard_map/ppermute | solution.py:115
  101.7 0.2 slice.152
  101.9 0.9 fusion.19
  102.8 0.0 collective-permute-start.8
  102.8 0.1 convert_add_fusion
  102.9 22.7 %collective-permute-done.10 = bf16[2,32,32,128]{3,1,2,0:T(8,128)(2,1)S(1)} collective-permute-done((bf16[2,32,32,128]{3,1,2,0:T(8,128)(2,1)}, bf16[2,32,32,128]{3,1,2,0:T(8,128)(2,1)S(1)}, u32[]{:S(2)}, u32[]{:S(2)}) %collective-permute-start.10) | collective-permute-done | bytes 524320 | tf_op jit(solution)/shard_map/ppermute | solution.py:115
  125.6 1.4 slice_add_fusion
  127.0 0.7 slice.237
  127.8 0.0 collective-permute-start.11
  127.8 0.0 collective-permute-done.8
  127.8 1.2 fusion.11
  129.1 0.9 copy-done.5
  130.0 1.3 collective-permute-start.9
  131.3 0.1 eq.56
  131.4 5.9 %collective-permute-done.11 = bf16[1,32,32,128]{3,1,2,0:T(8,128)(2,1)S(1)} collective-permute-done((bf16[1,32,32,128]{3,1,2,0:T(8,128)(2,1)}, bf16[1,32,32,128]{3,1,2,0:T(8,128)(2,1)S(1)}, u32[]{:S(2)}, u32[]{:S(2)}) %collective-permute-start.11) | collective-permute-done | bytes 262176 | tf_op jit(solution)/shard_map/ppermute | solution.py:115
  137.3 1.1 slice_add_fusion.1
  138.5 5.3 %collective-permute-done.9 = bf16[1,32,32,128]{3,1,2,0:T(8,128)(2,1)S(1)} collective-permute-done((bf16[1,32,32,128]{3,1,2,0:T(8,128)(2,1)S(1)}, bf16[1,32,32,128]{3,1,2,0:T(8,128)(2,1)S(1)}, u32[]{:S(2)}, u32[]{:S(2)}) %collective-permute-start.9) | collective-permute-done | bytes 262176 | tf_op jit(solution)/shard_map/ppermute | solution.py:115
  143.7 1.1 fusion.20
  144.9 0.1 fusion.12
  145.0 16.4 %convolution_convert_fusion = bf16[64,4096]{1,0:T(8,128)(2,1)S(1)} fusion(bf16[4096,4096]{1,0:T(8,128)(2,1)} %param.14, f32[8,8,32,128]{3,2,1,0:T(8,128)S(1)} %bitcast.244, f32[64,4096]{1,0:T(8,128)S(1)} %copy-done.2, s32[4096]{0:T(1024)S(1)} %iota_add_fusion, f32[64]{0:T(128)S(1)} %get-tuple-element.7, f32[64]{0:T(128)S(1)} %get-tuple-element.5, ...), kind=kOutput, calls=%fused_computation.1 | convolution fusion | flops 2150367232 | bytes 36193280 | tf_op jit(solution)/shard_map/dot_general | solution.py:152
  161.4 0.2 reshape.345
  161.6 19.3 %all_to_all.10 = bf16[16,4,4096]{2,1,0:T(4,128)(2,1)S(1)} all-to-all(bf16[16,4,4096]{2,1,0:T(4,128)(2,1)S(1)} %reshape.345), channel_id=1, replica_groups=mesh['groups'=2,'dp'=8,'vocab'=2] {'dp','vocab'}, dimensions={0} | all-to-all | bytes 1048576 | tf_op jit(solution)/shard_map/all_to_all | solution.py:157
  180.9 0.8 reduce_sum.32
  (33 shorter events, 0.3 us)
Async XLA Ops:
  1.7 63.5 %all-to-all-start = ((bf16[8,8,4096]{2,1,0:T(8,128)(2,1)}), bf16[8,8,4096]{2,1,0:T(8,128)(2,1)}, u32[]{:S(2)}, u32[]{:S(2)}) async-start(bf16[8,8,4096]{2,1,0:T(8,128)(2,1)} %broadcast_in_dim.2), calls=%async_computation | async-start | bytes 1048576 | tf_op jit(solution)/shard_map/all_to_all | solution.py:51
  31.4 23.4 %copy-start.3 = (bf16[64,5248]{1,0:T(8,128)(2,1)}, bf16[64,5248]{1,0:T(8,128)(2,1)S(1)}, u32[]{:S(2)}) copy-start(bf16[64,5248]{1,0:T(8,128)(2,1)S(1)} %all_gather.3) | copy-start | bytes 2015236
  55.2 4.2 %copy-start.6 = (s32[48,4]{0,1:T(4,128)S(1)}, s32[48,4]{0,1:T(4,128)}, u32[]{:S(2)}) copy-start(s32[48,4]{0,1:T(4,128)} %param.11) | copy-start | bytes 2308
  55.2 4.2 %copy-start.7 = (s32[48,4]{0,1:T(4,128)S(1)}, s32[48,4]{0,1:T(4,128)}, u32[]{:S(2)}) copy-start(s32[48,4]{0,1:T(4,128)} %param.10) | copy-start | bytes 2308
  59.2 4.2 %collective-permute-start.3 = (f32[2,64]{1,0:T(2,128)S(1)}, f32[2,64]{1,0:T(2,128)S(1)}, u32[]{:S(2)}, u32[]{:S(2)}) collective-permute-start(f32[2,64]{1,0:T(2,128)S(1)} %pad_maximum_fusion.5), channel_id=1, source_target_pairs={{0,2},{2,0},{4,6},{6,4},{8,10},{10,8},{12,14},{14,12},{1,3},{3,1},... | collective-permute-start | bytes 1544 | tf_op jit(solution)/shard_map/ppermute | solution.py:99
  63.4 16.8 %collective-permute-start.4 = (f32[2,64]{1,0:T(2,128)S(1)}, f32[2,64]{1,0:T(2,128)S(1)}, u32[]{:S(2)}, u32[]{:S(2)}) collective-permute-start(f32[2,64]{1,0:T(2,128)S(1)} %pad_maximum_fusion.6), channel_id=1, source_target_pairs={{0,4},{2,6},{4,0},{6,2},{8,12},{10,14},{12,8},{14,10},{1,5},{3,7},... | collective-permute-start | bytes 1544 | tf_op jit(solution)/shard_map/ppermute | solution.py:99
  79.2 11.6 %copy-start.1 = (f32[64,4096]{1,0:T(8,128)}, f32[64,4096]{1,0:T(8,128)S(1)}, u32[]{:S(2)}) copy-start(f32[64,4096]{1,0:T(8,128)S(1)} %get-tuple-element.28) | copy-start | bytes 3145732
  79.5 1.5 collective-permute-start
  81.0 2.5 %collective-permute-start.1 = (f32[2,64]{1,0:T(2,128)S(1)}, f32[2,64]{1,0:T(2,128)S(1)}, u32[]{:S(2)}, u32[]{:S(2)}) collective-permute-start(f32[2,64]{1,0:T(2,128)S(1)} %pad_maximum_fusion.3), channel_id=1, source_target_pairs={{0,4},{2,6},{4,0},{6,2},{8,12},{10,14},{12,8},{14,10},{1,5},{3,7},... | collective-permute-start | bytes 1544 | tf_op jit(solution)/shard_map/ppermute | solution.py:100
  81.1 4.6 %collective-permute-start.5 = (f32[2,64]{1,0:T(2,128)S(1)}, f32[2,64]{1,0:T(2,128)S(1)}, u32[]{:S(2)}, u32[]{:S(2)}) collective-permute-start(f32[2,64]{1,0:T(2,128)S(1)} %pad_maximum_fusion.7), channel_id=1, source_target_pairs={{0,8},{2,10},{4,12},{6,14},{8,0},{10,2},{12,4},{14,6},{1,9},{3,11}... | collective-permute-start | bytes 1544 | tf_op jit(solution)/shard_map/ppermute | solution.py:99
  83.6 3.4 %collective-permute-start.2 = (f32[2,64]{1,0:T(2,128)S(1)}, f32[2,64]{1,0:T(2,128)S(1)}, u32[]{:S(2)}, u32[]{:S(2)}) collective-permute-start(f32[2,64]{1,0:T(2,128)S(1)} %pad_maximum_fusion.4), channel_id=1, source_target_pairs={{0,8},{2,10},{4,12},{6,14},{8,0},{10,2},{12,4},{14,6},{1,9},{3,11}... | collective-permute-start | bytes 1544 | tf_op jit(solution)/shard_map/ppermute | solution.py:100
  87.0 3.8 %collective-permute-start.6 = (f32[4,64]{1,0:T(4,128)S(1)}, f32[4,64]{1,0:T(4,128)S(1)}, u32[]{:S(2)}, u32[]{:S(2)}) collective-permute-start(f32[4,64]{1,0:T(4,128)S(1)} %pad_maximum_fusion.1), channel_id=1, source_target_pairs={{0,1},{1,0},{2,3},{3,2},{4,5},{5,4},{6,7},{7,6},{8,9},{9,8},{10,11... | collective-permute-start | bytes 3080 | tf_op jit(solution)/shard_map/ppermute | solution.py:134
  91.3 6.8 %collective-permute-start.7 = (bf16[4,32,64,128]{3,1,2,0:T(8,128)(2,1)S(1)}, bf16[4,32,64,128]{3,1,2,0:T(8,128)(2,1)S(1)}, u32[]{:S(2)}, u32[]{:S(2)}) collective-permute-start(bf16[4,32,64,128]{3,1,2,0:T(8,128)(2,1)S(1)} %fusion.1), channel_id=1, source_target_pairs={{0,2},{2,0},{4,6},{6,4},{8,10},{10,8},{12,14},{14,12},{1,3},{3,1},... | collective-permute-start | bytes 6291464 | tf_op jit(solution)/shard_map/ppermute | solution.py:121
  98.6 3.2 %copy-start = (f32[4,32,64,128]{3,1,2,0:T(8,128)}, f32[4,32,64,128]{3,1,2,0:T(8,128)S(1)}, u32[]{:S(2)}) copy-start(f32[4,32,64,128]{3,1,2,0:T(8,128)S(1)} %fusion.3) | copy-start | bytes 12582916
  98.6 4.2 %slice-start = ((bf16[64,5248]{1,0:T(8,128)(2,1)}), bf16[64,128]{1,0:T(8,128)(2,1)S(1)}, s32[]{:S(2)}) async-start(bf16[64,5248]{1,0:T(8,128)(2,1)} %copy-done.3), calls=%async_computation.2 | async-start | bytes 32768 | tf_op jit(solution)/shard_map/slice | solution.py:57
  99.6 26.0 %collective-permute-start.10 = (bf16[2,32,32,128]{3,1,2,0:T(8,128)(2,1)}, bf16[2,32,32,128]{3,1,2,0:T(8,128)(2,1)S(1)}, u32[]{:S(2)}, u32[]{:S(2)}) collective-permute-start(bf16[2,32,32,128]{3,1,2,0:T(8,128)(2,1)} %slice.236), channel_id=1, source_target_pairs={{0,8},{2,10},{4,12},{6,14},{8,0},{10,2},{12,4},{14,6},{1,9},{3,11}... | collective-permute-start | bytes 1572872 | tf_op jit(solution)/shard_map/ppermute | solution.py:115
  102.8 25.0 %collective-permute-start.8 = (bf16[2,32,32,128]{3,1,2,0:T(8,128)(2,1)}, bf16[2,32,32,128]{3,1,2,0:T(8,128)(2,1)}, u32[]{:S(2)}, u32[]{:S(2)}) collective-permute-start(bf16[2,32,32,128]{3,1,2,0:T(8,128)(2,1)} %fusion.19), channel_id=1, source_target_pairs={{0,4},{2,6},{4,0},{6,2},{8,12},{10,14},{12,8},{14,10},{1,5},{3,7},... | collective-permute-start | bytes 1572872 | tf_op jit(solution)/shard_map/ppermute | solution.py:115
  127.0 2.0 %copy-start.4 = (f32[2,32,32,128]{3,1,2,0:T(8,128)}, f32[2,32,32,128]{3,1,2,0:T(8,128)S(1)}, u32[]{:S(2)}) copy-start(f32[2,32,32,128]{3,1,2,0:T(8,128)S(1)} %slice_add_fusion) | copy-start | bytes 3145732
  127.0 18.0 %copy-start.2 = (f32[64,4096]{1,0:T(8,128)S(1)}, f32[64,4096]{1,0:T(8,128)}, u32[]{:S(2)}) copy-start(f32[64,4096]{1,0:T(8,128)} %copy-done.1) | copy-start | bytes 3145732
  127.8 9.6 %collective-permute-start.11 = (bf16[1,32,32,128]{3,1,2,0:T(8,128)(2,1)}, bf16[1,32,32,128]{3,1,2,0:T(8,128)(2,1)S(1)}, u32[]{:S(2)}, u32[]{:S(2)}) collective-permute-start(bf16[1,32,32,128]{3,1,2,0:T(8,128)(2,1)} %slice.237), channel_id=1, source_target_pairs={{0,4},{2,6},{4,0},{6,2},{8,12},{10,14},{12,8},{14,10},{1,5},{3,7},... | collective-permute-start | bytes 786440 | tf_op jit(solution)/shard_map/ppermute | solution.py:115
  129.0 1.0 copy-start.5
  130.0 13.7 %collective-permute-start.9 = (bf16[1,32,32,128]{3,1,2,0:T(8,128)(2,1)S(1)}, bf16[1,32,32,128]{3,1,2,0:T(8,128)(2,1)S(1)}, u32[]{:S(2)}, u32[]{:S(2)}) collective-permute-start(bf16[1,32,32,128]{3,1,2,0:T(8,128)(2,1)S(1)} %fusion.32), channel_id=1, source_target_pairs={{0,8},{2,10},{4,12},{6,14},{8,0},{10,2},{12,4},{14,6},{1,9},{3,11}... | collective-permute-start | bytes 786440 | tf_op jit(solution)/shard_map/ppermute | solution.py:115

commit v14 on v11

--- a/solution.py
+++ b/solution.py
@@ -122,6 +122,7 @@
         (pair[:, 1] * to_column).astype(jnp.bfloat16), "dp", [(j, j ^ 1) for j in range(dp_count)]
     )
     held = pair[:, 0] * to_column + arrived.astype(jnp.float32)
+    held, teacher_stats = lax.optimization_barrier((held, teacher_stats))
     bits = list(range(1, dp_count.bit_length() - 1))
     half = tokens_all // 2
     first = reduce_bits(held[:, :, :half], bits, True)

time: 180 us -> 183 us (1.017)
  waiting for transfers between devices: 43.8 us -> 48.6 us
  starting transfers between devices: 17.8 us -> 14.2 us
  blocking collectives: 38.3 us -> 35.4 us
  local copies, waits for them, and re-layouts: 5.6 us -> 8.42 us
  other arithmetic: 9.95 us -> 12.4 us
    ppermute x4, waiting for transfers between devices: 32.8 us -> 38.2 us  [reduce_bits(): lax.ppermute(send.astype(jnp.bfloat16), 'dp', pairs).astype(jnp.float32)]
    ppermute x3, waiting for transfers between devices: 7.61 us -> 3.64 us  [on_device(): lax.ppermute(teacher_stats, 'dp', pairs)]
    ppermute x3, waiting for transfers between devices: 3.38 us -> 6.75 us  [on_device(): lax.ppermute(student_stats, 'dp', pairs)]
    ppermute x4, starting transfers between devices: 3.61 us -> 0.5 us  [reduce_bits(): lax.ppermute(send.astype(jnp.bfloat16), 'dp', pairs).astype(jnp.float32)]
    all_to_all x1, blocking collectives: 21.5 us -> 18.6 us  [on_device(): lax.all_to_all(partial, ('dp', 'vocab'), split_axis=0, concat_axis=0, til...]
    unnamed x11 -> x13, local copies, waits for them, and re-layouts: 3.86 us -> 4.93 us
  transfers between devices with their start and end apart: 14 -> 14, of which waited for: 5 -> 7; matrix products, arithmetic and copies ran while one was open for 18% -> 20% of each run, Pallas kernels for 0% -> 0%
where the time goes in v14:
time: 183 us
  matrix products  63.5 us (35%)
  waiting for transfers between devices  48.6 us (27%)
  blocking collectives  35.4 us (19%)
  starting transfers between devices  14.2 us (8%)
  other arithmetic  12.4 us (7%)
  local copies, waits for them, and re-layouts  8.42 us (5%)
    ppermute x4, waiting for transfers between devices, reduce_bits(): lax.ppermute(send.astype(jnp.bfloat16), 'dp', pairs).astype(jnp.float32)  38.2 us
    dot_general x1, matrix products, on_device(): jnp.dot(teacher_all, teacher_head, preferred_element_type=jnp.float32)  23.4 us
    all_to_all x1, blocking collectives, on_device(): lax.all_to_all(partial, ('dp', 'vocab'), split_axis=0, concat_axis=0, til...  18.6 us
    all_gather x1, blocking collectives, on_device(): gathered = lax.all_gather(packed, 'dp', axis=0, tiled=True)  16.8 us
    dot_general x1, matrix products, on_device(): lax.dot_general(logit_grad, student_head, (((1,), (1,)), ((), ())), prefe...  16.6 us
    dot_general x1, matrix products, on_device(): jnp.dot(student_all, student_head, preferred_element_type=jnp.float32)  13.8 us
    ppermute x3, waiting for transfers between devices, on_device(): lax.ppermute(student_stats, 'dp', pairs)  6.75 us
    dot_general x1, matrix products, on_device(): jnp.dot(placement, mapped_terms.reshape(item_count, tokens_all * block_si...  5.68 us
  transfers between devices with their start and end apart: 14, of which 7 were waited for; matrix products, arithmetic and copies ran while one was open for 20% of the time, Pallas kernels for 0%

profile of v14, /device:TPU:1, one launch (start us, length us, event | category | flops | bytes accessed | tf_op | source)
XLA Modules:
  0.0 182.8 jit_solution(6724085573903572809)
XLA Ops:
  0.0 0.7 convert_convert_fusion
  0.7 0.1 fusion.40
  0.7 0.9 pad_maximum_fusion
  1.6 16.8 %all_gather.3 = bf16[64,5248]{1,0:T(8,128)(2,1)S(1)} all-gather(bf16[8,5248]{1,0:T(8,128)(2,1)S(1)} %pad_maximum_fusion), channel_id=1, replica_groups=mesh['groups'=2,'dp'=8,'vocab'=2] {'dp'}, dimensions={0}, use_global_device_ids=true | all-gather | bytes 755712 | tf_op jit(solution)/shard_map/all_gather | solution.py:50
  18.5 23.4 %fusion.63 = (f32[64]{0:T(128)S(1)}, f32[64,6144]{1,0:T(8,128)S(1)}) fusion(bf16[5120,6144]{1,0:T(8,128)(2,1)} %param.9, bf16[64,5248]{1,0:T(8,128)(2,1)S(1)} %all_gather.3), kind=kOutput, calls=%fused_computation.133 | convolution fusion | flops 4026925056 | bytes 65143040 | tf_op jit(solution)/shard_map/dot_general | solution.py:62
  41.9 0.3 fusion.14
  42.2 0.1 copy.30
  42.3 0.0 copy-start.2
  42.3 0.0 copy-start.3
  42.3 0.0 copy-start.4
  42.3 4.0 %convert_reduce_fusion = (f32[64]{0:T(128)S(1)}, bf16[48,64,4,128]{3,1,2,0:T(8,128)(2,1)S(1)}) fusion(bf16[48,4,128,128]{3,2,1,0:T(8,128)(2,1)} %param.12, bf16[64,48,128,1]{2,1,0,3:T(8,128)(2,1)S(1)} %bitcast.225), kind=kOutput, calls=%fused_computation | convolution fusion | flops 407371712 | bytes 10223872 | tf_op jit(solution)/shard_map/gkc,krcd->krgd/dot_general | solution.py:66
  46.3 0.2 collective-permute-start.4
  46.5 0.8 broadcast_in_dim.2
  47.4 5.0 %all-to-all-start = ((bf16[8,8,4096]{2,1,0:T(8,128)(2,1)}), bf16[8,8,4096]{2,1,0:T(8,128)(2,1)}, u32[]{:S(2)}, u32[]{:S(2)}) async-start(bf16[8,8,4096]{2,1,0:T(8,128)(2,1)} %broadcast_in_dim.2), calls=%async_computation | async-start | bytes 1048576 | tf_op jit(solution)/shard_map/all_to_all | solution.py:51
  52.4 0.0 collective-permute-done.4
  52.4 1.4 collective-permute-start.5
  53.9 2.8 %copy.53 = bf16[24,8,64,128]{3,1,2,0:T(8,128)(2,1)S(1)} copy(bf16[24,8,64,128]{3,2,1,0:T(8,128)(2,1)S(1)} %bitcast.220) | data formatting | bytes 6291456
  56.7 0.9 copy.32
  57.6 0.1 copy.11
  57.7 0.1 add.128
  57.8 3.6 %collective-permute-done.5 = f32[2,64]{1,0:T(2,128)S(1)} collective-permute-done((f32[2,64]{1,0:T(2,128)S(1)}, f32[2,64]{1,0:T(2,128)S(1)}, u32[]{:S(2)}, u32[]{:S(2)}) %collective-permute-start.5) | collective-permute-done | bytes 544 | tf_op jit(solution)/shard_map/ppermute | solution.py:99
  61.5 4.0 %collective-permute-start.6 = (f32[2,64]{1,0:T(2,128)S(1)}, f32[2,64]{1,0:T(2,128)S(1)}, u32[]{:S(2)}, u32[]{:S(2)}) collective-permute-start(f32[2,64]{1,0:T(2,128)S(1)} %pad_maximum_fusion.7), channel_id=1, source_target_pairs={{0,8},{2,10},{4,12},{6,14},{8,0},{10,2},{12,4},{14,6},{1,9},{3,11}... | collective-permute-start | bytes 1544 | tf_op jit(solution)/shard_map/ppermute | solution.py:99
  65.4 5.7 %fusion.4 = f32[4,2,32,64,128]{4,2,3,1,0:T(8,128)} fusion(bf16[64,128,192,1,1]{1,0,2,4,3:T(8,128)(2,1)S(1)} %bitcast.221, s32[192]{0:T(256)S(1)} %add.128, s32[4,2,32]{2,1,0:T(2,128)S(1)} %multiply_add_fusion), kind=kOutput, calls=%fused_computation.9 | convolution fusion | flops 805355520 | bytes 11536128 | tf_op jit(solution)/shard_map/dot_general | solution.py:76
  71.1 0.0 collective-permute-done.6
  71.2 2.6 %fusion.1 = bf16[4,32,64,128]{3,1,2,0:T(8,128)(2,1)S(1)} fusion(f32[4,2,32,64,128]{4,2,3,1,0:T(8,128)} %fusion.4, f32[64]{0:T(128)S(1)} %get-tuple-element.15), kind=kLoop, calls=%fused_computation.4 | loop fusion | flops 2097152 | bytes 6291712 | tf_op jit(solution)/shard_map/convert_element_type | solution.py:122
  73.8 1.2 collective-permute-start.7
  75.0 0.0 all-to-all-done
  75.0 13.8 %fusion.64 = (f32[64]{0:T(128)S(1)}, f32[64,4096]{1,0:T(8,128)S(1)}) fusion(bf16[4096,4096]{1,0:T(8,128)(2,1)} %param.14, bf16[8,8,4096]{2,1,0:T(8,128)(2,1)} %all-to-all-done), kind=kOutput, calls=%fused_computation.134 | convolution fusion | flops 2147745792 | bytes 35127552 | tf_op jit(solution)/shard_map/dot_general | solution.py:82
  88.8 0.3 exponential_reduce_fusion
  89.2 0.1 collective-permute-start
  89.3 0.1 convert_add_fusion.1
  89.3 1.1 collective-permute-done
  90.4 0.1 collective-permute-start.1
  90.5 2.4 %collective-permute-done.1 = f32[2,64]{1,0:T(2,128)S(1)} collective-permute-done((f32[2,64]{1,0:T(2,128)S(1)}, f32[2,64]{1,0:T(2,128)S(1)}, u32[]{:S(2)}, u32[]{:S(2)}) %collective-permute-start.1) | collective-permute-done | bytes 544 | tf_op jit(solution)/shard_map/ppermute | solution.py:100
  92.9 0.1 collective-permute-start.2
  93.0 3.3 %collective-permute-done.2 = f32[2,64]{1,0:T(2,128)S(1)} collective-permute-done((f32[2,64]{1,0:T(2,128)S(1)}, f32[2,64]{1,0:T(2,128)S(1)}, u32[]{:S(2)}, u32[]{:S(2)}) %collective-permute-start.2) | collective-permute-done | bytes 544 | tf_op jit(solution)/shard_map/ppermute | solution.py:100
  96.4 1.3 collective-permute-start.3
  97.6 0.0 collective-permute-done.7
  97.6 3.3 %fusion.3 = f32[4,32,64,128]{3,1,2,0:T(8,128)S(1)} fusion(f32[4,2,32,64,128]{4,2,3,1,0:T(8,128)} %fusion.4, bf16[4,32,64,128]{3,1,2,0:T(8,128)(2,1)} %collective-permute-done.7, f32[64]{0:T(128)S(1)} %get-tuple-element.15), kind=kLoop, calls=%fused_computation.7 | loop fusion | flops 3145728 | bytes 10486016 | tf_op jit(solution)/shard_map/add | solution.py:124
  101.0 1.0 slice.232
  102.0 1.1 copy-done
  103.1 0.2 slice.136
  103.3 0.1 collective-permute-start.10
  103.4 0.9 fusion.19
  104.2 0.3 collective-permute-start.8
  104.5 0.1 eq.56
  104.6 0.0 collective-permute-done.3
  104.6 0.3 collective-permute-start.12
  105.0 24.4 %collective-permute-done.10 = bf16[2,32,32,128]{3,1,2,0:T(8,128)(2,1)} collective-permute-done((bf16[2,32,32,128]{3,1,2,0:T(8,128)(2,1)}, bf16[2,32,32,128]{3,1,2,0:T(8,128)(2,1)}, u32[]{:S(2)}, u32[]{:S(2)}) %collective-permute-start.10) | collective-permute-done | bytes 524320 | tf_op jit(solution)/shard_map/ppermute | solution.py:115
  129.4 1.6 convert_add_fusion
  131.0 0.1 collective-permute-start.11
  131.1 0.0 collective-permute-done.8
  131.1 1.2 fusion.11
  132.4 0.1 collective-permute-start.9
  132.5 0.0 collective-permute-done.12
  132.5 8.3 %collective-permute-done.11 = bf16[1,32,32,128]{3,1,2,0:T(8,128)(2,1)S(1)} collective-permute-done((bf16[1,32,32,128]{3,1,2,0:T(8,128)(2,1)S(1)}, bf16[1,32,32,128]{3,1,2,0:T(8,128)(2,1)S(1)}, u32[]{:S(2)}, u32[]{:S(2)}) %collective-permute-start.11) | collective-permute-done | bytes 262176 | tf_op jit(solution)/shard_map/ppermute | solution.py:115
  140.8 0.1 slice_add_fusion
  140.9 5.5 %collective-permute-done.9 = bf16[1,32,32,128]{3,1,2,0:T(8,128)(2,1)S(1)} collective-permute-done((bf16[1,32,32,128]{3,1,2,0:T(8,128)(2,1)S(1)}, bf16[1,32,32,128]{3,1,2,0:T(8,128)(2,1)S(1)}, u32[]{:S(2)}, u32[]{:S(2)}) %collective-permute-start.9) | collective-permute-done | bytes 262176 | tf_op jit(solution)/shard_map/ppermute | solution.py:115
  146.4 0.1 fusion.20
  146.5 0.1 fusion.12
  146.6 16.6 %convolution_convert_fusion = bf16[64,4096]{1,0:T(8,128)(2,1)S(1)} fusion(bf16[4096,4096]{1,0:T(8,128)(2,1)} %param.14, f32[8,8,32,128]{3,2,1,0:T(8,128)S(1)} %bitcast.224, f32[64,4096]{1,0:T(8,128)S(1)} %get-tuple-element.34, s32[4096]{0:T(1024)S(1)} %iota_add_fusion, f32[64]{0:T(128)S(1)} %get-tuple-element.21, f32[64]{0:T(128)S(1)} %get-tuple-element.9, ...), kind=kOutput, calls=%fused_computation.1 | convolution fusion | flops 2150367232 | bytes 36193280 | tf_op jit(solution)/shard_map/dot_general | solution.py:152
  163.2 0.2 reshape.299
  163.4 18.6 %all_to_all.10 = bf16[16,4,4096]{2,1,0:T(4,128)(2,1)S(1)} all-to-all(bf16[16,4,4096]{2,1,0:T(4,128)(2,1)S(1)} %reshape.299), channel_id=1, replica_groups=mesh['groups'=2,'dp'=8,'vocab'=2] {'dp','vocab'}, dimensions={0} | all-to-all | bytes 1048576 | tf_op jit(solution)/shard_map/all_to_all | solution.py:157
  182.0 0.8 reduce_sum.32
  (31 shorter events, 0.3 us)
Async XLA Ops:
  18.5 23.4 %copy-start.1 = (bf16[64,5248]{1,0:T(8,128)(2,1)}, bf16[64,5248]{1,0:T(8,128)(2,1)S(1)}, u32[]{:S(2)}) copy-start(bf16[64,5248]{1,0:T(8,128)(2,1)S(1)} %all_gather.3) | copy-start | bytes 2015236
  42.3 4.3 %copy-start.2 = (bf16[8,4096]{1,0:T(8,128)(2,1)S(1)}, bf16[8,4096]{1,0:T(8,128)(2,1)}, u32[]{:S(2)}) copy-start(bf16[8,4096]{1,0:T(8,128)(2,1)} %param.13) | copy-start | bytes 196612
  42.3 10.1 %copy-start.3 = (s32[48,4]{0,1:T(4,128)S(1)}, s32[48,4]{0,1:T(4,128)}, u32[]{:S(2)}) copy-start(s32[48,4]{0,1:T(4,128)} %param.11) | copy-start | bytes 2308
  42.3 10.1 %copy-start.4 = (s32[48,4]{0,1:T(4,128)S(1)}, s32[48,4]{0,1:T(4,128)}, u32[]{:S(2)}) copy-start(s32[48,4]{0,1:T(4,128)} %param.10) | copy-start | bytes 2308
  46.3 6.1 %collective-permute-start.4 = (f32[2,64]{1,0:T(2,128)S(1)}, f32[2,64]{1,0:T(2,128)S(1)}, u32[]{:S(2)}, u32[]{:S(2)}) collective-permute-start(f32[2,64]{1,0:T(2,128)S(1)} %pad_maximum_fusion.5), channel_id=1, source_target_pairs={{0,2},{2,0},{4,6},{6,4},{8,10},{10,8},{12,14},{14,12},{1,3},{3,1},... | collective-permute-start | bytes 1544 | tf_op jit(solution)/shard_map/ppermute | solution.py:99
  47.4 27.6 %all-to-all-start = ((bf16[8,8,4096]{2,1,0:T(8,128)(2,1)}), bf16[8,8,4096]{2,1,0:T(8,128)(2,1)}, u32[]{:S(2)}, u32[]{:S(2)}) async-start(bf16[8,8,4096]{2,1,0:T(8,128)(2,1)} %broadcast_in_dim.2), calls=%async_computation | async-start | bytes 1048576 | tf_op jit(solution)/shard_map/all_to_all | solution.py:51
  52.4 9.0 %collective-permute-start.5 = (f32[2,64]{1,0:T(2,128)S(1)}, f32[2,64]{1,0:T(2,128)S(1)}, u32[]{:S(2)}, u32[]{:S(2)}) collective-permute-start(f32[2,64]{1,0:T(2,128)S(1)} %pad_maximum_fusion.6), channel_id=1, source_target_pairs={{0,4},{2,6},{4,0},{6,2},{8,12},{10,14},{12,8},{14,10},{1,5},{3,7},... | collective-permute-start | bytes 1544 | tf_op jit(solution)/shard_map/ppermute | solution.py:99
  61.5 9.7 %collective-permute-start.6 = (f32[2,64]{1,0:T(2,128)S(1)}, f32[2,64]{1,0:T(2,128)S(1)}, u32[]{:S(2)}, u32[]{:S(2)}) collective-permute-start(f32[2,64]{1,0:T(2,128)S(1)} %pad_maximum_fusion.7), channel_id=1, source_target_pairs={{0,8},{2,10},{4,12},{6,14},{8,0},{10,2},{12,4},{14,6},{1,9},{3,11}... | collective-permute-start | bytes 1544 | tf_op jit(solution)/shard_map/ppermute | solution.py:99
  65.4 5.7 %slice-start = ((bf16[64,5248]{1,0:T(8,128)(2,1)}), bf16[64,128]{1,0:T(8,128)(2,1)S(1)}, s32[]{:S(2)}) async-start(bf16[64,5248]{1,0:T(8,128)(2,1)} %copy-done.1), calls=%async_computation.2 | async-start | bytes 32768 | tf_op jit(solution)/shard_map/slice | solution.py:57
  73.8 23.9 %collective-permute-start.7 = (bf16[4,32,64,128]{3,1,2,0:T(8,128)(2,1)S(1)}, bf16[4,32,64,128]{3,1,2,0:T(8,128)(2,1)}, u32[]{:S(2)}, u32[]{:S(2)}) collective-permute-start(bf16[4,32,64,128]{3,1,2,0:T(8,128)(2,1)S(1)} %fusion.1), channel_id=1, source_target_pairs={{0,2},{2,0},{4,6},{6,4},{8,10},{10,8},{12,14},{14,12},{1,3},{3,1},... | collective-permute-start | bytes 6291464 | tf_op jit(solution)/shard_map/ppermute | solution.py:121
  89.2 1.2 collective-permute-start
  90.4 2.5 %collective-permute-start.1 = (f32[2,64]{1,0:T(2,128)S(1)}, f32[2,64]{1,0:T(2,128)S(1)}, u32[]{:S(2)}, u32[]{:S(2)}) collective-permute-start(f32[2,64]{1,0:T(2,128)S(1)} %pad_maximum_fusion.2), channel_id=1, source_target_pairs={{0,4},{2,6},{4,0},{6,2},{8,12},{10,14},{12,8},{14,10},{1,5},{3,7},... | collective-permute-start | bytes 1544 | tf_op jit(solution)/shard_map/ppermute | solution.py:100
  92.9 3.4 %collective-permute-start.2 = (f32[2,64]{1,0:T(2,128)S(1)}, f32[2,64]{1,0:T(2,128)S(1)}, u32[]{:S(2)}, u32[]{:S(2)}) collective-permute-start(f32[2,64]{1,0:T(2,128)S(1)} %pad_maximum_fusion.3), channel_id=1, source_target_pairs={{0,8},{2,10},{4,12},{6,14},{8,0},{10,2},{12,4},{14,6},{1,9},{3,11}... | collective-permute-start | bytes 1544 | tf_op jit(solution)/shard_map/ppermute | solution.py:100
  96.4 8.3 %collective-permute-start.3 = (f32[2,64]{1,0:T(2,128)S(1)}, f32[2,64]{1,0:T(2,128)S(1)}, u32[]{:S(2)}, u32[]{:S(2)}) collective-permute-start(f32[2,64]{1,0:T(2,128)S(1)} %pad_maximum_fusion.4), channel_id=1, source_target_pairs={{0,1},{1,0},{2,3},{3,2},{4,5},{5,4},{6,7},{7,6},{8,9},{9,8},{10,11... | collective-permute-start | bytes 1544 | tf_op jit(solution)/shard_map/ppermute | solution.py:136
  101.0 2.1 %copy-start = (f32[4,32,64,128]{3,1,2,0:T(8,128)}, f32[4,32,64,128]{3,1,2,0:T(8,128)S(1)}, u32[]{:S(2)}) copy-start(f32[4,32,64,128]{3,1,2,0:T(8,128)S(1)} %fusion.3) | copy-start | bytes 12582916
  103.3 26.1 %collective-permute-start.10 = (bf16[2,32,32,128]{3,1,2,0:T(8,128)(2,1)}, bf16[2,32,32,128]{3,1,2,0:T(8,128)(2,1)}, u32[]{:S(2)}, u32[]{:S(2)}) collective-permute-start(bf16[2,32,32,128]{3,1,2,0:T(8,128)(2,1)} %slice.232), channel_id=1, source_target_pairs={{0,8},{2,10},{4,12},{6,14},{8,0},{10,2},{12,4},{14,6},{1,9},{3,11}... | collective-permute-start | bytes 1572872 | tf_op jit(solution)/shard_map/ppermute | solution.py:115
  104.2 26.9 %collective-permute-start.8 = (bf16[2,32,32,128]{3,1,2,0:T(8,128)(2,1)}, bf16[2,32,32,128]{3,1,2,0:T(8,128)(2,1)}, u32[]{:S(2)}, u32[]{:S(2)}) collective-permute-start(bf16[2,32,32,128]{3,1,2,0:T(8,128)(2,1)} %fusion.19), channel_id=1, source_target_pairs={{0,4},{2,6},{4,0},{6,2},{8,12},{10,14},{12,8},{14,10},{1,5},{3,7},... | collective-permute-start | bytes 1572872 | tf_op jit(solution)/shard_map/ppermute | solution.py:115
  104.6 27.8 %collective-permute-start.12 = (f32[2,64]{1,0:T(2,128)S(1)}, f32[2,64]{1,0:T(2,128)S(1)}, u32[]{:S(2)}, u32[]{:S(2)}) collective-permute-start(f32[2,64]{1,0:T(2,128)S(1)} %pad_maximum_fusion.8), channel_id=1, source_target_pairs={{0,1},{1,0},{2,3},{3,2},{4,5},{5,4},{6,7},{7,6},{8,9},{9,8},{10,11... | collective-permute-start | bytes 1544 | tf_op jit(solution)/shard_map/ppermute | solution.py:135
  131.0 9.8 %collective-permute-start.11 = (bf16[1,32,32,128]{3,1,2,0:T(8,128)(2,1)S(1)}, bf16[1,32,32,128]{3,1,2,0:T(8,128)(2,1)S(1)}, u32[]{:S(2)}, u32[]{:S(2)}) collective-permute-start(bf16[1,32,32,128]{3,1,2,0:T(8,128)(2,1)S(1)} %slice.233), channel_id=1, source_target_pairs={{0,4},{2,6},{4,0},{6,2},{8,12},{10,14},{12,8},{14,10},{1,5},{3,7},... | collective-permute-start | bytes 786440 | tf_op jit(solution)/shard_map/ppermute | solution.py:115
  132.4 14.0 %collective-permute-start.9 = (bf16[1,32,32,128]{3,1,2,0:T(8,128)(2,1)S(1)}, bf16[1,32,32,128]{3,1,2,0:T(8,128)(2,1)S(1)}, u32[]{:S(2)}, u32[]{:S(2)}) collective-permute-start(bf16[1,32,32,128]{3,1,2,0:T(8,128)(2,1)S(1)} %fusion.32), channel_id=1, source_target_pairs={{0,8},{2,10},{4,12},{6,14},{8,0},{10,2},{12,4},{14,6},{1,9},{3,11}... | collective-permute-start | bytes 786440 | tf_op jit(solution)/shard_map/ppermute | solution.py:115

commit v15 on v11

--- a/solution.py
+++ b/solution.py
@@ -48,10 +48,10 @@
         [teacher_hidden, coded.reshape(local_tokens, extra_width)], axis=1
     )
     gathered = lax.all_gather(packed, "dp", axis=0, tiled=True)
-    student_all = lax.all_to_all(
-        jnp.broadcast_to(student_hidden[None], (dp_count,) + student_hidden.shape),
-        "dp", split_axis=0, concat_axis=0, tiled=True,
-    ).reshape(dp_count * local_tokens, student_width)
+    student_all = lax.all_gather(
+        jnp.pad(student_hidden, ((0, 0), (0, teacher_width + extra_width))),
+        "dp", axis=0, tiled=True,
+    )[:, :student_width]
     tokens_all = gathered.shape[0]
     teacher_all = gathered[:, :teacher_width]
     extra_all = gathered[:, teacher_width:].reshape(dp_count, local_tokens * extra_width)

time: 180 us -> 186 us (1.033)
  between operations: 0.33 us -> 13.7 us
  waiting for transfers between devices: 43.8 us -> 39.6 us
  starting transfers between devices: 17.8 us -> 14.6 us
    ppermute x3, waiting for transfers between devices: 7.61 us -> 1.51 us  [on_device(): lax.ppermute(teacher_stats, 'dp', pairs)]
    all_to_all x1 -> x0, starting transfers between devices: 5.01 us -> none  [on_device(): lax.all_to_all(jnp.broadcast_to(student_hidden[None], (dp_count,) + stude...]
    all_gather x0 -> x1, waiting for transfers between devices: none -> 3.98 us  [on_device(): lax.all_gather(jnp.pad(student_hidden, ((0, 0), (0, teacher_width + extra...]
    ppermute x3, starting transfers between devices: 0.46 us -> 2.87 us  [on_device(): lax.ppermute(student_stats, 'dp', pairs)]
    ppermute x3, starting transfers between devices: 5.61 us -> 3.49 us  [on_device(): lax.ppermute(teacher_stats, 'dp', pairs)]
  transfers between devices with their start and end apart: 14 -> 14, of which waited for: 5 -> 7; matrix products, arithmetic and copies ran while one was open for 18% -> 17% of each run, Pallas kernels for 0% -> 0%
where the time goes in v15:
time: 186 us
  matrix products  63.3 us (34%)
  waiting for transfers between devices  39.6 us (21%)
  blocking collectives  39.4 us (21%)
  starting transfers between devices  14.6 us (8%)
  between operations  13.7 us (7%)
  other arithmetic  9.97 us (5%)
  local copies, waits for them, and re-layouts  5.45 us (3%)
    ppermute x4, waiting for transfers between devices, reduce_bits(): lax.ppermute(send.astype(jnp.bfloat16), 'dp', pairs).astype(jnp.float32)  31.9 us
    dot_general x1, matrix products, on_device(): jnp.dot(teacher_all, teacher_head, preferred_element_type=jnp.float32)  23.4 us
    all_to_all x1, blocking collectives, on_device(): lax.all_to_all(partial, ('dp', 'vocab'), split_axis=0, concat_axis=0, til...  22.6 us
    all_gather x1, blocking collectives, on_device(): gathered = lax.all_gather(packed, 'dp', axis=0, tiled=True)  16.8 us
    dot_general x1, matrix products, on_device(): lax.dot_general(logit_grad, student_head, (((1,), (1,)), ((), ())), prefe...  16.4 us
    dot_general x1, matrix products, on_device(): jnp.dot(student_all, student_head, preferred_element_type=jnp.float32)  13.8 us
    dot_general x1, matrix products, on_device(): jnp.dot(placement, mapped_terms.reshape(item_count, tokens_all * block_si...  5.68 us
    ppermute x4, starting transfers between devices, reduce_bits(): lax.ppermute(send.astype(jnp.bfloat16), 'dp', pairs).astype(jnp.float32)  4.06 us
  transfers between devices with their start and end apart: 14, of which 7 were waited for; matrix products, arithmetic and copies ran while one was open for 17% of the time, Pallas kernels for 0%

profile of v15, /device:TPU:1, one launch (start us, length us, event | category | flops | bytes accessed | tf_op | source)
XLA Modules:
  0.0 185.9 jit_solution(7863535924720454595)
XLA Ops:
  6.5 0.0 all-gather.2.cloned.1.call-start
  6.5 0.7 convert_convert_fusion
  7.2 0.1 fusion.40
  7.3 0.9 pad_maximum_fusion
  8.2 16.8 %all_gather.7 = bf16[64,5248]{1,0:T(8,128)(2,1)S(1)} all-gather(bf16[8,5248]{1,0:T(8,128)(2,1)S(1)} %pad_maximum_fusion), channel_id=1, replica_groups=mesh['groups'=2,'dp'=8,'vocab'=2] {'dp'}, dimensions={0}, use_global_device_ids=true | all-gather | bytes 755712 | tf_op jit(solution)/shard_map/all_gather | solution.py:50
  25.0 23.4 %fusion.71 = (f32[64]{0:T(128)S(1)}, f32[64,6144]{1,0:T(8,128)S(1)}) fusion(bf16[5120,6144]{1,0:T(8,128)(2,1)} %param.9, bf16[64,5248]{1,0:T(8,128)(2,1)S(1)} %all_gather.7), kind=kOutput, calls=%fused_computation.144 | convolution fusion | flops 4026925056 | bytes 65143040 | tf_op jit(solution)/shard_map/dot_general | solution.py:62
  48.4 0.3 fusion.14
  48.7 0.1 copy.30
  48.8 0.0 copy-start.1
  48.8 0.0 copy-start.2
  48.8 0.0 copy-start.3
  48.8 4.0 %convert_reduce_fusion = (f32[64]{0:T(128)S(1)}, bf16[48,64,4,128]{3,1,2,0:T(8,128)(2,1)S(1)}) fusion(bf16[48,4,128,128]{3,2,1,0:T(8,128)(2,1)} %param.12, bf16[64,48,128,1]{2,1,0,3:T(8,128)(2,1)S(1)} %bitcast.240), kind=kOutput, calls=%fused_computation | convolution fusion | flops 407371712 | bytes 10223872 | tf_op jit(solution)/shard_map/gkc,krcd->krgd/dot_general | solution.py:66
  52.8 0.2 collective-permute-start.4
  53.1 0.7 pad.8
  53.7 0.0 all-gather.2.cloned.1.call-update
  53.8 0.3 collective-permute-done.4
  54.1 1.3 collective-permute-start.5
  55.4 1.2 collective-permute-done.5
  56.6 2.0 %collective-permute-start.6 = (f32[2,64]{1,0:T(2,128)S(1)}, f32[2,64]{1,0:T(2,128)S(1)}, u32[]{:S(2)}, u32[]{:S(2)}) collective-permute-start(f32[2,64]{1,0:T(2,128)S(1)} %pad_maximum_fusion.7), channel_id=1, source_target_pairs={{0,8},{2,10},{4,12},{6,14},{8,0},{10,2},{12,4},{14,6},{1,9},{3,11}... | collective-permute-start | bytes 1544 | tf_op jit(solution)/shard_map/ppermute | solution.py:99
  58.6 2.8 %copy.53 = bf16[24,8,64,128]{3,1,2,0:T(8,128)(2,1)S(1)} copy(bf16[24,8,64,128]{3,2,1,0:T(8,128)(2,1)S(1)} %bitcast.235) | data formatting | bytes 6291456
  61.5 0.9 copy.32
  62.4 0.1 copy.11
  62.4 0.1 add.148
  62.6 0.0 collective-permute-done.6
  62.6 1.3 collective-permute-start.12
  63.9 5.7 %fusion.4 = f32[4,2,32,64,128]{4,2,3,1,0:T(8,128)} fusion(bf16[64,128,192,1,1]{1,0,2,4,3:T(8,128)(2,1)S(1)} %bitcast.236, s32[192]{0:T(256)S(1)} %add.148, s32[4,2,32]{2,1,0:T(2,128)S(1)} %multiply_add_fusion), kind=kOutput, calls=%fused_computation.9 | convolution fusion | flops 805355520 | bytes 11536128 | tf_op jit(solution)/shard_map/dot_general | solution.py:76
  69.6 0.0 collective-permute-done.12
  69.6 2.6 %fusion.1 = bf16[4,32,64,128]{3,1,2,0:T(8,128)(2,1)S(1)} fusion(f32[4,2,32,64,128]{4,2,3,1,0:T(8,128)} %fusion.4, f32[64]{0:T(128)S(1)} %get-tuple-element.22), kind=kLoop, calls=%fused_computation.4 | loop fusion | flops 2097152 | bytes 6291712 | tf_op jit(solution)/shard_map/convert_element_type | solution.py:122
  72.3 1.7 collective-permute-start.7
  73.9 4.0 %all-gather.2.cloned.1.call-done = bf16[64,9344]{1,0:T(8,128)(2,1)} async-done(((bf16[8,9344]{1,0:T(8,128)(2,1)}), bf16[64,9344]{1,0:T(8,128)(2,1)}) %all-gather.2.cloned.1.call-update) | async-done | bytes 1196048 | tf_op jit(solution)/shard_map/all_gather | solution.py:51
  77.9 13.8 %fusion.72 = (f32[64]{0:T(128)S(1)}, f32[64,4096]{1,0:T(8,128)S(1)}) fusion(bf16[4096,4096]{1,0:T(8,128)(2,1)} %param.14, bf16[64,9344]{1,0:T(8,128)(2,1)} %all-gather.2.cloned.1.call-done), kind=kOutput, calls=%fused_computation.145 | convolution fusion | flops 2147745792 | bytes 35127552 | tf_op jit(solution)/shard_map/dot_general | solution.py:82
  91.8 0.3 exponential_reduce_fusion
  92.1 0.3 collective-permute-start
  92.4 0.1 convert_add_fusion
  92.5 0.8 collective-permute-done
  93.4 1.0 collective-permute-start.1
  94.4 0.1 eq.56
  94.5 1.4 collective-permute-done.1
  95.9 1.5 collective-permute-start.2
  97.4 0.0 collective-permute-done.7
  97.4 3.3 %fusion.3 = f32[4,32,64,128]{3,1,2,0:T(8,128)S(1)} fusion(f32[4,2,32,64,128]{4,2,3,1,0:T(8,128)} %fusion.4, bf16[4,32,64,128]{3,1,2,0:T(8,128)(2,1)} %collective-permute-done.7, f32[64]{0:T(128)S(1)} %get-tuple-element.22), kind=kLoop, calls=%fused_computation.7 | loop fusion | flops 3145728 | bytes 10486016 | tf_op jit(solution)/shard_map/add | solution.py:124
  100.8 0.1 slice.237
  100.9 0.2 slice.151
  101.0 1.0 collective-permute-start.10
  102.0 0.1 fusion.19
  102.1 1.0 collective-permute-start.8
  103.1 0.0 collective-permute-done.2
  103.2 1.2 collective-permute-start.3
  104.4 22.4 %collective-permute-done.10 = bf16[2,32,32,128]{3,1,2,0:T(8,128)(2,1)S(1)} collective-permute-done((bf16[2,32,32,128]{3,1,2,0:T(8,128)(2,1)S(1)}, bf16[2,32,32,128]{3,1,2,0:T(8,128)(2,1)S(1)}, u32[]{:S(2)}, u32[]{:S(2)}) %collective-permute-start.10) | collective-permute-done | bytes 524320 | tf_op jit(solution)/shard_map/ppermute | solution.py:115
  126.8 0.2 slice_add_fusion
  127.0 0.1 collective-permute-start.11
  127.1 0.0 collective-permute-done.8
  127.1 0.2 fusion.11
  127.3 2.0 %collective-permute-start.9 = (bf16[1,32,32,128]{3,1,2,0:T(8,128)(2,1)S(1)}, bf16[1,32,32,128]{3,1,2,0:T(8,128)(2,1)S(1)}, u32[]{:S(2)}, u32[]{:S(2)}) collective-permute-start(bf16[1,32,32,128]{3,1,2,0:T(8,128)(2,1)S(1)} %fusion.32), channel_id=1, source_target_pairs={{0,8},{2,10},{4,12},{6,14},{8,0},{10,2},{12,4},{14,6},{1,9},{3,11}... | collective-permute-start | bytes 786440 | tf_op jit(solution)/shard_map/ppermute | solution.py:115
  129.3 0.0 collective-permute-done.3
  129.3 9.5 %collective-permute-done.11 = bf16[1,32,32,128]{3,1,2,0:T(8,128)(2,1)S(1)} collective-permute-done((bf16[1,32,32,128]{3,1,2,0:T(8,128)(2,1)S(1)}, bf16[1,32,32,128]{3,1,2,0:T(8,128)(2,1)S(1)}, u32[]{:S(2)}, u32[]{:S(2)}) %collective-permute-start.11) | collective-permute-done | bytes 262176 | tf_op jit(solution)/shard_map/ppermute | solution.py:115
  138.8 0.1 slice_add_fusion.1
  138.9 0.0 collective-permute-done.9
  138.9 0.1 fusion.20
  139.0 0.1 fusion.12
  139.1 16.4 %convolution_convert_fusion = bf16[64,4096]{1,0:T(8,128)(2,1)S(1)} fusion(bf16[4096,4096]{1,0:T(8,128)(2,1)} %param.14, f32[8,8,32,128]{3,2,1,0:T(8,128)S(1)} %bitcast.239, f32[64,4096]{1,0:T(8,128)S(1)} %get-tuple-element.30, s32[4096]{0:T(1024)S(1)} %iota_add_fusion, f32[64]{0:T(128)S(1)} %get-tuple-element.11, f32[64]{0:T(128)S(1)} %get-tuple-element.5, ...), kind=kOutput, calls=%fused_computation.1 | convolution fusion | flops 2150367232 | bytes 36193280 | tf_op jit(solution)/shard_map/dot_general | solution.py:151
  155.5 0.2 reshape.340
  155.7 22.6 %all_to_all.5 = bf16[16,4,4096]{2,1,0:T(4,128)(2,1)S(1)} all-to-all(bf16[16,4,4096]{2,1,0:T(4,128)(2,1)S(1)} %reshape.340), channel_id=1, replica_groups=mesh['groups'=2,'dp'=8,'vocab'=2] {'dp','vocab'}, dimensions={0} | all-to-all | bytes 1048576 | tf_op jit(solution)/shard_map/all_to_all | solution.py:156
  178.3 0.8 reduce_sum.32
  (30 shorter events, 0.3 us)
Async XLA Ops:
  6.5 71.4 %all-gather.2.cloned.1.call-start = ((), (), s32[]{:S(2)}) async-start(), calls=%async_computation.1 | async-start | bytes 1345536 | tf_op jit(solution)/shard_map/all_gather | solution.py:51
  25.0 23.4 %copy-start = (bf16[64,5248]{1,0:T(8,128)(2,1)}, bf16[64,5248]{1,0:T(8,128)(2,1)S(1)}, u32[]{:S(2)}) copy-start(bf16[64,5248]{1,0:T(8,128)(2,1)S(1)} %all_gather.7) | copy-start | bytes 2015236
  48.8 4.3 %copy-start.1 = (bf16[8,4096]{1,0:T(8,128)(2,1)S(1)}, bf16[8,4096]{1,0:T(8,128)(2,1)}, u32[]{:S(2)}) copy-start(bf16[8,4096]{1,0:T(8,128)(2,1)} %param.13) | copy-start | bytes 196612
  48.8 6.5 %copy-start.2 = (s32[48,4]{0,1:T(4,128)S(1)}, s32[48,4]{0,1:T(4,128)}, u32[]{:S(2)}) copy-start(s32[48,4]{0,1:T(4,128)} %param.11) | copy-start | bytes 2308
  48.8 6.5 %copy-start.3 = (s32[48,4]{0,1:T(4,128)S(1)}, s32[48,4]{0,1:T(4,128)}, u32[]{:S(2)}) copy-start(s32[48,4]{0,1:T(4,128)} %param.10) | copy-start | bytes 2308
  52.8 1.2 collective-permute-start.4
  54.1 2.5 %collective-permute-start.5 = (f32[2,64]{1,0:T(2,128)S(1)}, f32[2,64]{1,0:T(2,128)S(1)}, u32[]{:S(2)}, u32[]{:S(2)}) collective-permute-start(f32[2,64]{1,0:T(2,128)S(1)} %pad_maximum_fusion.6), channel_id=1, source_target_pairs={{0,4},{2,6},{4,0},{6,2},{8,12},{10,14},{12,8},{14,10},{1,5},{3,7},... | collective-permute-start | bytes 1544 | tf_op jit(solution)/shard_map/ppermute | solution.py:99
  56.6 5.9 %collective-permute-start.6 = (f32[2,64]{1,0:T(2,128)S(1)}, f32[2,64]{1,0:T(2,128)S(1)}, u32[]{:S(2)}, u32[]{:S(2)}) collective-permute-start(f32[2,64]{1,0:T(2,128)S(1)} %pad_maximum_fusion.7), channel_id=1, source_target_pairs={{0,8},{2,10},{4,12},{6,14},{8,0},{10,2},{12,4},{14,6},{1,9},{3,11}... | collective-permute-start | bytes 1544 | tf_op jit(solution)/shard_map/ppermute | solution.py:99
  62.6 7.0 %collective-permute-start.12 = (f32[2,64]{1,0:T(2,128)S(1)}, f32[2,64]{1,0:T(2,128)S(1)}, u32[]{:S(2)}, u32[]{:S(2)}) collective-permute-start(f32[2,64]{1,0:T(2,128)S(1)} %pad_maximum_fusion.8), channel_id=1, source_target_pairs={{0,1},{1,0},{2,3},{3,2},{4,5},{5,4},{6,7},{7,6},{8,9},{9,8},{10,11... | collective-permute-start | bytes 1544 | tf_op jit(solution)/shard_map/ppermute | solution.py:134
  63.9 5.7 %slice-start = ((bf16[64,5248]{1,0:T(8,128)(2,1)}), bf16[64,128]{1,0:T(8,128)(2,1)S(1)}, s32[]{:S(2)}) async-start(bf16[64,5248]{1,0:T(8,128)(2,1)} %copy-done), calls=%async_computation.2 | async-start | bytes 32768 | tf_op jit(solution)/shard_map/slice | solution.py:57
  72.3 25.1 %collective-permute-start.7 = (bf16[4,32,64,128]{3,1,2,0:T(8,128)(2,1)S(1)}, bf16[4,32,64,128]{3,1,2,0:T(8,128)(2,1)}, u32[]{:S(2)}, u32[]{:S(2)}) collective-permute-start(bf16[4,32,64,128]{3,1,2,0:T(8,128)(2,1)S(1)} %fusion.1), channel_id=1, source_target_pairs={{0,2},{2,0},{4,6},{6,4},{8,10},{10,8},{12,14},{14,12},{1,3},{3,1},... | collective-permute-start | bytes 6291464 | tf_op jit(solution)/shard_map/ppermute | solution.py:121
  92.1 1.2 collective-permute-start
  93.4 2.5 %collective-permute-start.1 = (f32[2,64]{1,0:T(2,128)S(1)}, f32[2,64]{1,0:T(2,128)S(1)}, u32[]{:S(2)}, u32[]{:S(2)}) collective-permute-start(f32[2,64]{1,0:T(2,128)S(1)} %pad_maximum_fusion.2), channel_id=1, source_target_pairs={{0,4},{2,6},{4,0},{6,2},{8,12},{10,14},{12,8},{14,10},{1,5},{3,7},... | collective-permute-start | bytes 1544 | tf_op jit(solution)/shard_map/ppermute | solution.py:100
  95.9 7.3 %collective-permute-start.2 = (f32[2,64]{1,0:T(2,128)S(1)}, f32[2,64]{1,0:T(2,128)S(1)}, u32[]{:S(2)}, u32[]{:S(2)}) collective-permute-start(f32[2,64]{1,0:T(2,128)S(1)} %pad_maximum_fusion.3), channel_id=1, source_target_pairs={{0,8},{2,10},{4,12},{6,14},{8,0},{10,2},{12,4},{14,6},{1,9},{3,11}... | collective-permute-start | bytes 1544 | tf_op jit(solution)/shard_map/ppermute | solution.py:100
  101.0 25.7 %collective-permute-start.10 = (bf16[2,32,32,128]{3,1,2,0:T(8,128)(2,1)S(1)}, bf16[2,32,32,128]{3,1,2,0:T(8,128)(2,1)S(1)}, u32[]{:S(2)}, u32[]{:S(2)}) collective-permute-start(bf16[2,32,32,128]{3,1,2,0:T(8,128)(2,1)S(1)} %slice.237), channel_id=1, source_target_pairs={{0,8},{2,10},{4,12},{6,14},{8,0},{10,2},{12,4},{14,6},{1,9},{3,11}... | collective-permute-start | bytes 1572872 | tf_op jit(solution)/shard_map/ppermute | solution.py:115
  102.1 25.0 %collective-permute-start.8 = (bf16[2,32,32,128]{3,1,2,0:T(8,128)(2,1)S(1)}, bf16[2,32,32,128]{3,1,2,0:T(8,128)(2,1)S(1)}, u32[]{:S(2)}, u32[]{:S(2)}) collective-permute-start(bf16[2,32,32,128]{3,1,2,0:T(8,128)(2,1)S(1)} %fusion.19), channel_id=1, source_target_pairs={{0,4},{2,6},{4,0},{6,2},{8,12},{10,14},{12,8},{14,10},{1,5},{3,7},... | collective-permute-start | bytes 1572872 | tf_op jit(solution)/shard_map/ppermute | solution.py:115
  103.2 26.2 %collective-permute-start.3 = (f32[2,64]{1,0:T(2,128)S(1)}, f32[2,64]{1,0:T(2,128)S(1)}, u32[]{:S(2)}, u32[]{:S(2)}) collective-permute-start(f32[2,64]{1,0:T(2,128)S(1)} %pad_maximum_fusion.4), channel_id=1, source_target_pairs={{0,1},{1,0},{2,3},{3,2},{4,5},{5,4},{6,7},{7,6},{8,9},{9,8},{10,11... | collective-permute-start | bytes 1544 | tf_op jit(solution)/shard_map/ppermute | solution.py:135
  127.0 11.8 %collective-permute-start.11 = (bf16[1,32,32,128]{3,1,2,0:T(8,128)(2,1)S(1)}, bf16[1,32,32,128]{3,1,2,0:T(8,128)(2,1)S(1)}, u32[]{:S(2)}, u32[]{:S(2)}) collective-permute-start(bf16[1,32,32,128]{3,1,2,0:T(8,128)(2,1)S(1)} %slice.238), channel_id=1, source_target_pairs={{0,4},{2,6},{4,0},{6,2},{8,12},{10,14},{12,8},{14,10},{1,5},{3,7},... | collective-permute-start | bytes 786440 | tf_op jit(solution)/shard_map/ppermute | solution.py:115
  127.3 11.6 %collective-permute-start.9 = (bf16[1,32,32,128]{3,1,2,0:T(8,128)(2,1)S(1)}, bf16[1,32,32,128]{3,1,2,0:T(8,128)(2,1)S(1)}, u32[]{:S(2)}, u32[]{:S(2)}) collective-permute-start(bf16[1,32,32,128]{3,1,2,0:T(8,128)(2,1)S(1)} %fusion.32), channel_id=1, source_target_pairs={{0,8},{2,10},{4,12},{6,14},{8,0},{10,2},{12,4},{14,6},{1,9},{3,11}... | collective-permute-start | bytes 786440 | tf_op jit(solution)/shard_map/ppermute | solution.py:115
Sparse Core Ops, SparseCore 0:
  53.9 23.9 all-gather.1
